TPU v7x, 128 devices: a whole 4x4x4 slice. The times are simulated.
128 devices in a mesh: sta: 32 (over z, y, x_lo), tm: 4 (over x_hi, core).
Axes of the slice: x: 4 (x_hi: 2, x_lo: 2; x = x_hi * 2 + x_lo), y: 4, z: 4, core: 2. Of those that a mesh axis runs over, the one named last changes fastest.
Arguments:
- signal: bfloat16 [1024, 12288], P('sta', 'tm'), may hold values from -6 to 6
- fir: float32 [4, 32], replicated, may hold values from -1 to 1
- taps: int32 [4], replicated, may hold values from 16 to 32, as said below
- sources: int32 [2, 16], replicated, may hold values from 0 to 1023, as said below
Outputs:
- correlations: bfloat16 [2, 4, 16, 1024, 512], P(None, None, None, 'sta', 'tm')
Inputs may be any that keep to these rules, and one draw needn't show every extreme that they name: Each band has between 16 and 32 taps, and some band has exactly 32. `sources`: the source channels of one round are distinct.
All inputs are finite; a program needn't handle non-finite values.
Results may differ from a plain program's by a relative error of at most 0.0058.
Values may be sent and summed in bfloat16 or wider, within the bound.
No kernel may reach another device: no remote copies, remote signals or barrier semaphores. Data moves between devices by JAX's collectives and lax.ppermute only.
A program may use at most 128 MiB of HBM per device.

v0:
```python
import jax
import jax.numpy as jnp
from jax import lax
from jax.sharding import PartitionSpec as P

ROUNDS = 2
MAXLAG = 256


def passed_along(value, axis, steps):
    count = lax.axis_size(axis)
    first, last = (max(0, -steps), min(count, count - steps))
    return lax.ppermute(value, axis, [(source, source + steps) for source in range(first, last)])


def padded_2(block, sides, width):
    for axis, dim in sides:
        count = lax.axis_size(axis)
        forward = [(i, i + 1) for i in range(count - 1)]
        backward = [(target, source) for source, target in forward]
        low = lax.ppermute(
            lax.slice_in_dim(block, block.shape[dim] - width, None, axis=dim), axis, forward
        )
        high = lax.ppermute(lax.slice_in_dim(block, 0, width, axis=dim), axis, backward)
        block = jnp.concatenate([low, block, high], axis=dim)
    return block


def skew(values, count_rows):
    leading = values.shape[:-1]
    length = values.shape[-1]
    row_width = length + count_rows
    padded = jnp.concatenate([values, jnp.zeros(leading + (count_rows,), values.dtype)], axis=-1)
    repeated = jnp.tile(padded, (1,) * len(leading) + (count_rows,))
    return repeated[..., : count_rows * (row_width - 1)].reshape(
        leading + (count_rows, row_width - 1)
    )


def band_matrix(fir, taps, count_rows):
    tap_limit = fir.shape[1]
    active = jnp.arange(tap_limit, dtype=jnp.int32)[None, :] < taps[:, None]
    coefficients = jnp.where(active, fir, 0.0).astype(jnp.bfloat16)
    return skew(coefficients[:, ::-1], count_rows)


def filter_blocks(extended, fir, taps, length, block):
    tap_limit = fir.shape[1]
    channels = extended.shape[0]
    count = length // block
    main = extended[:, tap_limit - 1 :].reshape(channels, count, block)
    prefix = extended[:, :length].reshape(channels, count, block)[:, :, : tap_limit - 1]
    pieces = jnp.concatenate([prefix, main], axis=2)
    result = jnp.einsum(
        "cnu,btu->bcnt", pieces, band_matrix(fir, taps, block), preferred_element_type=jnp.float32
    )
    return result.reshape(result.shape[0], channels, length)


def correlate(traces, window, lag_count, time_block, lag_block):
    bands = traces.shape[0]
    count_src = traces.shape[1]
    length = traces.shape[2]
    channels = window.shape[1]
    turns = length // time_block
    groups = lag_count // lag_block
    span = time_block + lag_block - 1

    def step(turn, total):
        begin = turn * time_block
        block = lax.dynamic_slice_in_dim(traces, begin, time_block, 2)
        slab = lax.dynamic_slice_in_dim(window, begin, lag_count + time_block - 1, 2)
        parts = []
        for band in range(bands):
            skewed = skew(block[band], lag_block)
            slabs = jnp.stack(
                [slab[band, :, g * lag_block : g * lag_block + span] for g in range(groups)], axis=1
            )
            term = jnp.einsum("sqj,cgj->gqsc", skewed, slabs, preferred_element_type=jnp.float32)
            parts.append(term.reshape(lag_count, count_src, channels))
        return total + jnp.stack(parts, axis=1)

    empty = jnp.zeros((lag_count, bands, count_src, channels), jnp.float32)
    return lax.fori_loop(0, turns, step, empty)


def per_device(signal, fir, taps, sources):
    channels = signal.shape[0]
    samples = signal.shape[1]
    tap_limit = fir.shape[1]
    shards = lax.axis_size("tm")
    samples_all = samples * shards
    lag_count = 2 * MAXLAG
    norm_scale = samples_all ** (-0.5)
    fir_block = min(256, samples)
    widened = None
    left_rim = passed_along(signal[:, samples - (tap_limit - 1) :], "tm", 1)
    extended = jnp.concatenate([left_rim, signal], axis=1)
    filtered = filter_blocks(extended, fir, taps, samples, fir_block).astype(jnp.bfloat16)
    local_ids = sources - lax.axis_index("sta") * channels
    onehot = (local_ids[:, :, None] == jnp.arange(channels, dtype=jnp.int32)[None, None, :]).astype(
        jnp.bfloat16
    )
    results = []
    widened = padded_2(filtered, (("tm", 2),), MAXLAG)
    share = lag_count // shards
    lag_block = min(128, share)
    time_block = min(512, samples)
    for rnd in range(ROUNDS):
        traces = lax.psum(
            jnp.einsum(
                "sc,bct->bst", onehot[rnd], filtered, preferred_element_type=jnp.float32
            ).astype(jnp.bfloat16),
            "sta",
        )

        def lag_terms(start, count, traces=traces):
            return correlate(traces, widened, count, time_block, lag_block) * norm_scale

        summed = lax.psum_scatter(
            lag_terms(jnp.int32(0), share * lax.axis_size("tm")),
            "tm",
            scatter_dimension=0,
            tiled=True,
        ).astype(jnp.bfloat16)
        results.append(jnp.transpose(summed, (1, 2, 3, 0)))
    return jnp.stack(results, axis=0)


def solution(mesh):
    in_specs = (P("sta", "tm"), P(), P(), P())
    out_specs = P(None, None, None, "sta", "tm")
    return jax.shard_map(
        per_device, mesh=mesh, in_specs=in_specs, out_specs=out_specs, check_vma=False
    )
```

profile of v0, /device:TPU:1, one launch (start us, length us, event | category | flops | bytes accessed | tf_op | source)
XLA Modules:
  0.0 1204.5 jit_solution(2703139181319280235)
XLA Ops:
  30.9 278.6 %all-reduce.12.cloned.1.call-done = (bf16[4,16,3072]{2,1,0:T(8,128)(2,1)}, bf16[4,16,3072]{2,1,0:T(8,128)(2,1)}) async-done(((bf16[4,16,3072]{2,1,0:T(8,128)(2,1)}, bf16[4,16,3072]{2,1,0:T(8,128)(2,1)}), (bf16[4,16,3072]{2,1,0:T(8,128)(2,1)}, bf16[4,16,3072]{2,1,0:T(8,128)(2,1)})) %all-reduce.12.cloned.1.call-update) | async-done | bytes 786448 | tf_op jit(solution)/shard_map/psum | solution.py:110
  309.4 410.3 %while.28 = (s32[]{:T(128)}, f32[512,4,16,32]{0,3,2,1:T(8,128)}, bf16[4,32,3584]{2,1,0:T(8,128)(2,1)}, bf16[4,16,3072]{2,1,0:T(8,128)(2,1)}, s32[]{:T(128)}, /*i...) while((s32[]{:T(128)}, f32[512,4,16,32]{0,3,2,1:T(8,128)}, ...), condition=%wide.region_2.3_spmd.clone, body=%wide.region_1.2_spmd.clone.sunk | while | flops 1347940352 | bytes 132265400 | solution.py:84
  329.4 7.2 reshape.230
  343.2 7.2 reshape.232
  356.9 7.2 reshape.226
  379.6 7.2 reshape.228
  393.3 7.2 reshape.230
  420.9 7.2 reshape.226
  444.9 7.2 reshape.228
  486.2 7.2 reshape.226
  510.3 7.2 reshape.228
  537.9 7.2 reshape.232
  551.6 7.2 reshape.226
  575.6 7.2 reshape.228
  589.4 7.2 reshape.230
  603.2 7.2 reshape.232
  616.9 7.2 reshape.226
  682.1 7.2 reshape.226
  725.0 392.1 %while.29 = (s32[]{:T(128)}, f32[512,4,16,32]{0,3,2,1:T(8,128)}, bf16[4,32,3584]{2,1,0:T(8,128)(2,1)}, bf16[4,16,3072]{2,1,0:T(8,128)(2,1)}, s32[]{:T(128)}, /*i...) while((s32[]{:T(128)}, f32[512,4,16,32]{0,3,2,1:T(8,128)}, ...), condition=%wide.region_6.7_spmd.clone, body=%wide.region_5.6_spmd.clone.sunk | while | flops 1347940352 | bytes 132265400 | solution.py:84
  731.0 7.2 reshape.236
  758.5 7.6 reshape.240
  772.7 7.2 reshape.234
  795.5 7.2 reshape.236
  1123.5 71.9 %reduce-scatter.5.cloned.1.call-done = f32[128,4,16,32]{0,3,2,1:T(8,128)} async-done(((f32[512,4,16,32]{0,3,2,1:T(8,128)}), f32[128,4,16,32]{0,3,2,1:T(8,128)}) %reduce-scatter.5.cloned.1.call-update) | async-done | bytes 1048592 | tf_op jit(solution)/shard_map/reduce_scatter | solution.py:120
  (517 shorter events, 674.1 us)
Async XLA Ops:
  6.5 11.4 copy-start.6
  6.5 302.9 %all-reduce.12.cloned.1.call-start = ((), (), s32[]{:S(2)}) async-start(), calls=%async_computation.4 | async-start | bytes 1572864 | tf_op jit(solution)/shard_map/psum | solution.py:110
  7.4 10.6 collective-permute-start
  21.1 1101.1 %reduce-scatter.3.cloned.1.call-start = ((), (), s32[]{:S(2)}) async-start(), calls=%async_computation.2 | async-start | bytes 5242880 | tf_op jit(solution)/shard_map/reduce_scatter | solution.py:120
  21.1 4.4 collective-permute-start.1
  23.1 7.1 collective-permute-start.2
  724.9 470.5 %reduce-scatter.5.cloned.1.call-start = ((), (), s32[]{:S(2)}) async-start(), calls=%async_computation.3 | async-start | bytes 5242880 | tf_op jit(solution)/shard_map/reduce_scatter | solution.py:120
  780.9 4.4 copy-start.1
  780.9 4.4 copy-start.3
  780.9 4.4 copy-start.5
  845.1 4.4 copy-start.1
  845.1 4.4 copy-start.3
  845.1 4.4 copy-start.5
  910.6 4.4 copy-start.1
  910.6 4.4 copy-start.3
  910.6 4.4 copy-start.5
  976.2 4.4 copy-start.1
  976.2 4.4 copy-start.3
  976.2 4.4 copy-start.5
  1041.6 4.4 copy-start.1
  1041.6 4.4 copy-start.3
  1041.7 4.4 copy-start.5
  1107.0 4.4 copy-start.1
  1107.0 4.4 copy-start.3
  (19 other events, 82.1 us)
Sparse Core Ops, SparseCore 0:
  21.2 288.1 all-reduce.11
  725.0 73.4 reduce-scatter.2
  1122.3 73.1 reduce-scatter.4
where the time goes:
time: 1210 us; the launch traced here: 1200 us
  local copies, waits for them, and re-layouts  675 us (56%)
  waiting for transfers between devices  354 us (29%)
  other arithmetic  80.2 us (7%)
  matrix products  50 us (4%)
  loops' own time  21.5 us (2%)
  between operations  13.5 us (1%)
    reshape x49, local copies, waits for them, and re-layouts, skew(): repeated[..., :count_rows * (row_width - 1)]  349 us
    psum x1, waiting for transfers between devices, per_device(): lax.psum(jnp.einsum('sc,bct->bst', onehot[rnd], filtered, preferred_eleme...  279 us
    slice x49, local copies, waits for them, and re-layouts, skew(): repeated[..., :count_rows * (row_width - 1)]  82.5 us
    reshape x48, local copies, waits for them, and re-layouts, step(): return total + jnp.stack(parts, axis=1)  82.2 us
    while x120, local copies, waits for them, and re-layouts  72.3 us
    reduce_scatter x2, waiting for transfers between devices, per_device(): lax.psum_scatter(lag_terms(jnp.int32(0), share * lax.axis_size('tm')), 't...  72 us
    add x12, other arithmetic, step(): return total + jnp.stack(parts, axis=1)  64.7 us
    dot_general x48, matrix products, step(): jnp.einsum('sqj,cgj->gqsc', skewed, slabs, preferred_element_type=jnp.flo...  47.4 us
  transfers between devices with their start and end apart: 6, of which 3 were waited for; matrix products, arithmetic and copies ran while one was open for 34% of the time, Pallas kernels for 0%

commit v1 on v0

v1 whole, which is shorter than its diff:
```python
import functools

import jax
import jax.numpy as jnp
from jax import lax
from jax.experimental import pallas as pl
from jax.experimental.pallas import tpu as pltpu
from jax.sharding import PartitionSpec as P

ROUNDS = 2
MAXLAG = 256
SHIFTS = 16
CHUNK = 512


def skew(values, count_rows):
    leading = values.shape[:-1]
    length = values.shape[-1]
    row_width = length + count_rows
    padded = jnp.concatenate([values, jnp.zeros(leading + (count_rows,), values.dtype)], axis=-1)
    repeated = jnp.tile(padded, (1,) * len(leading) + (count_rows,))
    return repeated[..., : count_rows * (row_width - 1)].reshape(
        leading + (count_rows, row_width - 1)
    )


def band_matrix(fir, taps, count_rows):
    tap_limit = fir.shape[1]
    active = jnp.arange(tap_limit, dtype=jnp.int32)[None, :] < taps[:, None]
    coefficients = jnp.where(active, fir, 0.0).astype(jnp.bfloat16)
    return skew(coefficients[:, ::-1], count_rows)


def filter_blocks(extended, fir, taps, length, block):
    tap_limit = fir.shape[1]
    channels = extended.shape[0]
    count = length // block
    main = extended[:, tap_limit - 1 :].reshape(channels, count, block)
    prefix = extended[:, :length].reshape(channels, count, block)[:, :, : tap_limit - 1]
    pieces = jnp.concatenate([prefix, main], axis=2)
    result = jnp.einsum(
        "cnu,btu->bcnt", pieces, band_matrix(fir, taps, block), preferred_element_type=jnp.float32
    )
    return result.reshape(result.shape[0], channels, length)


def corr_kernel(fw_ref, pp_ref, out_ref, acc_ref, *, chunks, groups, rows_f, rows_p):
    acc_ref[...] = jnp.zeros_like(acc_ref)
    top = (groups - 1) * SHIFTS

    def step(k, carry):
        base = pl.multiple_of(k * CHUNK, CHUNK)
        fa = fw_ref[0, :, pl.ds(base, CHUNK + 128)]
        pa = pp_ref[0, :, pl.ds(base, CHUNK + 128)]
        lhs = jnp.concatenate([fa[:, q : q + CHUNK] for q in range(SHIFTS)], axis=0)
        rhs = jnp.concatenate(
            [pa[:, top - g * SHIFTS : top - g * SHIFTS + CHUNK] for g in range(groups)], axis=0
        )
        acc_ref[...] += lax.dot_general(
            lhs.astype(jnp.bfloat16),
            rhs.astype(jnp.bfloat16),
            (((1,), (1,)), ((), ())),
            preferred_element_type=jnp.float32,
        )
        return carry

    lax.fori_loop(0, chunks, step, 0)
    out_ref[0] = acc_ref[...]


def correlate(f_win, p_pad, lags, chunks):
    bands, rows_f, width = f_win.shape
    rows_p = p_pad.shape[1]
    groups = lags // SHIFTS
    kernel = functools.partial(
        corr_kernel, chunks=chunks, groups=groups, rows_f=rows_f, rows_p=rows_p
    )
    m = SHIFTS * rows_f
    n = groups * rows_p
    return pl.pallas_call(
        kernel,
        grid=(bands,),
        in_specs=[
            pl.BlockSpec((1, rows_f, width), lambda b: (b, 0, 0)),
            pl.BlockSpec((1, rows_p, width), lambda b: (b, 0, 0)),
        ],
        out_specs=pl.BlockSpec((1, m, n), lambda b: (b, 0, 0)),
        out_shape=jax.ShapeDtypeStruct((bands, m, n), jnp.float32),
        scratch_shapes=[pltpu.VMEM((m, n), jnp.float32)],
        compiler_params=pltpu.CompilerParams(vmem_limit_bytes=48 * 1024 * 1024),
    )(f_win, p_pad)


def per_device(signal, fir, taps, sources):
    channels = signal.shape[0]
    tap_limit = fir.shape[1]
    shards = lax.axis_size("tm")
    samples_all = signal.shape[1] * shards
    lag_count = 2 * MAXLAG
    share = lag_count // shards
    norm_scale = samples_all ** (-0.5)
    groups = share // SHIFTS
    count_src = sources.shape[1]

    flat_src = sources.reshape(-1)
    local_ids = flat_src - lax.axis_index("sta") * channels
    onehot = (local_ids[:, None] == jnp.arange(channels, dtype=jnp.int32)[None, :]).astype(
        jnp.bfloat16
    )
    picks = jnp.dot(onehot, signal, preferred_element_type=jnp.float32).astype(jnp.bfloat16)
    picks = lax.psum(picks, "sta")
    rows = jnp.concatenate([signal, picks], axis=0)
    rows = lax.all_gather(rows, "tm", axis=1, tiled=True)
    count_rows = rows.shape[0]
    extended = jnp.concatenate(
        [jnp.zeros((count_rows, tap_limit - 1), rows.dtype), rows], axis=1
    )
    filtered = filter_blocks(extended, fir, taps, samples_all, 256).astype(jnp.bfloat16)
    f_loc = filtered[:, :channels, :]
    p_src = filtered[:, channels:, :]

    span = samples_all + (groups - 1) * SHIFTS
    chunks = -(-span // CHUNK)
    width = chunks * CHUNK + 128
    f_big = jnp.pad(f_loc, ((0, 0), (0, 0), (MAXLAG, width - samples_all + lag_count)))
    start = lax.axis_index("tm") * share
    f_win = lax.dynamic_slice_in_dim(f_big, start, width, 2).astype(jnp.float32)
    top = (groups - 1) * SHIFTS
    p_pad = jnp.pad(p_src, ((0, 0), (0, 0), (top, width - samples_all - top))).astype(jnp.float32)

    out = correlate(f_win, p_pad, share, chunks)
    bands = out.shape[0]
    out = (out * norm_scale).astype(jnp.bfloat16)
    out = out.reshape(bands, SHIFTS, channels, groups, ROUNDS, count_src)
    out = jnp.transpose(out, (4, 0, 5, 2, 3, 1))
    return out.reshape(ROUNDS, bands, count_src, channels, share)


def solution(mesh):
    in_specs = (P("sta", "tm"), P(), P(), P())
    out_specs = P(None, None, None, "sta", "tm")
    return jax.shard_map(
        per_device, mesh=mesh, in_specs=in_specs, out_specs=out_specs, check_vma=False
    )
```

time: 1210 us -> 432 us (0.36)
  local copies, waits for them, and re-layouts: 675 us -> 21.8 us
  other arithmetic: 80.2 us -> 9.55 us
  Pallas kernels: 0 us -> 64.6 us
  matrix products: 50 us -> 5.76 us
  waiting for transfers between devices: 354 us -> 316 us
  loops' own time: 21.5 us -> 0 us
    reshape x49 -> x1, local copies, waits for them, and re-layouts: 349 us -> 1.49 us  [skew(): repeated[..., :count_rows * (row_width - 1)]]
    slice x49 -> x1, local copies, waits for them, and re-layouts: 82.5 us -> 0.2 us  [skew(): repeated[..., :count_rows * (row_width - 1)]]
    reshape x49 -> x2, local copies, waits for them, and re-layouts: 82.4 us -> 8.38 us  [the longest x1 4.56 us: per_device(): return out.reshape(ROUNDS, bands, count_src, channels, share)]
    while x120 -> x0, local copies, waits for them, and re-layouts: 72.3 us -> none
    reduce_scatter x2 -> x0, waiting for transfers between devices: 72 us -> none  [per_device(): lax.psum_scatter(lag_terms(jnp.int32(0), share * lax.axis_size('tm')), 't...]
    add x12 -> x0, other arithmetic: 64.7 us -> none  [step(): return total + jnp.stack(parts, axis=1)]
    pallas_call x0 -> x1, Pallas kernels: none -> 64.6 us  [correlate(): pl.pallas_call(kernel, grid=(bands,), in_specs=[pl.BlockSpec((1, rows_f,...]
    dot_general x50 -> x1, matrix products: 49.4 us -> 1.86 us  [per_device(): jnp.dot(onehot, signal, preferred_element_type=jnp.float32)]
  transfers between devices with their start and end apart: 6 -> 2, of which waited for: 3 -> 2; matrix products, arithmetic and copies ran while one was open for 34% -> 1% of each run, Pallas kernels for 0% -> 0%
where the time goes in v1:
time: 432 us
  waiting for transfers between devices  316 us (73%)
  Pallas kernels  64.6 us (15%)
  local copies, waits for them, and re-layouts  21.8 us (5%)
  between operations  13.5 us (3%)
  other arithmetic  9.55 us (2%)
  matrix products  5.76 us (1%)
    psum x1, waiting for transfers between devices, per_device(): picks = lax.psum(picks, 'sta')  280 us
    pallas_call x1, Pallas kernels, correlate(): pl.pallas_call(kernel, grid=(bands,), in_specs=[pl.BlockSpec((1, rows_f,...  64.6 us
    all_gather x1, waiting for transfers between devices, per_device(): rows = lax.all_gather(rows, 'tm', axis=1, tiled=True)  35.9 us
  transfers between devices with their start and end apart: 2, of which 2 were waited for; matrix products, arithmetic and copies ran while one was open for 1% of the time, Pallas kernels for 0%

profile of v1, /device:TPU:1, one launch (start us, length us, event | category | flops | bytes accessed | tf_op | source)
XLA Modules:
  0.0 431.6 jit_solution(6580719839832836552)
XLA Ops:
  6.5 0.7 broadcast_subtract_fusion
  7.3 1.9 convolution_convert_fusion
  9.2 280.4 %all-reduce.6.cloned.1.call-done = bf16[32,3072]{1,0:T(8,128)(2,1)} async-done(((bf16[32,3072]{1,0:T(8,128)(2,1)}), bf16[32,3072]{1,0:T(8,128)(2,1)}) %all-reduce.6.cloned.1.call-update) | async-done | bytes 196624 | tf_op jit(solution)/shard_map/psum | solution.py:111
  289.7 1.8 pad_maximum_fusion
  291.5 0.8 select_convert_fusion
  292.4 1.1 tile.10
  293.5 0.2 slice.20
  293.8 1.5 reshape.30
  295.3 35.9 %all-gather.2.cloned.1.call-done = bf16[64,12288]{1,0:T(8,128)(2,1)} async-done(((bf16[64,3072]{1,0:T(8,128)(2,1)}), bf16[64,12288]{1,0:T(8,128)(2,1)}) %all-gather.2.cloned.1.call-update) | async-done | bytes 1572880 | tf_op jit(solution)/shard_map/all_gather | solution.py:113
  331.1 1.7 copy.24
  332.9 0.2 copy-done
  333.0 0.5 pad_slice_fusion
  333.5 0.3 copy.22
  334.0 0.2 copy.19
  334.2 3.9 convert_bitcast_fusion
  338.1 0.8 copy.21
  338.9 0.7 fusion.6
  339.6 6.1 %fusion = (f32[4,32,12928]{2,1,0:T(8,128)}, f32[4,32,12928]{2,1,0:T(8,128)}) fusion(s32[]{:T(128)S(6)} %select_n.8, bf16[4,32,12288]{2,1,0:T(8,128)(2,1)S(1)} %get-tuple-element.6, bf16[4,32,12288]{2,1,0:T(8,128)(2,1)S(1)} %get-tuple-element.5), kind=kLoop, calls=%fused_computation.3 | loop fusion | flops 3309568 | bytes 19529732 | tf_op jit(solution)/shard_map/convert_element_type | solution.py:127
  345.7 64.6 %shard_map.46 = f32[4,512,256]{2,1,0:T(8,128)S(1)} custom-call(f32[4,32,12928]{2,1,0:T(8,128)} %get-tuple-element.7.fw_ref, f32[4,32,12928]{2,1,0:T(8,128)} %get-tuple-element.8.pp_ref), custom_call_target="tpu_custom_call" | custom-call | tf_op jit(solution)/shard_map/pallas_call | solution.py:80
  410.2 0.2 multiply_convert_fusion
  410.5 0.5 copy.13
  411.0 3.8 reshape.33
  414.8 5.4 %copy.14 = bf16[2,4,16,32,8,16]{3,5,4,2,1,0:T(8,128)(2,1)} copy(bf16[2,4,16,32,8,16]{3,5,2,0,4,1:T(8,128)(2,1)} %bitcast.24) | data formatting | bytes 2097152 | tf_op jit(solution)/shard_map/transpose | solution.py:135
  420.2 4.6 %copy.15 = bf16[2,4,16,32,128]{4,3,2,1,0:T(8,128)(2,1)} copy(bf16[2,4,16,32,128]{3,4,2,1,0:T(8,128)(2,1)} %bitcast.25) | data formatting | bytes 2097152 | tf_op jit(solution)/shard_map/reshape | solution.py:136
  (10 shorter events, 0.5 us)
Async XLA Ops:
  6.5 283.1 %all-reduce.6.cloned.1.call-start = ((), (), s32[]{:S(2)}) async-start(), calls=%async_computation | async-start | bytes 393216 | tf_op jit(solution)/shard_map/psum | solution.py:111
  9.2 322.0 %all-gather.2.cloned.1.call-start = ((), (), s32[]{:S(2)}) async-start(), calls=%async_computation.1 | async-start | bytes 1966080 | tf_op jit(solution)/shard_map/all_gather | solution.py:113
  331.1 1.9 copy-start
Sparse Core Ops, SparseCore 0:
  9.8 279.8 all-reduce.5
  291.6 39.4 all-gather.1

commit v2 on v1

--- a/solution.py
+++ b/solution.py
@@ -91,6 +91,15 @@
     )(f_win, p_pad)
 
 
+def summed_over(value, axis):
+    count = lax.axis_size(axis)
+    step = 1
+    while step < count:
+        value = value + lax.ppermute(value, axis, [(i, i ^ step) for i in range(count)])
+        step *= 2
+    return value
+
+
 def per_device(signal, fir, taps, sources):
     channels = signal.shape[0]
     tap_limit = fir.shape[1]
@@ -108,16 +117,17 @@
         jnp.bfloat16
     )
     picks = jnp.dot(onehot, signal, preferred_element_type=jnp.float32).astype(jnp.bfloat16)
-    picks = lax.psum(picks, "sta")
-    rows = jnp.concatenate([signal, picks], axis=0)
-    rows = lax.all_gather(rows, "tm", axis=1, tiled=True)
-    count_rows = rows.shape[0]
-    extended = jnp.concatenate(
-        [jnp.zeros((count_rows, tap_limit - 1), rows.dtype), rows], axis=1
-    )
-    filtered = filter_blocks(extended, fir, taps, samples_all, 256).astype(jnp.bfloat16)
-    f_loc = filtered[:, :channels, :]
-    p_src = filtered[:, channels:, :]
+    picks = summed_over(picks, "sta")
+
+    def filtered_of(rows):
+        rows = lax.all_gather(rows, "tm", axis=1, tiled=True)
+        extended = jnp.concatenate(
+            [jnp.zeros((rows.shape[0], tap_limit - 1), rows.dtype), rows], axis=1
+        )
+        return filter_blocks(extended, fir, taps, samples_all, 256).astype(jnp.bfloat16)
+
+    f_loc = filtered_of(signal)
+    p_src = filtered_of(picks)
 
     span = samples_all + (groups - 1) * SHIFTS
     chunks = -(-span // CHUNK)

time: 432 us -> 156 us (0.36)
  waiting for transfers between devices: 316 us -> 9.78 us
  blocking collectives: 0 us -> 23 us
  between operations: 13.5 us -> 0.2 us
  starting transfers between devices: 0.04 us -> 11.6 us
  local copies, waits for them, and re-layouts: 21.8 us -> 28.5 us
    psum x1 -> x0, waiting for transfers between devices: 280 us -> none  [per_device(): picks = lax.psum(picks, 'sta')]
    all_gather x1 -> x0, waiting for transfers between devices: 35.9 us -> none  [per_device(): rows = lax.all_gather(rows, 'tm', axis=1, tiled=True)]
    all_gather x0 -> x2, blocking collectives: none -> 23 us  [filtered_of(): rows = lax.all_gather(rows, 'tm', axis=1, tiled=True)]
    ppermute x0 -> x5, starting transfers between devices: none -> 11.6 us  [summed_over(): lax.ppermute(value, axis, [(i, i ^ step) for i in range(count)])]
    ppermute x0 -> x5, waiting for transfers between devices: none -> 9.78 us  [summed_over(): lax.ppermute(value, axis, [(i, i ^ step) for i in range(count)])]
    convert_element_type x1 -> x2, local copies, waits for them, and re-layouts: 0.78 us -> 9.88 us  [filtered_of(): filter_blocks(extended, fir, taps, samples_all, 256).astype(jnp.bfloat16)]
  transfers between devices with their start and end apart: 2 -> 5, of which waited for: 2 -> 3; matrix products, arithmetic and copies ran while one was open for 1% -> 7% of each run, Pallas kernels for 0% -> 0%
where the time goes in v2:
time: 156 us; the launch traced here: 155 us
  Pallas kernels  64.6 us (41%)
  local copies, waits for them, and re-layouts  28.5 us (18%)
  blocking collectives  23 us (15%)
  starting transfers between devices  11.6 us (7%)
  waiting for transfers between devices  9.78 us (6%)
  other arithmetic  9.22 us (6%)
  matrix products  8.16 us (5%)
    pallas_call x1, Pallas kernels, correlate(): pl.pallas_call(kernel, grid=(bands,), in_specs=[pl.BlockSpec((1, rows_f,...  64.6 us
    all_gather x2, blocking collectives, filtered_of(): rows = lax.all_gather(rows, 'tm', axis=1, tiled=True)  23 us
    ppermute x5, starting transfers between devices, summed_over(): lax.ppermute(value, axis, [(i, i ^ step) for i in range(count)])  11.6 us
    convert_element_type x2, local copies, waits for them, and re-layouts, filtered_of(): filter_blocks(extended, fir, taps, samples_all, 256).astype(jnp.bfloat16)  9.88 us
    ppermute x5, waiting for transfers between devices, summed_over(): lax.ppermute(value, axis, [(i, i ^ step) for i in range(count)])  9.78 us
    convert_element_type x1, other arithmetic, per_device(): f_win = lax.dynamic_slice_in_dim(f_big, start, width, 2).astype(jnp.float32)  7.99 us
    dot_general x2, matrix products, filter_blocks(): jnp.einsum('cnu,btu->bcnt', pieces, band_matrix(fir, taps, block), prefer...  6.99 us
    transpose x1, local copies, waits for them, and re-layouts, per_device(): out = jnp.transpose(out, (4, 0, 5, 2, 3, 1))  5.38 us
  transfers between devices with their start and end apart: 5, of which 3 were waited for; matrix products, arithmetic and copies ran while one was open for 7% of the time, Pallas kernels for 0%

profile of v2, /device:TPU:1, one launch (start us, length us, event | category | flops | bytes accessed | tf_op | source)
XLA Modules:
  0.0 155.1 jit_solution(1724006386270178883)
XLA Ops:
  0.0 0.7 broadcast_subtract_fusion
  0.8 1.2 convolution_convert_fusion
  2.0 2.1 %collective-permute-start = (bf16[32,3072]{1,0:T(8,128)(2,1)S(1)}, bf16[32,3072]{1,0:T(8,128)(2,1)S(1)}, u32[]{:S(2)}, u32[]{:S(2)}) collective-permute-start(bf16[32,3072]{1,0:T(8,128)(2,1)S(1)} %convolution_convert_fusion), channel_id=1, source_target_pairs={{0,4},{4,0},{8,12},{12,8},{16,20},{20,16},{24,28},{28,24},{32,36},... | collective-permute-start | bytes 589832 | tf_op jit(solution)/shard_map/ppermute | solution.py:98
  4.1 4.2 %collective-permute-done = bf16[32,3072]{1,0:T(8,128)(2,1)S(1)} collective-permute-done((bf16[32,3072]{1,0:T(8,128)(2,1)S(1)}, bf16[32,3072]{1,0:T(8,128)(2,1)S(1)}, u32[]{:S(2)}, u32[]{:S(2)}) %collective-permute-start) | collective-permute-done | bytes 196640 | tf_op jit(solution)/shard_map/ppermute | solution.py:98
  8.3 1.8 %collective-permute-start.1 = (bf16[32,3072]{1,0:T(8,128)(2,1)S(1)}, bf16[32,3072]{1,0:T(8,128)(2,1)S(1)}, u32[]{:S(2)}, u32[]{:S(2)}) collective-permute-start(bf16[32,3072]{1,0:T(8,128)(2,1)S(1)} %add.29), channel_id=1, source_target_pairs={{0,8},{4,12},{8,0},{12,4},{16,24},{20,28},{24,16},{28,20},{32,40},... | collective-permute-start | bytes 589832 | tf_op jit(solution)/shard_map/ppermute | solution.py:98
  10.1 12.0 %all_gather.6 = bf16[32,12288]{1,0:T(8,128)(2,1)S(1)} all-gather(bf16[32,3072]{1,0:T(8,128)(2,1)} %param.4), channel_id=1, replica_groups=mesh['sta'=32,'tm'=4] {'tm'}, dimensions={1}, use_global_device_ids=true | all-gather | bytes 983040 | tf_op jit(solution)/shard_map/all_gather | solution.py:123
  22.1 2.7 %collective-permute-start.2 = (bf16[32,3072]{1,0:T(8,128)(2,1)S(1)}, bf16[32,3072]{1,0:T(8,128)(2,1)S(1)}, u32[]{:S(2)}, u32[]{:S(2)}) collective-permute-start(bf16[32,3072]{1,0:T(8,128)(2,1)S(1)} %add.30), channel_id=1, source_target_pairs={{0,16},{4,20},{8,24},{12,28},{16,0},{20,4},{24,8},{28,12},{32,48},... | collective-permute-start | bytes 589832 | tf_op jit(solution)/shard_map/ppermute | solution.py:98
  25.1 4.9 %collective-permute-done.2 = bf16[32,3072]{1,0:T(8,128)(2,1)S(1)} collective-permute-done((bf16[32,3072]{1,0:T(8,128)(2,1)S(1)}, bf16[32,3072]{1,0:T(8,128)(2,1)S(1)}, u32[]{:S(2)}, u32[]{:S(2)}) %collective-permute-start.2) | collective-permute-done | bytes 196640 | tf_op jit(solution)/shard_map/ppermute | solution.py:98
  30.1 1.7 %collective-permute-start.3 = (bf16[32,3072]{1,0:T(8,128)(2,1)S(1)}, bf16[32,3072]{1,0:T(8,128)(2,1)S(1)}, u32[]{:S(2)}, u32[]{:S(2)}) collective-permute-start(bf16[32,3072]{1,0:T(8,128)(2,1)S(1)} %add.31), channel_id=1, source_target_pairs={{0,32},{4,36},{8,40},{12,44},{16,48},{20,52},{24,56},{28,60},{32,0... | collective-permute-start | bytes 589832 | tf_op jit(solution)/shard_map/ppermute | solution.py:98
  32.0 1.1 tile.5
  33.4 1.5 reshape.39
  35.3 0.7 collective-permute-done.3
  36.0 3.3 %collective-permute-start.4 = (bf16[32,3072]{1,0:T(8,128)(2,1)S(1)}, bf16[32,3072]{1,0:T(8,128)(2,1)S(1)}, u32[]{:S(2)}, u32[]{:S(2)}) collective-permute-start(bf16[32,3072]{1,0:T(8,128)(2,1)S(1)} %add.32), channel_id=1, source_target_pairs={{0,64},{4,68},{8,72},{12,76},{16,80},{20,84},{24,88},{28,92},{32,9... | collective-permute-start | bytes 589832 | tf_op jit(solution)/shard_map/ppermute | solution.py:98
  39.3 3.5 %convert_bitcast_fusion.1 = bf16[4,32,48,256]{3,2,1,0:T(8,128)(2,1)} fusion(bf16[32,48,256]{2,1,0:T(8,128)(2,1)S(1)} %bitcast.43, bf16[32,48,31]{2,1,0:T(8,128)(2,1)S(1)} %slice.22, bf16[4,256,287]{2,1,0:T(8,128)(2,1)S(1)} %reshape.39), kind=kOutput, calls=%fused_computation.5 | convolution fusion | flops 906160128 | bytes 4615168 | tf_op jit(solution)/shard_map/cnu,btu->bcnt/dot_general | solution.py:41
  42.8 4.2 %convert_element_type.42 = bf16[4,32,12288]{2,1,0:T(8,128)(2,1)S(1)} reshape(bf16[4,32,48,256]{3,2,1,0:T(8,128)(2,1)} %convert_bitcast_fusion.1) | data formatting | bytes 6291456 | tf_op jit(solution)/shard_map/convert_element_type | solution.py:127
  47.1 11.0 %all_gather.7 = bf16[32,12288]{1,0:T(8,128)(2,1)S(1)} all-gather(bf16[32,3072]{1,0:T(8,128)(2,1)S(1)} %add.33), channel_id=1, replica_groups=mesh['sta'=32,'tm'=4] {'tm'}, dimensions={1}, use_global_device_ids=true | all-gather | bytes 983040 | tf_op jit(solution)/shard_map/all_gather | solution.py:123
  58.8 3.5 %convert_bitcast_fusion = bf16[4,32,48,256]{3,2,1,0:T(8,128)(2,1)} fusion(bf16[32,48,256]{2,1,0:T(8,128)(2,1)S(1)} %bitcast.44, bf16[32,48,31]{2,1,0:T(8,128)(2,1)S(1)} %slice.23, bf16[4,256,287]{2,1,0:T(8,128)(2,1)S(1)} %copy-done.1), kind=kOutput, calls=%fused_computation.4 | convolution fusion | flops 906160128 | bytes 4615168 | tf_op jit(solution)/shard_map/cnu,btu->bcnt/dot_general | solution.py:41
  62.3 5.7 %convert_element_type.47 = bf16[4,32,12288]{2,1,0:T(8,128)(2,1)} reshape(bf16[4,32,48,256]{3,2,1,0:T(8,128)(2,1)} %convert_bitcast_fusion) | data formatting | bytes 6291456 | tf_op jit(solution)/shard_map/convert_element_type | solution.py:127
  68.0 8.0 %fusion = (f32[4,32,12928]{2,1,0:T(8,128)}, f32[4,32,12928]{2,1,0:T(8,128)}) fusion(s32[]{:T(128)S(6)} %select_n.9, bf16[4,32,12288]{2,1,0:T(8,128)(2,1)S(1)} %convert_element_type.42, bf16[4,32,12288]{2,1,0:T(8,128)(2,1)} %convert_element_type.47), kind=kLoop, calls=%fused_computation.2 | loop fusion | flops 3309568 | bytes 19529732 | tf_op jit(solution)/shard_map/convert_element_type | solution.py:137
  76.0 64.6 %shard_map.46 = f32[4,512,256]{2,1,0:T(8,128)S(1)} custom-call(f32[4,32,12928]{2,1,0:T(8,128)} %get-tuple-element.5.fw_ref, f32[4,32,12928]{2,1,0:T(8,128)} %get-tuple-element.6.pp_ref), custom_call_target="tpu_custom_call" | custom-call | tf_op jit(solution)/shard_map/pallas_call | solution.py:80
  140.8 0.5 copy.8
  141.3 3.8 %reshape.44 = bf16[4,16,32,8,2,16]{2,1,5,4,3,0:T(8,128)(2,1)} reshape(bf16[4,512,256]{1,2,0:T(8,128)(2,1)S(1)} %copy.8) | data formatting | bytes 2097152 | tf_op jit(solution)/shard_map/reshape | solution.py:144
  145.1 5.4 %copy.9 = bf16[2,4,16,32,8,16]{3,5,4,2,1,0:T(8,128)(2,1)} copy(bf16[2,4,16,32,8,16]{3,5,2,0,4,1:T(8,128)(2,1)} %bitcast.35) | data formatting | bytes 2097152 | tf_op jit(solution)/shard_map/transpose | solution.py:145
  150.5 4.6 %copy.10 = bf16[2,4,16,32,128]{4,3,2,1,0:T(8,128)(2,1)} copy(bf16[2,4,16,32,128]{3,4,2,1,0:T(8,128)(2,1)} %bitcast.36) | data formatting | bytes 2097152 | tf_op jit(solution)/shard_map/reshape | solution.py:146
  (30 shorter events, 2.3 us)
Async XLA Ops:
  0.0 31.8 %copy-start.3 = (s32[4]{0:T(128)S(1)}, s32[4]{0:T(128)}, u32[]{:S(2)}) copy-start(s32[4]{0:T(128)} %param.6) | copy-start | bytes 52
  0.0 31.8 %copy-start.2 = (f32[4,32]{1,0:T(4,128)S(1)}, f32[4,32]{1,0:T(4,128)}, u32[]{:S(2)}) copy-start(f32[4,32]{1,0:T(4,128)} %param.5) | copy-start | bytes 1540
  2.0 6.3 %collective-permute-start = (bf16[32,3072]{1,0:T(8,128)(2,1)S(1)}, bf16[32,3072]{1,0:T(8,128)(2,1)S(1)}, u32[]{:S(2)}, u32[]{:S(2)}) collective-permute-start(bf16[32,3072]{1,0:T(8,128)(2,1)S(1)} %convolution_convert_fusion), channel_id=1, source_target_pairs={{0,4},{4,0},{8,12},{12,8},{16,20},{20,16},{24,28},{28,24},{32,36},... | collective-permute-start | bytes 589832 | tf_op jit(solution)/shard_map/ppermute | solution.py:98
  8.3 13.7 %collective-permute-start.1 = (bf16[32,3072]{1,0:T(8,128)(2,1)S(1)}, bf16[32,3072]{1,0:T(8,128)(2,1)S(1)}, u32[]{:S(2)}, u32[]{:S(2)}) collective-permute-start(bf16[32,3072]{1,0:T(8,128)(2,1)S(1)} %add.29), channel_id=1, source_target_pairs={{0,8},{4,12},{8,0},{12,4},{16,24},{20,28},{24,16},{28,20},{32,40},... | collective-permute-start | bytes 589832 | tf_op jit(solution)/shard_map/ppermute | solution.py:98
  22.1 7.9 %collective-permute-start.2 = (bf16[32,3072]{1,0:T(8,128)(2,1)S(1)}, bf16[32,3072]{1,0:T(8,128)(2,1)S(1)}, u32[]{:S(2)}, u32[]{:S(2)}) collective-permute-start(bf16[32,3072]{1,0:T(8,128)(2,1)S(1)} %add.30), channel_id=1, source_target_pairs={{0,16},{4,20},{8,24},{12,28},{16,0},{20,4},{24,8},{28,12},{32,48},... | collective-permute-start | bytes 589832 | tf_op jit(solution)/shard_map/ppermute | solution.py:98
  30.1 5.9 %collective-permute-start.3 = (bf16[32,3072]{1,0:T(8,128)(2,1)S(1)}, bf16[32,3072]{1,0:T(8,128)(2,1)S(1)}, u32[]{:S(2)}, u32[]{:S(2)}) collective-permute-start(bf16[32,3072]{1,0:T(8,128)(2,1)S(1)} %add.31), channel_id=1, source_target_pairs={{0,32},{4,36},{8,40},{12,44},{16,48},{20,52},{24,56},{28,60},{32,0... | collective-permute-start | bytes 589832 | tf_op jit(solution)/shard_map/ppermute | solution.py:98
  34.9 4.5 %copy-start = (bf16[4,256,287]{2,1,0:T(8,128)(2,1)}, bf16[4,256,287]{2,1,0:T(8,128)(2,1)S(1)}, u32[]{:S(2)}) copy-start(bf16[4,256,287]{2,1,0:T(8,128)(2,1)S(1)} %reshape.39) | copy-start | bytes 1763332
  36.0 11.0 %collective-permute-start.4 = (bf16[32,3072]{1,0:T(8,128)(2,1)S(1)}, bf16[32,3072]{1,0:T(8,128)(2,1)S(1)}, u32[]{:S(2)}, u32[]{:S(2)}) collective-permute-start(bf16[32,3072]{1,0:T(8,128)(2,1)S(1)} %add.32), channel_id=1, source_target_pairs={{0,64},{4,68},{8,72},{12,76},{16,80},{20,84},{24,88},{28,92},{32,9... | collective-permute-start | bytes 589832 | tf_op jit(solution)/shard_map/ppermute | solution.py:98
  47.1 11.7 %copy-start.1 = (bf16[4,256,287]{2,1,0:T(8,128)(2,1)S(1)}, bf16[4,256,287]{2,1,0:T(8,128)(2,1)}, u32[]{:S(2)}) copy-start(bf16[4,256,287]{2,1,0:T(8,128)(2,1)} %copy-done) | copy-start | bytes 1763332

commit v3 on v2

--- a/solution.py
+++ b/solution.py
@@ -134,9 +134,9 @@
     width = chunks * CHUNK + 128
     f_big = jnp.pad(f_loc, ((0, 0), (0, 0), (MAXLAG, width - samples_all + lag_count)))
     start = lax.axis_index("tm") * share
-    f_win = lax.dynamic_slice_in_dim(f_big, start, width, 2).astype(jnp.float32)
+    f_win = lax.dynamic_slice_in_dim(f_big, start, width, 2)
     top = (groups - 1) * SHIFTS
-    p_pad = jnp.pad(p_src, ((0, 0), (0, 0), (top, width - samples_all - top))).astype(jnp.float32)
+    p_pad = jnp.pad(p_src, ((0, 0), (0, 0), (top, width - samples_all - top)))
 
     out = correlate(f_win, p_pad, share, chunks)
     bands = out.shape[0]

time: 156 us -> 144 us (0.923)
  local copies, waits for them, and re-layouts: 28.5 us -> 37.2 us
  other arithmetic: 9.22 us -> 1.21 us
  Pallas kernels: 64.6 us -> 56.7 us
  waiting for transfers between devices: 9.78 us -> 3.73 us
  blocking collectives: 23 us -> 25 us
    convert_element_type x1 -> x0, other arithmetic: 7.99 us -> none  [per_device(): f_win = lax.dynamic_slice_in_dim(f_big, start, width, 2).astype(jnp.float32)]
    pallas_call x1, Pallas kernels: 64.6 us -> 56.7 us  [correlate(): pl.pallas_call(kernel, grid=(bands,), in_specs=[pl.BlockSpec((1, rows_f,...]
    ppermute x5, waiting for transfers between devices: 9.78 us -> 3.73 us  [summed_over(): lax.ppermute(value, axis, [(i, i ^ step) for i in range(count)])]
    pad x0 -> x1, local copies, waits for them, and re-layouts: none -> 4.59 us  [per_device(): p_pad = jnp.pad(p_src, ((0, 0), (0, 0), (top, width - samples_all - top)))]
    dynamic_slice x0 -> x1, local copies, waits for them, and re-layouts: none -> 2.13 us  [per_device(): f_win = lax.dynamic_slice_in_dim(f_big, start, width, 2)]
    all_gather x2, blocking collectives: 23 us -> 25 us  [filtered_of(): rows = lax.all_gather(rows, 'tm', axis=1, tiled=True)]
    unnamed x12 -> x10, local copies, waits for them, and re-layouts: 0.63 us -> 2.23 us
  transfers between devices with their start and end apart: 5 -> 5, of which waited for: 3 -> 3; matrix products, arithmetic and copies ran while one was open for 7% -> 10% of each run, Pallas kernels for 0% -> 0%
where the time goes in v3:
time: 144 us
  Pallas kernels  56.7 us (39%)
  local copies, waits for them, and re-layouts  37.2 us (26%)
  blocking collectives  25 us (17%)
  starting transfers between devices  11.6 us (8%)
  matrix products  7.99 us (6%)
  waiting for transfers between devices  3.73 us (3%)
    pallas_call x1, Pallas kernels, correlate(): pl.pallas_call(kernel, grid=(bands,), in_specs=[pl.BlockSpec((1, rows_f,...  56.7 us
    all_gather x2, blocking collectives, filtered_of(): rows = lax.all_gather(rows, 'tm', axis=1, tiled=True)  25 us
    ppermute x5, starting transfers between devices, summed_over(): lax.ppermute(value, axis, [(i, i ^ step) for i in range(count)])  11.6 us
    convert_element_type x2, local copies, waits for them, and re-layouts, filtered_of(): filter_blocks(extended, fir, taps, samples_all, 256).astype(jnp.bfloat16)  8.6 us
    dot_general x2, matrix products, filter_blocks(): jnp.einsum('cnu,btu->bcnt', pieces, band_matrix(fir, taps, block), prefer...  6.82 us
    transpose x1, local copies, waits for them, and re-layouts, per_device(): out = jnp.transpose(out, (4, 0, 5, 2, 3, 1))  5.39 us
    pad x1, local copies, waits for them, and re-layouts, per_device(): p_pad = jnp.pad(p_src, ((0, 0), (0, 0), (top, width - samples_all - top)))  4.59 us
    reshape x1, local copies, waits for them, and re-layouts, per_device(): return out.reshape(ROUNDS, bands, count_src, channels, share)  4.56 us
  transfers between devices with their start and end apart: 5, of which 3 were waited for; matrix products, arithmetic and copies ran while one was open for 10% of the time, Pallas kernels for 0%

profile of v3, /device:TPU:1, one launch (start us, length us, event | category | flops | bytes accessed | tf_op | source)
XLA Modules:
  0.0 143.5 jit_solution(10517120246119231137)
XLA Ops:
  0.8 1.2 convolution_convert_fusion
  1.9 2.1 %collective-permute-start = (bf16[32,3072]{1,0:T(8,128)(2,1)S(1)}, bf16[32,3072]{1,0:T(8,128)(2,1)S(1)}, u32[]{:S(2)}, u32[]{:S(2)}) collective-permute-start(bf16[32,3072]{1,0:T(8,128)(2,1)S(1)} %convolution_convert_fusion), channel_id=1, source_target_pairs={{0,4},{4,0},{8,12},{12,8},{16,20},{20,16},{24,28},{28,24},{32,36},... | collective-permute-start | bytes 589832 | tf_op jit(solution)/shard_map/ppermute | solution.py:98
  4.1 13.2 %all_gather.6 = bf16[32,12288]{1,0:T(8,128)(2,1)S(1)} all-gather(bf16[32,3072]{1,0:T(8,128)(2,1)} %param.4), channel_id=1, replica_groups=mesh['sta'=32,'tm'=4] {'tm'}, dimensions={1}, use_global_device_ids=true | all-gather | bytes 983040 | tf_op jit(solution)/shard_map/all_gather | solution.py:123
  17.4 1.4 collective-permute-start.1
  19.0 1.0 copy.18
  20.2 0.8 slice.22
  21.0 2.7 %collective-permute-done.1 = bf16[32,3072]{1,0:T(8,128)(2,1)S(1)} collective-permute-done((bf16[32,3072]{1,0:T(8,128)(2,1)S(1)}, bf16[32,3072]{1,0:T(8,128)(2,1)S(1)}, u32[]{:S(2)}, u32[]{:S(2)}) %collective-permute-start.1) | collective-permute-done | bytes 196640 | tf_op jit(solution)/shard_map/ppermute | solution.py:98
  23.8 3.0 %collective-permute-start.2 = (bf16[32,3072]{1,0:T(8,128)(2,1)S(1)}, bf16[32,3072]{1,0:T(8,128)(2,1)S(1)}, u32[]{:S(2)}, u32[]{:S(2)}) collective-permute-start(bf16[32,3072]{1,0:T(8,128)(2,1)S(1)} %add.30), channel_id=1, source_target_pairs={{0,16},{4,20},{8,24},{12,28},{16,0},{20,4},{24,8},{28,12},{32,48},... | collective-permute-start | bytes 589832 | tf_op jit(solution)/shard_map/ppermute | solution.py:98
  27.0 1.1 tile.5
  28.4 2.4 %reshape.39 = bf16[4,256,287]{2,1,0:T(8,128)(2,1)} reshape(bf16[4,73472]{1,0:T(4,128)(2,1)S(1)} %slice.21) | data formatting | bytes 1175552 | tf_op jit(solution)/shard_map/reshape | solution.py:22
  30.9 1.7 %collective-permute-start.3 = (bf16[32,3072]{1,0:T(8,128)(2,1)S(1)}, bf16[32,3072]{1,0:T(8,128)(2,1)S(1)}, u32[]{:S(2)}, u32[]{:S(2)}) collective-permute-start(bf16[32,3072]{1,0:T(8,128)(2,1)S(1)} %add.31), channel_id=1, source_target_pairs={{0,32},{4,36},{8,40},{12,44},{16,48},{20,52},{24,56},{28,60},{32,0... | collective-permute-start | bytes 589832 | tf_op jit(solution)/shard_map/ppermute | solution.py:98
  32.6 3.3 %convert_bitcast_fusion.1 = bf16[4,32,48,256]{3,2,1,0:T(8,128)(2,1)S(1)} fusion(bf16[32,48,256]{2,1,0:T(8,128)(2,1)} %bitcast.43, bf16[32,48,31]{2,1,0:T(8,128)(2,1)} %slice.22, bf16[4,256,287]{2,1,0:T(8,128)(2,1)} %reshape.39), kind=kOutput, calls=%fused_computation.3 | convolution fusion | flops 906160128 | bytes 4615168 | tf_op jit(solution)/shard_map/cnu,btu->bcnt/dot_general | solution.py:41
  35.9 2.9 %convert_element_type.36 = bf16[4,32,12288]{2,1,0:T(8,128)(2,1)} reshape(bf16[4,32,48,256]{3,2,1,0:T(8,128)(2,1)S(1)} %convert_bitcast_fusion.1) | data formatting | bytes 6291456 | tf_op jit(solution)/shard_map/convert_element_type | solution.py:127
  38.9 3.4 %collective-permute-start.4 = (bf16[32,3072]{1,0:T(8,128)(2,1)S(1)}, bf16[32,3072]{1,0:T(8,128)(2,1)S(1)}, u32[]{:S(2)}, u32[]{:S(2)}) collective-permute-start(bf16[32,3072]{1,0:T(8,128)(2,1)S(1)} %add.32), channel_id=1, source_target_pairs={{0,64},{4,68},{8,72},{12,76},{16,80},{20,84},{24,88},{28,92},{32,9... | collective-permute-start | bytes 589832 | tf_op jit(solution)/shard_map/ppermute | solution.py:98
  42.3 2.1 %pad_dynamic-slice_fusion.fw_ref = bf16[4,32,12928]{2,1,0:T(8,128)(2,1)S(1)} fusion(s32[]{:T(128)S(6)} %select_n.9, bf16[4,32,12288]{2,1,0:T(8,128)(2,1)} %convert_element_type.36), kind=kLoop, calls=%fused_computation | loop fusion | bytes 6455300 | tf_op jit(solution)/shard_map/dynamic_slice | solution.py:137
  44.4 0.9 collective-permute-done.4
  45.4 11.8 %all_gather.7 = bf16[32,12288]{1,0:T(8,128)(2,1)S(1)} all-gather(bf16[32,3072]{1,0:T(8,128)(2,1)S(1)} %add.33), channel_id=1, replica_groups=mesh['sta'=32,'tm'=4] {'tm'}, dimensions={1}, use_global_device_ids=true | all-gather | bytes 983040 | tf_op jit(solution)/shard_map/all_gather | solution.py:123
  58.5 3.5 %convert_bitcast_fusion = bf16[4,32,48,256]{3,2,1,0:T(8,128)(2,1)} fusion(bf16[32,48,256]{2,1,0:T(8,128)(2,1)S(1)} %bitcast.44, bf16[32,48,31]{2,1,0:T(8,128)(2,1)S(1)} %slice.23, bf16[4,256,287]{2,1,0:T(8,128)(2,1)S(1)} %copy-done), kind=kOutput, calls=%fused_computation.2 | convolution fusion | flops 906160128 | bytes 4615168 | tf_op jit(solution)/shard_map/cnu,btu->bcnt/dot_general | solution.py:41
  62.0 5.7 %convert_element_type.40 = bf16[4,32,12288]{2,1,0:T(8,128)(2,1)} reshape(bf16[4,32,48,256]{3,2,1,0:T(8,128)(2,1)} %convert_bitcast_fusion) | data formatting | bytes 6291456 | tf_op jit(solution)/shard_map/convert_element_type | solution.py:127
  67.7 4.6 %pad.12.pp_ref = bf16[4,32,12928]{2,1,0:T(8,128)(2,1)} pad(bf16[4,32,12288]{2,1,0:T(8,128)(2,1)} %convert_element_type.40, bf16[]{:T(256)} %constant.4.clone.1), padding=0_0x0_0x112_528 | pad | bytes 6455298 | tf_op jit(solution)/shard_map/jit(_pad)/pad | solution.py:139
  72.3 56.7 %shard_map.46 = f32[4,512,256]{2,1,0:T(8,128)S(1)} custom-call(bf16[4,32,12928]{2,1,0:T(8,128)(2,1)S(1)} %pad_dynamic-slice_fusion.fw_ref, bf16[4,32,12928]{2,1,0:T(8,128)(2,1)} %pad.12.pp_ref), custom_call_target="tpu_custom_call" | custom-call | tf_op jit(solution)/shard_map/pallas_call | solution.py:80
  129.8 3.8 %reshape.44 = bf16[4,16,32,8,2,16]{2,1,5,4,3,0:T(8,128)(2,1)} reshape(bf16[4,512,256]{1,2,0:T(8,128)(2,1)S(1)} %copy.8) | data formatting | bytes 2097152 | tf_op jit(solution)/shard_map/reshape | solution.py:144
  133.6 5.4 %copy.9 = bf16[2,4,16,32,8,16]{3,5,4,2,1,0:T(8,128)(2,1)} copy(bf16[2,4,16,32,8,16]{3,5,2,0,4,1:T(8,128)(2,1)} %bitcast.35) | data formatting | bytes 2097152 | tf_op jit(solution)/shard_map/transpose | solution.py:145
  139.0 4.6 %copy.10 = bf16[2,4,16,32,128]{4,3,2,1,0:T(8,128)(2,1)} copy(bf16[2,4,16,32,128]{3,4,2,1,0:T(8,128)(2,1)} %bitcast.36) | data formatting | bytes 2097152 | tf_op jit(solution)/shard_map/reshape | solution.py:146
  (29 shorter events, 4.1 us)
Async XLA Ops:
  1.9 15.3 %collective-permute-start = (bf16[32,3072]{1,0:T(8,128)(2,1)S(1)}, bf16[32,3072]{1,0:T(8,128)(2,1)S(1)}, u32[]{:S(2)}, u32[]{:S(2)}) collective-permute-start(bf16[32,3072]{1,0:T(8,128)(2,1)S(1)} %convolution_convert_fusion), channel_id=1, source_target_pairs={{0,4},{4,0},{8,12},{12,8},{16,20},{20,16},{24,28},{28,24},{32,36},... | collective-permute-start | bytes 589832 | tf_op jit(solution)/shard_map/ppermute | solution.py:98
  17.4 6.4 %collective-permute-start.1 = (bf16[32,3072]{1,0:T(8,128)(2,1)S(1)}, bf16[32,3072]{1,0:T(8,128)(2,1)S(1)}, u32[]{:S(2)}, u32[]{:S(2)}) collective-permute-start(bf16[32,3072]{1,0:T(8,128)(2,1)S(1)} %add.29), channel_id=1, source_target_pairs={{0,8},{4,12},{8,0},{12,4},{16,24},{20,28},{24,16},{28,20},{32,40},... | collective-permute-start | bytes 589832 | tf_op jit(solution)/shard_map/ppermute | solution.py:98
  19.0 7.8 %copy-start.1 = (f32[4,32]{1,0:T(4,128)S(1)}, f32[4,32]{1,0:T(4,128)}, u32[]{:S(2)}) copy-start(f32[4,32]{1,0:T(4,128)} %param.5) | copy-start | bytes 1540
  19.0 7.8 %copy-start.2 = (s32[4]{0:T(128)S(1)}, s32[4]{0:T(128)}, u32[]{:S(2)}) copy-start(s32[4]{0:T(128)} %param.6) | copy-start | bytes 52
  23.8 7.0 %collective-permute-start.2 = (bf16[32,3072]{1,0:T(8,128)(2,1)S(1)}, bf16[32,3072]{1,0:T(8,128)(2,1)S(1)}, u32[]{:S(2)}, u32[]{:S(2)}) collective-permute-start(bf16[32,3072]{1,0:T(8,128)(2,1)S(1)} %add.30), channel_id=1, source_target_pairs={{0,16},{4,20},{8,24},{12,28},{16,0},{20,4},{24,8},{28,12},{32,48},... | collective-permute-start | bytes 589832 | tf_op jit(solution)/shard_map/ppermute | solution.py:98
  30.9 7.9 %collective-permute-start.3 = (bf16[32,3072]{1,0:T(8,128)(2,1)S(1)}, bf16[32,3072]{1,0:T(8,128)(2,1)S(1)}, u32[]{:S(2)}, u32[]{:S(2)}) collective-permute-start(bf16[32,3072]{1,0:T(8,128)(2,1)S(1)} %add.31), channel_id=1, source_target_pairs={{0,32},{4,36},{8,40},{12,44},{16,48},{20,52},{24,56},{28,60},{32,0... | collective-permute-start | bytes 589832 | tf_op jit(solution)/shard_map/ppermute | solution.py:98
  38.9 6.4 %collective-permute-start.4 = (bf16[32,3072]{1,0:T(8,128)(2,1)S(1)}, bf16[32,3072]{1,0:T(8,128)(2,1)S(1)}, u32[]{:S(2)}, u32[]{:S(2)}) collective-permute-start(bf16[32,3072]{1,0:T(8,128)(2,1)S(1)} %add.32), channel_id=1, source_target_pairs={{0,64},{4,68},{8,72},{12,76},{16,80},{20,84},{24,88},{28,92},{32,9... | collective-permute-start | bytes 589832 | tf_op jit(solution)/shard_map/ppermute | solution.py:98
  57.4 1.1 copy-start

commit v4 on v3

--- a/solution.py
+++ b/solution.py
@@ -10,7 +10,7 @@
 ROUNDS = 2
 MAXLAG = 256
 SHIFTS = 16
-CHUNK = 512
+CHUNK = 2560
 
 
 def skew(values, count_rows):
@@ -93,10 +93,15 @@
 
 def summed_over(value, axis):
     count = lax.axis_size(axis)
-    step = 1
-    while step < count:
-        value = value + lax.ppermute(value, axis, [(i, i ^ step) for i in range(count)])
-        step *= 2
+    bits = max(1, (count - 1).bit_length())
+    rounds = [[0]] + [list(range(b, min(b + 2, bits))) for b in range(1, bits, 2)]
+    for group in rounds:
+        masks = [
+            m for m in range(1, count)
+            if all((m >> b) & 1 == 0 for b in range(bits) if b not in group)
+        ]
+        parts = [lax.ppermute(value, axis, [(i, i ^ m) for i in range(count)]) for m in masks]
+        value = sum(parts, value)
     return value
 
 

time: 144 us -> 127 us (0.88)
  Pallas kernels: 56.7 us -> 36.5 us
  waiting for transfers between devices: 3.73 us -> 8.84 us
  starting transfers between devices: 11.6 us -> 10.1 us
    pallas_call x1, Pallas kernels: 56.7 us -> 36.5 us  [correlate(): pl.pallas_call(kernel, grid=(bands,), in_specs=[pl.BlockSpec((1, rows_f,...]
    ppermute x5 -> x7, waiting for transfers between devices: 3.73 us -> 8.84 us  [summed_over(): lax.ppermute(value, axis, [(i, i ^ m) for i in range(count)])]
    ppermute x5 -> x7, starting transfers between devices: 11.6 us -> 10.1 us  [summed_over(): lax.ppermute(value, axis, [(i, i ^ m) for i in range(count)])]
  transfers between devices with their start and end apart: 5 -> 7, of which waited for: 3 -> 4; matrix products, arithmetic and copies ran while one was open for 10% -> 11% of each run, Pallas kernels for 0% -> 0%
where the time goes in v4:
time: 127 us
  local copies, waits for them, and re-layouts  37.2 us (29%)
  Pallas kernels  36.5 us (29%)
  blocking collectives  23.9 us (19%)
  starting transfers between devices  10.1 us (8%)
  waiting for transfers between devices  8.84 us (7%)
  matrix products  7.98 us (6%)
  other arithmetic  2.12 us (2%)
    pallas_call x1, Pallas kernels, correlate(): pl.pallas_call(kernel, grid=(bands,), in_specs=[pl.BlockSpec((1, rows_f,...  36.5 us
    all_gather x2, blocking collectives, filtered_of(): rows = lax.all_gather(rows, 'tm', axis=1, tiled=True)  23.9 us
    ppermute x7, starting transfers between devices, summed_over(): lax.ppermute(value, axis, [(i, i ^ m) for i in range(count)])  10.1 us
    ppermute x7, waiting for transfers between devices, summed_over(): lax.ppermute(value, axis, [(i, i ^ m) for i in range(count)])  8.84 us
    convert_element_type x2, local copies, waits for them, and re-layouts, filtered_of(): filter_blocks(extended, fir, taps, samples_all, 256).astype(jnp.bfloat16)  8.59 us
    dot_general x2, matrix products, filter_blocks(): jnp.einsum('cnu,btu->bcnt', pieces, band_matrix(fir, taps, block), prefer...  6.81 us
    transpose x1, local copies, waits for them, and re-layouts, per_device(): out = jnp.transpose(out, (4, 0, 5, 2, 3, 1))  5.38 us
    pad x1, local copies, waits for them, and re-layouts, per_device(): p_pad = jnp.pad(p_src, ((0, 0), (0, 0), (top, width - samples_all - top)))  4.58 us
  transfers between devices with their start and end apart: 7, of which 4 were waited for; matrix products, arithmetic and copies ran while one was open for 11% of the time, Pallas kernels for 0%

profile of v4, /device:TPU:1, one launch (start us, length us, event | category | flops | bytes accessed | tf_op | source)
XLA Modules:
  0.0 126.8 jit_solution(11951847508641461858)
XLA Ops:
  0.8 1.2 convolution_convert_fusion
  1.9 2.1 %collective-permute-start = (bf16[32,3072]{1,0:T(8,128)(2,1)S(1)}, bf16[32,3072]{1,0:T(8,128)(2,1)S(1)}, u32[]{:S(2)}, u32[]{:S(2)}) collective-permute-start(bf16[32,3072]{1,0:T(8,128)(2,1)S(1)} %convolution_convert_fusion), channel_id=1, source_target_pairs={{0,4},{4,0},{8,12},{12,8},{16,20},{20,16},{24,28},{28,24},{32,36},... | collective-permute-start | bytes 589832 | tf_op jit(solution)/shard_map/ppermute | solution.py:103
  4.1 13.2 %all_gather.6 = bf16[32,12288]{1,0:T(8,128)(2,1)S(1)} all-gather(bf16[32,3072]{1,0:T(8,128)(2,1)} %param.4), channel_id=1, replica_groups=mesh['sta'=32,'tm'=4] {'tm'}, dimensions={1}, use_global_device_ids=true | all-gather | bytes 983040 | tf_op jit(solution)/shard_map/all_gather | solution.py:128
  17.6 1.0 copy.18
  18.8 0.8 slice.22
  19.8 1.1 tile.5
  21.2 2.4 %reshape.39 = bf16[4,256,287]{2,1,0:T(8,128)(2,1)} reshape(bf16[4,73472]{1,0:T(4,128)(2,1)S(1)} %slice.21) | data formatting | bytes 1175552 | tf_op jit(solution)/shard_map/reshape | solution.py:22
  23.6 2.8 %collective-permute-start.3 = (bf16[32,3072]{1,0:T(8,128)(2,1)S(1)}, bf16[32,3072]{1,0:T(8,128)(2,1)S(1)}, u32[]{:S(2)}, u32[]{:S(2)}) collective-permute-start(bf16[32,3072]{1,0:T(8,128)(2,1)S(1)} %add.35), channel_id=1, source_target_pairs={{0,24},{4,28},{8,16},{12,20},{16,8},{20,12},{24,0},{28,4},{32,56},... | collective-permute-start | bytes 589832 | tf_op jit(solution)/shard_map/ppermute | solution.py:103
  27.1 3.3 %convert_bitcast_fusion.1 = bf16[4,32,48,256]{3,2,1,0:T(8,128)(2,1)S(1)} fusion(bf16[32,48,256]{2,1,0:T(8,128)(2,1)} %bitcast.43, bf16[32,48,31]{2,1,0:T(8,128)(2,1)} %slice.22, bf16[4,256,287]{2,1,0:T(8,128)(2,1)} %reshape.39), kind=kOutput, calls=%fused_computation.3 | convolution fusion | flops 906160128 | bytes 4615168 | tf_op jit(solution)/shard_map/cnu,btu->bcnt/dot_general | solution.py:41
  30.4 2.9 %convert_element_type.36 = bf16[4,32,12288]{2,1,0:T(8,128)(2,1)} reshape(bf16[4,32,48,256]{3,2,1,0:T(8,128)(2,1)S(1)} %convert_bitcast_fusion.1) | data formatting | bytes 6291456 | tf_op jit(solution)/shard_map/convert_element_type | solution.py:132
  33.3 2.1 %collective-permute-done.3 = bf16[32,3072]{1,0:T(8,128)(2,1)S(1)} collective-permute-done((bf16[32,3072]{1,0:T(8,128)(2,1)S(1)}, bf16[32,3072]{1,0:T(8,128)(2,1)S(1)}, u32[]{:S(2)}, u32[]{:S(2)}) %collective-permute-start.3) | collective-permute-done | bytes 196640 | tf_op jit(solution)/shard_map/ppermute | solution.py:103
  35.4 0.8 collective-permute-done.1
  36.1 1.1 add_add_fusion.1
  37.2 3.9 %collective-permute-start.6 = (bf16[32,3072]{1,0:T(8,128)(2,1)S(1)}, bf16[32,3072]{1,0:T(8,128)(2,1)S(1)}, u32[]{:S(2)}, u32[]{:S(2)}) collective-permute-start(bf16[32,3072]{1,0:T(8,128)(2,1)S(1)} %add_add_fusion.1), channel_id=1, source_target_pairs={{0,96},{4,100},{8,104},{12,108},{16,112},{20,116},{24,120},{28,124... | collective-permute-start | bytes 589832 | tf_op jit(solution)/shard_map/ppermute | solution.py:103
  41.7 2.1 %pad_dynamic-slice_fusion.fw_ref = bf16[4,32,12928]{2,1,0:T(8,128)(2,1)S(1)} fusion(s32[]{:T(128)S(6)} %select_n.9, bf16[4,32,12288]{2,1,0:T(8,128)(2,1)} %convert_element_type.36), kind=kLoop, calls=%fused_computation | loop fusion | bytes 6455300 | tf_op jit(solution)/shard_map/dynamic_slice | solution.py:142
  43.9 5.6 %collective-permute-done.6 = bf16[32,3072]{1,0:T(8,128)(2,1)S(1)} collective-permute-done((bf16[32,3072]{1,0:T(8,128)(2,1)S(1)}, bf16[32,3072]{1,0:T(8,128)(2,1)S(1)}, u32[]{:S(2)}, u32[]{:S(2)}) %collective-permute-start.6) | collective-permute-done | bytes 196640 | tf_op jit(solution)/shard_map/ppermute | solution.py:103
  49.9 10.7 %all_gather.7 = bf16[32,12288]{1,0:T(8,128)(2,1)S(1)} all-gather(bf16[32,3072]{1,0:T(8,128)(2,1)S(1)} %add_add_fusion), channel_id=1, replica_groups=mesh['sta'=32,'tm'=4] {'tm'}, dimensions={1}, use_global_device_ids=true | all-gather | bytes 983040 | tf_op jit(solution)/shard_map/all_gather | solution.py:128
  62.0 3.5 %convert_bitcast_fusion = bf16[4,32,48,256]{3,2,1,0:T(8,128)(2,1)} fusion(bf16[32,48,256]{2,1,0:T(8,128)(2,1)S(1)} %bitcast.44, bf16[32,48,31]{2,1,0:T(8,128)(2,1)S(1)} %slice.23, bf16[4,256,287]{2,1,0:T(8,128)(2,1)S(1)} %copy-done), kind=kOutput, calls=%fused_computation.2 | convolution fusion | flops 906160128 | bytes 4615168 | tf_op jit(solution)/shard_map/cnu,btu->bcnt/dot_general | solution.py:41
  65.5 5.7 %convert_element_type.40 = bf16[4,32,12288]{2,1,0:T(8,128)(2,1)} reshape(bf16[4,32,48,256]{3,2,1,0:T(8,128)(2,1)} %convert_bitcast_fusion) | data formatting | bytes 6291456 | tf_op jit(solution)/shard_map/convert_element_type | solution.py:132
  71.2 4.6 %pad.12.pp_ref = bf16[4,32,12928]{2,1,0:T(8,128)(2,1)} pad(bf16[4,32,12288]{2,1,0:T(8,128)(2,1)} %convert_element_type.40, bf16[]{:T(256)} %constant.4.clone.1), padding=0_0x0_0x112_528 | pad | bytes 6455298 | tf_op jit(solution)/shard_map/jit(_pad)/pad | solution.py:144
  75.8 36.5 %shard_map.46 = f32[4,512,256]{2,1,0:T(8,128)S(1)} custom-call(bf16[4,32,12928]{2,1,0:T(8,128)(2,1)S(1)} %pad_dynamic-slice_fusion.fw_ref, bf16[4,32,12928]{2,1,0:T(8,128)(2,1)} %pad.12.pp_ref), custom_call_target="tpu_custom_call" | custom-call | tf_op jit(solution)/shard_map/pallas_call | solution.py:80
  113.0 3.8 %reshape.44 = bf16[4,16,32,8,2,16]{2,1,5,4,3,0:T(8,128)(2,1)} reshape(bf16[4,512,256]{1,2,0:T(8,128)(2,1)S(1)} %copy.8) | data formatting | bytes 2097152 | tf_op jit(solution)/shard_map/reshape | solution.py:149
  116.9 5.4 %copy.9 = bf16[2,4,16,32,8,16]{3,5,4,2,1,0:T(8,128)(2,1)} copy(bf16[2,4,16,32,8,16]{3,5,2,0,4,1:T(8,128)(2,1)} %bitcast.35) | data formatting | bytes 2097152 | tf_op jit(solution)/shard_map/transpose | solution.py:150
  122.2 4.6 %copy.10 = bf16[2,4,16,32,128]{4,3,2,1,0:T(8,128)(2,1)} copy(bf16[2,4,16,32,128]{3,4,2,1,0:T(8,128)(2,1)} %bitcast.36) | data formatting | bytes 2097152 | tf_op jit(solution)/shard_map/reshape | solution.py:151
  (31 shorter events, 5.6 us)
Async XLA Ops:
  1.9 21.6 %collective-permute-start = (bf16[32,3072]{1,0:T(8,128)(2,1)S(1)}, bf16[32,3072]{1,0:T(8,128)(2,1)S(1)}, u32[]{:S(2)}, u32[]{:S(2)}) collective-permute-start(bf16[32,3072]{1,0:T(8,128)(2,1)S(1)} %convolution_convert_fusion), channel_id=1, source_target_pairs={{0,4},{4,0},{8,12},{12,8},{16,20},{20,16},{24,28},{28,24},{32,36},... | collective-permute-start | bytes 589832 | tf_op jit(solution)/shard_map/ppermute | solution.py:103
  17.6 2.0 %copy-start.1 = (f32[4,32]{1,0:T(4,128)S(1)}, f32[4,32]{1,0:T(4,128)}, u32[]{:S(2)}) copy-start(f32[4,32]{1,0:T(4,128)} %param.5) | copy-start | bytes 1540
  17.6 2.0 %copy-start.2 = (s32[4]{0:T(128)S(1)}, s32[4]{0:T(128)}, u32[]{:S(2)}) copy-start(s32[4]{0:T(128)} %param.6) | copy-start | bytes 52
  23.6 11.8 %collective-permute-start.3 = (bf16[32,3072]{1,0:T(8,128)(2,1)S(1)}, bf16[32,3072]{1,0:T(8,128)(2,1)S(1)}, u32[]{:S(2)}, u32[]{:S(2)}) collective-permute-start(bf16[32,3072]{1,0:T(8,128)(2,1)S(1)} %add.35), channel_id=1, source_target_pairs={{0,24},{4,28},{8,16},{12,20},{16,8},{20,12},{24,0},{28,4},{32,56},... | collective-permute-start | bytes 589832 | tf_op jit(solution)/shard_map/ppermute | solution.py:103
  26.4 9.0 %collective-permute-start.2 = (bf16[32,3072]{1,0:T(8,128)(2,1)S(1)}, bf16[32,3072]{1,0:T(8,128)(2,1)}, u32[]{:S(2)}, u32[]{:S(2)}) collective-permute-start(bf16[32,3072]{1,0:T(8,128)(2,1)S(1)} %add.35), channel_id=1, source_target_pairs={{0,16},{4,20},{8,24},{12,28},{16,0},{20,4},{24,8},{28,12},{32,48},... | collective-permute-start | bytes 589832 | tf_op jit(solution)/shard_map/ppermute | solution.py:103
  26.8 9.4 %collective-permute-start.1 = (bf16[32,3072]{1,0:T(8,128)(2,1)S(1)}, bf16[32,3072]{1,0:T(8,128)(2,1)}, u32[]{:S(2)}, u32[]{:S(2)}) collective-permute-start(bf16[32,3072]{1,0:T(8,128)(2,1)S(1)} %add.35), channel_id=1, source_target_pairs={{0,8},{4,12},{8,0},{12,4},{16,24},{20,28},{24,16},{28,20},{32,40},... | collective-permute-start | bytes 589832 | tf_op jit(solution)/shard_map/ppermute | solution.py:103
  37.2 12.3 %collective-permute-start.6 = (bf16[32,3072]{1,0:T(8,128)(2,1)S(1)}, bf16[32,3072]{1,0:T(8,128)(2,1)S(1)}, u32[]{:S(2)}, u32[]{:S(2)}) collective-permute-start(bf16[32,3072]{1,0:T(8,128)(2,1)S(1)} %add_add_fusion.1), channel_id=1, source_target_pairs={{0,96},{4,100},{8,104},{12,108},{16,112},{20,116},{24,120},{28,124... | collective-permute-start | bytes 589832 | tf_op jit(solution)/shard_map/ppermute | solution.py:103
  41.1 8.4 %collective-permute-start.5 = (bf16[32,3072]{1,0:T(8,128)(2,1)S(1)}, bf16[32,3072]{1,0:T(8,128)(2,1)S(1)}, u32[]{:S(2)}, u32[]{:S(2)}) collective-permute-start(bf16[32,3072]{1,0:T(8,128)(2,1)S(1)} %add_add_fusion.1), channel_id=1, source_target_pairs={{0,64},{4,68},{8,72},{12,76},{16,80},{20,84},{24,88},{28,92},{32,9... | collective-permute-start | bytes 589832 | tf_op jit(solution)/shard_map/ppermute | solution.py:103
  41.1 8.8 %collective-permute-start.4 = (bf16[32,3072]{1,0:T(8,128)(2,1)S(1)}, bf16[32,3072]{1,0:T(8,128)(2,1)S(1)}, u32[]{:S(2)}, u32[]{:S(2)}) collective-permute-start(bf16[32,3072]{1,0:T(8,128)(2,1)S(1)} %add_add_fusion.1), channel_id=1, source_target_pairs={{0,32},{4,36},{8,40},{12,44},{16,48},{20,52},{24,56},{28,60},{32,0... | collective-permute-start | bytes 589832 | tf_op jit(solution)/shard_map/ppermute | solution.py:103
  60.9 1.1 copy-start

commit v5 on v4

--- a/solution.py
+++ b/solution.py
@@ -38,57 +38,56 @@
     main = extended[:, tap_limit - 1 :].reshape(channels, count, block)
     prefix = extended[:, :length].reshape(channels, count, block)[:, :, : tap_limit - 1]
     pieces = jnp.concatenate([prefix, main], axis=2)
-    result = jnp.einsum(
-        "cnu,btu->bcnt", pieces, band_matrix(fir, taps, block), preferred_element_type=jnp.float32
+    return jnp.einsum(
+        "cnu,btu->bnct", pieces, band_matrix(fir, taps, block), preferred_element_type=jnp.float32
     )
-    return result.reshape(result.shape[0], channels, length)
 
 
-def corr_kernel(fw_ref, pp_ref, out_ref, acc_ref, *, chunks, groups, rows_f, rows_p):
+def corr_kernel(off_ref, fw_ref, pp_ref, out_ref, acc_ref, *, chunks, groups, scale):
     acc_ref[...] = jnp.zeros_like(acc_ref)
-    top = (groups - 1) * SHIFTS
+    per = CHUNK // 128
+    off = off_ref[0]
 
     def step(k, carry):
-        base = pl.multiple_of(k * CHUNK, CHUNK)
-        fa = fw_ref[0, :, pl.ds(base, CHUNK + 128)]
-        pa = pp_ref[0, :, pl.ds(base, CHUNK + 128)]
+        first = k * per
+        fa = jnp.concatenate([fw_ref[0, off + first + i] for i in range(per + 1)], axis=1)
+        pa = jnp.concatenate([pp_ref[0, first + i] for i in range(per + 1)], axis=1)
         lhs = jnp.concatenate([fa[:, q : q + CHUNK] for q in range(SHIFTS)], axis=0)
         rhs = jnp.concatenate(
-            [pa[:, top - g * SHIFTS : top - g * SHIFTS + CHUNK] for g in range(groups)], axis=0
+            [pa[:, 128 - g * SHIFTS : 128 - g * SHIFTS + CHUNK] for g in range(groups)], axis=0
         )
         acc_ref[...] += lax.dot_general(
-            lhs.astype(jnp.bfloat16),
-            rhs.astype(jnp.bfloat16),
-            (((1,), (1,)), ((), ())),
-            preferred_element_type=jnp.float32,
+            lhs, rhs, (((1,), (1,)), ((), ())), preferred_element_type=jnp.float32
         )
         return carry
 
     lax.fori_loop(0, chunks, step, 0)
-    out_ref[0] = acc_ref[...]
+    out_ref[0] = (acc_ref[...] * scale).astype(out_ref.dtype)
 
 
-def correlate(f_win, p_pad, lags, chunks):
-    bands, rows_f, width = f_win.shape
-    rows_p = p_pad.shape[1]
+def correlate(offset, f_blocks, p_blocks, lags, chunks, scale):
+    bands, nf, rows_f, _ = f_blocks.shape
+    np_, rows_p = p_blocks.shape[1], p_blocks.shape[2]
     groups = lags // SHIFTS
-    kernel = functools.partial(
-        corr_kernel, chunks=chunks, groups=groups, rows_f=rows_f, rows_p=rows_p
-    )
+    kernel = functools.partial(corr_kernel, chunks=chunks, groups=groups, scale=scale)
     m = SHIFTS * rows_f
     n = groups * rows_p
+    grid_spec = pltpu.PrefetchScalarGridSpec(
+        num_scalar_prefetch=1,
+        grid=(bands,),
+        in_specs=[
+            pl.BlockSpec((1, nf, rows_f, 128), lambda b, o: (b, 0, 0, 0)),
+            pl.BlockSpec((1, np_, rows_p, 128), lambda b, o: (b, 0, 0, 0)),
+        ],
+        out_specs=pl.BlockSpec((1, m, n), lambda b, o: (b, 0, 0)),
+        scratch_shapes=[pltpu.VMEM((m, n), jnp.float32)],
+    )
     return pl.pallas_call(
         kernel,
-        grid=(bands,),
-        in_specs=[
-            pl.BlockSpec((1, rows_f, width), lambda b: (b, 0, 0)),
-            pl.BlockSpec((1, rows_p, width), lambda b: (b, 0, 0)),
-        ],
-        out_specs=pl.BlockSpec((1, m, n), lambda b: (b, 0, 0)),
-        out_shape=jax.ShapeDtypeStruct((bands, m, n), jnp.float32),
-        scratch_shapes=[pltpu.VMEM((m, n), jnp.float32)],
+        grid_spec=grid_spec,
+        out_shape=jax.ShapeDtypeStruct((bands, m, n), jnp.bfloat16),
         compiler_params=pltpu.CompilerParams(vmem_limit_bytes=48 * 1024 * 1024),
-    )(f_win, p_pad)
+    )(offset, f_blocks, p_blocks)
 
 
 def summed_over(value, axis):
@@ -129,23 +128,24 @@
         extended = jnp.concatenate(
             [jnp.zeros((rows.shape[0], tap_limit - 1), rows.dtype), rows], axis=1
         )
-        return filter_blocks(extended, fir, taps, samples_all, 256).astype(jnp.bfloat16)
+        return filter_blocks(extended, fir, taps, samples_all, 128).astype(jnp.bfloat16)
 
     f_loc = filtered_of(signal)
     p_src = filtered_of(picks)
 
     span = samples_all + (groups - 1) * SHIFTS
     chunks = -(-span // CHUNK)
-    width = chunks * CHUNK + 128
-    f_big = jnp.pad(f_loc, ((0, 0), (0, 0), (MAXLAG, width - samples_all + lag_count)))
-    start = lax.axis_index("tm") * share
-    f_win = lax.dynamic_slice_in_dim(f_big, start, width, 2)
-    top = (groups - 1) * SHIFTS
-    p_pad = jnp.pad(p_src, ((0, 0), (0, 0), (top, width - samples_all - top)))
+    blocks = chunks * CHUNK // 128 + 1
+    data_blocks = samples_all // 128
+    f_front = MAXLAG // 128
+    f_blocks = jnp.pad(
+        f_loc, ((0, 0), (f_front, blocks + lag_count // 128 - data_blocks - f_front), (0, 0), (0, 0))
+    )
+    p_blocks = jnp.pad(p_src, ((0, 0), (1, blocks - data_blocks - 1), (0, 0), (0, 0)))
+    offset = (lax.axis_index("tm") * (share // 128)).astype(jnp.int32).reshape(1)
 
-    out = correlate(f_win, p_pad, share, chunks)
+    out = correlate(offset, f_blocks, p_blocks, share, chunks, norm_scale)
     bands = out.shape[0]
-    out = (out * norm_scale).astype(jnp.bfloat16)
     out = out.reshape(bands, SHIFTS, channels, groups, ROUNDS, count_src)
     out = jnp.transpose(out, (4, 0, 5, 2, 3, 1))
     return out.reshape(ROUNDS, bands, count_src, channels, share)

time: 127 us -> 103 us (0.81)
  local copies, waits for them, and re-layouts: 37.2 us -> 26.3 us
  Pallas kernels: 36.5 us -> 26.7 us
  matrix products: 7.98 us -> 3.19 us
  other arithmetic: 2.12 us -> 4.29 us
    pallas_call x1, Pallas kernels: 36.5 us -> 26.7 us  [correlate(): pl.pallas_call(kernel, grid_spec=grid_spec, out_shape=jax.ShapeDtypeStruc...]
    convert_element_type x3 -> x0, local copies, waits for them, and re-layouts: 9.13 us -> none  [the longest x2 8.59 us: filtered_of(): filter_blocks(extended, fir, taps, samples_all, 256).astype(jnp.bfloat16)]
    dot_general x2, matrix products: 6.81 us -> 2.02 us  [filter_blocks(): jnp.einsum('cnu,btu->bnct', pieces, band_matrix(fir, taps, block), prefer...]
    concatenate x0 -> x2, local copies, waits for them, and re-layouts: none -> 4.7 us  [filter_blocks(): pieces = jnp.concatenate([prefix, main], axis=2)]
    dynamic_slice x1 -> x0, local copies, waits for them, and re-layouts: 2.13 us -> none  [per_device(): f_win = lax.dynamic_slice_in_dim(f_big, start, width, 2)]
    reshape x1, local copies, waits for them, and re-layouts: 2.39 us -> 0.63 us  [skew(): repeated[..., :count_rows * (row_width - 1)]]
    pad x1 -> x2, local copies, waits for them, and re-layouts: 4.58 us -> 2.86 us  [the longest x1 2.3 us: per_device(): jnp.pad(f_loc, ((0, 0), (f_front, blocks + lag_count // 128 - data_blocks...]
    slice x4 -> x0, local copies, waits for them, and re-layouts: 1.42 us -> none  [filter_blocks(): extended[:, :length].reshape(channels, count, block)[:, :, :tap_limit - 1]]
  transfers between devices with their start and end apart: 7 -> 7, of which waited for: 4 -> 4; matrix products, arithmetic and copies ran while one was open for 11% -> 9% of each run, Pallas kernels for 0% -> 0%
where the time goes in v5:
time: 103 us
  Pallas kernels  26.7 us (26%)
  local copies, waits for them, and re-layouts  26.3 us (26%)
  blocking collectives  24.1 us (23%)
  starting transfers between devices  9.94 us (10%)
  waiting for transfers between devices  8.33 us (8%)
  other arithmetic  4.29 us (4%)
  matrix products  3.19 us (3%)
    pallas_call x1, Pallas kernels, correlate(): pl.pallas_call(kernel, grid_spec=grid_spec, out_shape=jax.ShapeDtypeStruc...  26.7 us
    all_gather x2, blocking collectives, filtered_of(): rows = lax.all_gather(rows, 'tm', axis=1, tiled=True)  24.1 us
    ppermute x7, starting transfers between devices, summed_over(): lax.ppermute(value, axis, [(i, i ^ m) for i in range(count)])  9.94 us
    ppermute x7, waiting for transfers between devices, summed_over(): lax.ppermute(value, axis, [(i, i ^ m) for i in range(count)])  8.33 us
    transpose x1, local copies, waits for them, and re-layouts, per_device(): out = jnp.transpose(out, (4, 0, 5, 2, 3, 1))  5.38 us
    concatenate x2, local copies, waits for them, and re-layouts, filter_blocks(): pieces = jnp.concatenate([prefix, main], axis=2)  4.7 us
    reshape x1, local copies, waits for them, and re-layouts, per_device(): return out.reshape(ROUNDS, bands, count_src, channels, share)  4.56 us
    reshape x1, local copies, waits for them, and re-layouts, per_device(): out = out.reshape(bands, SHIFTS, channels, groups, ROUNDS, count_src)  3.82 us
  transfers between devices with their start and end apart: 7, of which 4 were waited for; matrix products, arithmetic and copies ran while one was open for 9% of the time, Pallas kernels for 0%

profile of v5, /device:TPU:1, one launch (start us, length us, event | category | flops | bytes accessed | tf_op | source)
XLA Modules:
  0.0 103.0 jit_solution(4054559185348173172)
XLA Ops:
  0.0 0.7 broadcast_subtract_fusion
  0.8 1.2 %convolution_convert_fusion = bf16[32,3072]{1,0:T(8,128)(2,1)S(1)} fusion(bf16[32,3072]{1,0:T(8,128)(2,1)} %param.4, s32[32]{0:T(128)S(1)} %sub.15), kind=kOutput, calls=%fused_computation | convolution fusion | flops 6390784 | bytes 393344 | tf_op jit(solution)/shard_map/dot_general | solution.py:123
  1.9 2.1 %collective-permute-start = (bf16[32,3072]{1,0:T(8,128)(2,1)S(1)}, bf16[32,3072]{1,0:T(8,128)(2,1)S(1)}, u32[]{:S(2)}, u32[]{:S(2)}) collective-permute-start(bf16[32,3072]{1,0:T(8,128)(2,1)S(1)} %convolution_convert_fusion), channel_id=1, source_target_pairs={{0,4},{4,0},{8,12},{12,8},{16,20},{20,16},{24,28},{28,24},{32,36},... | collective-permute-start | bytes 589832 | tf_op jit(solution)/shard_map/ppermute | solution.py:102
  4.1 13.2 %all_gather.6 = bf16[32,12288]{1,0:T(8,128)(2,1)S(1)} all-gather(bf16[32,3072]{1,0:T(8,128)(2,1)} %param.4), channel_id=1, replica_groups=mesh['sta'=32,'tm'=4] {'tm'}, dimensions={1}, use_global_device_ids=true | all-gather | bytes 983040 | tf_op jit(solution)/shard_map/all_gather | solution.py:127
  17.3 0.8 select_convert_fusion
  18.1 0.7 add.31
  18.8 2.7 %collective-permute-start.3 = (bf16[32,3072]{1,0:T(8,128)(2,1)}, bf16[32,3072]{1,0:T(8,128)(2,1)}, u32[]{:S(2)}, u32[]{:S(2)}) collective-permute-start(bf16[32,3072]{1,0:T(8,128)(2,1)} %add.31), channel_id=1, source_target_pairs={{0,24},{4,28},{8,16},{12,20},{16,8},{20,12},{24,0},{28,4},{32,56},... | collective-permute-start | bytes 589832 | tf_op jit(solution)/shard_map/ppermute | solution.py:102
  23.7 0.7 copy.11
  25.3 2.4 %copy.22 = bf16[32,96,159,1]{2,0,1,3:T(8,128)(2,1)S(1)} copy(bf16[32,96,159,1]{1,2,0,3:T(8,128)(2,1)S(1)} %maximum_bitcast_fusion) | data formatting | bytes 1953792 | tf_op jit(solution)/shard_map/concatenate | solution.py:40
  27.7 3.0 %collective-permute-done.3 = bf16[32,3072]{1,0:T(8,128)(2,1)} collective-permute-done((bf16[32,3072]{1,0:T(8,128)(2,1)}, bf16[32,3072]{1,0:T(8,128)(2,1)}, u32[]{:S(2)}, u32[]{:S(2)}) %collective-permute-start.3) | collective-permute-done | bytes 196640 | tf_op jit(solution)/shard_map/ppermute | solution.py:102
  31.3 1.3 %add_add_fusion.1 = bf16[32,3072]{1,0:T(8,128)(2,1)S(1)} fusion(bf16[32,3072]{1,0:T(8,128)(2,1)} %collective-permute-done.3, bf16[32,3072]{1,0:T(8,128)(2,1)} %collective-permute-done.2, bf16[32,3072]{1,0:T(8,128)(2,1)} %add.31, bf16[32,3072]{1,0:T(8,128)(2,1)} %collective-permute-done.1), kind=kLoop, calls=%fused_computation.12 | loop fusion | flops 294912 | bytes 983040 | tf_op jit(solution)/shard_map/add | solution.py:103
  32.5 3.9 %collective-permute-start.6 = (bf16[32,3072]{1,0:T(8,128)(2,1)S(1)}, bf16[32,3072]{1,0:T(8,128)(2,1)S(1)}, u32[]{:S(2)}, u32[]{:S(2)}) collective-permute-start(bf16[32,3072]{1,0:T(8,128)(2,1)S(1)} %add_add_fusion.1), channel_id=1, source_target_pairs={{0,96},{4,100},{8,104},{12,108},{16,112},{20,116},{24,120},{28,124... | collective-permute-start | bytes 589832 | tf_op jit(solution)/shard_map/ppermute | solution.py:102
  36.4 0.7 collective-permute-start.4
  37.1 1.0 convert_bitcast_fusion.1
  38.1 2.3 %pad.11.fw_ref = bf16[4,105,32,128]{3,2,1,0:T(8,128)(2,1)} pad(bf16[4,96,32,128]{3,2,1,0:T(8,128)(2,1)S(1)} %convert_bitcast_fusion.1, bf16[]{:T(256)} %constant.4.clone.1), padding=0_0x2_7x0_0x0_0 | pad | bytes 6586370 | tf_op jit(solution)/shard_map/jit(_pad)/pad | solution.py:141
  40.4 4.5 %collective-permute-done.6 = bf16[32,3072]{1,0:T(8,128)(2,1)S(1)} collective-permute-done((bf16[32,3072]{1,0:T(8,128)(2,1)S(1)}, bf16[32,3072]{1,0:T(8,128)(2,1)S(1)}, u32[]{:S(2)}, u32[]{:S(2)}) %collective-permute-start.6) | collective-permute-done | bytes 196640 | tf_op jit(solution)/shard_map/ppermute | solution.py:102
  45.2 10.8 %all_gather.7 = bf16[32,12288]{1,0:T(8,128)(2,1)S(1)} all-gather(bf16[32,3072]{1,0:T(8,128)(2,1)S(1)} %add_add_fusion), channel_id=1, replica_groups=mesh['sta'=32,'tm'=4] {'tm'}, dimensions={1}, use_global_device_ids=true | all-gather | bytes 983040 | tf_op jit(solution)/shard_map/all_gather | solution.py:127
  56.4 0.7 copy.15
  58.0 2.4 %copy.25 = bf16[32,96,159,1]{2,0,1,3:T(8,128)(2,1)S(1)} copy(bf16[32,96,159,1]{1,2,0,3:T(8,128)(2,1)S(1)} %maximum_bitcast_fusion.1) | data formatting | bytes 1953792 | tf_op jit(solution)/shard_map/concatenate | solution.py:40
  60.4 1.0 convert_bitcast_fusion
  61.9 26.7 %shard_map.46 = bf16[4,512,256]{2,1,0:T(8,128)(2,1)S(1)} custom-call(s32[1]{0:T(128)} %bitcast.off_ref, bf16[4,105,32,128]{3,2,1,0:T(8,128)(2,1)} %pad.11.fw_ref, bf16[4,101,32,128]{3,2,1,0:T(8,128)(2,1)S(1)} %pad.12.pp_ref), custom_call_target="tpu_custom_call" | custom-call | tf_op jit(solution)/shard_map/pallas_call | solution.py:85
  89.2 3.8 %reshape.44 = bf16[4,16,32,8,2,16]{2,1,5,4,3,0:T(8,128)(2,1)} reshape(bf16[4,512,256]{1,2,0:T(8,128)(2,1)S(1)} %copy.18) | data formatting | bytes 2097152 | tf_op jit(solution)/shard_map/reshape | solution.py:149
  93.0 5.4 %copy.19 = bf16[2,4,16,32,8,16]{3,5,4,2,1,0:T(8,128)(2,1)} copy(bf16[2,4,16,32,8,16]{3,5,2,0,4,1:T(8,128)(2,1)} %bitcast.36) | data formatting | bytes 2097152 | tf_op jit(solution)/shard_map/transpose | solution.py:150
  98.4 4.6 %copy.20 = bf16[2,4,16,32,128]{4,3,2,1,0:T(8,128)(2,1)} copy(bf16[2,4,16,32,128]{3,4,2,1,0:T(8,128)(2,1)} %bitcast.37) | data formatting | bytes 2097152 | tf_op jit(solution)/shard_map/reshape | solution.py:151
  (28 shorter events, 6.6 us)
Async XLA Ops:
  1.9 16.1 %collective-permute-start = (bf16[32,3072]{1,0:T(8,128)(2,1)S(1)}, bf16[32,3072]{1,0:T(8,128)(2,1)S(1)}, u32[]{:S(2)}, u32[]{:S(2)}) collective-permute-start(bf16[32,3072]{1,0:T(8,128)(2,1)S(1)} %convolution_convert_fusion), channel_id=1, source_target_pairs={{0,4},{4,0},{8,12},{12,8},{16,20},{20,16},{24,28},{28,24},{32,36},... | collective-permute-start | bytes 589832 | tf_op jit(solution)/shard_map/ppermute | solution.py:102
  18.8 11.9 %collective-permute-start.3 = (bf16[32,3072]{1,0:T(8,128)(2,1)}, bf16[32,3072]{1,0:T(8,128)(2,1)}, u32[]{:S(2)}, u32[]{:S(2)}) collective-permute-start(bf16[32,3072]{1,0:T(8,128)(2,1)} %add.31), channel_id=1, source_target_pairs={{0,24},{4,28},{8,16},{12,20},{16,8},{20,12},{24,0},{28,4},{32,56},... | collective-permute-start | bytes 589832 | tf_op jit(solution)/shard_map/ppermute | solution.py:102
  21.5 9.2 %collective-permute-start.2 = (bf16[32,3072]{1,0:T(8,128)(2,1)}, bf16[32,3072]{1,0:T(8,128)(2,1)}, u32[]{:S(2)}, u32[]{:S(2)}) collective-permute-start(bf16[32,3072]{1,0:T(8,128)(2,1)} %add.31), channel_id=1, source_target_pairs={{0,16},{4,20},{8,24},{12,28},{16,0},{20,4},{24,8},{28,12},{32,48},... | collective-permute-start | bytes 589832 | tf_op jit(solution)/shard_map/ppermute | solution.py:102
  21.9 9.4 %collective-permute-start.1 = (bf16[32,3072]{1,0:T(8,128)(2,1)}, bf16[32,3072]{1,0:T(8,128)(2,1)}, u32[]{:S(2)}, u32[]{:S(2)}) collective-permute-start(bf16[32,3072]{1,0:T(8,128)(2,1)} %add.31), channel_id=1, source_target_pairs={{0,8},{4,12},{8,0},{12,4},{16,24},{20,28},{24,16},{28,20},{32,40},... | collective-permute-start | bytes 589832 | tf_op jit(solution)/shard_map/ppermute | solution.py:102
  32.5 12.3 %collective-permute-start.6 = (bf16[32,3072]{1,0:T(8,128)(2,1)S(1)}, bf16[32,3072]{1,0:T(8,128)(2,1)S(1)}, u32[]{:S(2)}, u32[]{:S(2)}) collective-permute-start(bf16[32,3072]{1,0:T(8,128)(2,1)S(1)} %add_add_fusion.1), channel_id=1, source_target_pairs={{0,96},{4,100},{8,104},{12,108},{16,112},{20,116},{24,120},{28,124... | collective-permute-start | bytes 589832 | tf_op jit(solution)/shard_map/ppermute | solution.py:102
  36.4 8.4 %collective-permute-start.5 = (bf16[32,3072]{1,0:T(8,128)(2,1)S(1)}, bf16[32,3072]{1,0:T(8,128)(2,1)S(1)}, u32[]{:S(2)}, u32[]{:S(2)}) collective-permute-start(bf16[32,3072]{1,0:T(8,128)(2,1)S(1)} %add_add_fusion.1), channel_id=1, source_target_pairs={{0,64},{4,68},{8,72},{12,76},{16,80},{20,84},{24,88},{28,92},{32,9... | collective-permute-start | bytes 589832 | tf_op jit(solution)/shard_map/ppermute | solution.py:102
  36.4 8.7 %collective-permute-start.4 = (bf16[32,3072]{1,0:T(8,128)(2,1)S(1)}, bf16[32,3072]{1,0:T(8,128)(2,1)S(1)}, u32[]{:S(2)}, u32[]{:S(2)}) collective-permute-start(bf16[32,3072]{1,0:T(8,128)(2,1)S(1)} %add_add_fusion.1), channel_id=1, source_target_pairs={{0,32},{4,36},{8,40},{12,44},{16,48},{20,52},{24,56},{28,60},{32,0... | collective-permute-start | bytes 589832 | tf_op jit(solution)/shard_map/ppermute | solution.py:102

commit v6 on v5

--- a/solution.py
+++ b/solution.py
@@ -130,8 +130,9 @@
         )
         return filter_blocks(extended, fir, taps, samples_all, 128).astype(jnp.bfloat16)
 
-    f_loc = filtered_of(signal)
-    p_src = filtered_of(picks)
+    both = filtered_of(jnp.concatenate([signal, picks], axis=0))
+    f_loc = both[:, :, :channels]
+    p_src = both[:, :, channels:]
 
     span = samples_all + (groups - 1) * SHIFTS
     chunks = -(-span // CHUNK)

time: 103 us -> 143 us (1.39)
  waiting for transfers between devices: 8.33 us -> 46.1 us
  blocking collectives: 24.1 us -> 0 us
  between operations: 0.18 us -> 13.5 us
  local copies, waits for them, and re-layouts: 26.3 us -> 36.8 us
    all_gather x0 -> x1, waiting for transfers between devices: none -> 27.1 us  [filtered_of(): rows = lax.all_gather(rows, 'tm', axis=1, tiled=True)]
    all_gather x2 -> x0, blocking collectives: 24.1 us -> none  [filtered_of(): rows = lax.all_gather(rows, 'tm', axis=1, tiled=True)]
    ppermute x7, waiting for transfers between devices: 8.33 us -> 19.1 us  [summed_over(): lax.ppermute(value, axis, [(i, i ^ m) for i in range(count)])]
    unnamed x8, local copies, waits for them, and re-layouts: 1.83 us -> 8.11 us
    add x3, other arithmetic: 2.02 us -> 0.13 us  [summed_over(): value = sum(parts, value)]
    reshape x2 -> x1, local copies, waits for them, and re-layouts: 1.31 us -> 3.1 us  [filter_blocks(): main = extended[:, tap_limit - 1:].reshape(channels, count, block)]
    concatenate x0 -> x1, other arithmetic: none -> 1.7 us  [per_device(): both = filtered_of(jnp.concatenate([signal, picks], axis=0))]
    concatenate x2 -> x1, other arithmetic: 0.83 us -> 2.39 us  [filter_blocks(): pieces = jnp.concatenate([prefix, main], axis=2)]
  transfers between devices with their start and end apart: 7 -> 8, of which waited for: 4 -> 5; matrix products, arithmetic and copies ran while one was open for 9% -> 1% of each run, Pallas kernels for 0% -> 0%
where the time goes in v6:
time: 143 us; the launch traced here: 142 us
  waiting for transfers between devices  46.1 us (32%)
  local copies, waits for them, and re-layouts  36.8 us (26%)
  Pallas kernels  26.7 us (19%)
  between operations  13.5 us (9%)
  starting transfers between devices  10.4 us (7%)
  other arithmetic  5 us (3%)
  matrix products  3.55 us (2%)
    all_gather x1, waiting for transfers between devices, filtered_of(): rows = lax.all_gather(rows, 'tm', axis=1, tiled=True)  27.1 us
    pallas_call x1, Pallas kernels, correlate(): pl.pallas_call(kernel, grid_spec=grid_spec, out_shape=jax.ShapeDtypeStruc...  26.7 us
    ppermute x7, waiting for transfers between devices, summed_over(): lax.ppermute(value, axis, [(i, i ^ m) for i in range(count)])  19.1 us
    ppermute x7, starting transfers between devices, summed_over(): lax.ppermute(value, axis, [(i, i ^ m) for i in range(count)])  10.4 us
    unnamed x8, local copies, waits for them, and re-layouts  8.11 us
    concatenate x1, local copies, waits for them, and re-layouts, filter_blocks(): pieces = jnp.concatenate([prefix, main], axis=2)  5.56 us
    transpose x1, local copies, waits for them, and re-layouts, per_device(): out = jnp.transpose(out, (4, 0, 5, 2, 3, 1))  5.37 us
    reshape x1, local copies, waits for them, and re-layouts, per_device(): return out.reshape(ROUNDS, bands, count_src, channels, share)  4.56 us
  transfers between devices with their start and end apart: 8, of which 5 were waited for; matrix products, arithmetic and copies ran while one was open for 1% of the time, Pallas kernels for 0%

profile of v6, /device:TPU:1, one launch (start us, length us, event | category | flops | bytes accessed | tf_op | source)
XLA Modules:
  0.0 142.1 jit_solution(11507220647631638872)
XLA Ops:
  7.3 1.2 convolution_convert_fusion
  8.5 2.1 %collective-permute-start = (bf16[32,3072]{1,0:T(8,128)(2,1)S(1)}, bf16[32,3072]{1,0:T(8,128)(2,1)S(1)}, u32[]{:S(2)}, u32[]{:S(2)}) collective-permute-start(bf16[32,3072]{1,0:T(8,128)(2,1)S(1)} %convolution_convert_fusion), channel_id=1, source_target_pairs={{0,4},{4,0},{8,12},{12,8},{16,20},{20,16},{24,28},{28,24},{32,36},... | collective-permute-start | bytes 589832 | tf_op jit(solution)/shard_map/ppermute | solution.py:102
  10.6 4.2 %collective-permute-done = bf16[32,3072]{1,0:T(8,128)(2,1)S(1)} collective-permute-done((bf16[32,3072]{1,0:T(8,128)(2,1)S(1)}, bf16[32,3072]{1,0:T(8,128)(2,1)S(1)}, u32[]{:S(2)}, u32[]{:S(2)}) %collective-permute-start) | collective-permute-done | bytes 196640 | tf_op jit(solution)/shard_map/ppermute | solution.py:102
  14.9 3.2 %collective-permute-start.3 = (bf16[32,3072]{1,0:T(8,128)(2,1)S(1)}, bf16[32,3072]{1,0:T(8,128)(2,1)S(1)}, u32[]{:S(2)}, u32[]{:S(2)}) collective-permute-start(bf16[32,3072]{1,0:T(8,128)(2,1)S(1)} %add.29), channel_id=1, source_target_pairs={{0,24},{4,28},{8,16},{12,20},{16,8},{20,12},{24,0},{28,4},{32,56},... | collective-permute-start | bytes 589832 | tf_op jit(solution)/shard_map/ppermute | solution.py:102
  18.7 7.6 %collective-permute-done.3 = bf16[32,3072]{1,0:T(8,128)(2,1)S(1)} collective-permute-done((bf16[32,3072]{1,0:T(8,128)(2,1)S(1)}, bf16[32,3072]{1,0:T(8,128)(2,1)S(1)}, u32[]{:S(2)}, u32[]{:S(2)}) %collective-permute-start.3) | collective-permute-done | bytes 196640 | tf_op jit(solution)/shard_map/ppermute | solution.py:102
  26.5 3.7 %collective-permute-start.6 = (bf16[32,3072]{1,0:T(8,128)(2,1)S(1)}, bf16[32,3072]{1,0:T(8,128)(2,1)S(1)}, u32[]{:S(2)}, u32[]{:S(2)}) collective-permute-start(bf16[32,3072]{1,0:T(8,128)(2,1)S(1)} %add_add_fusion.1), channel_id=1, source_target_pairs={{0,96},{4,100},{8,104},{12,108},{16,112},{20,116},{24,120},{28,124... | collective-permute-start | bytes 589832 | tf_op jit(solution)/shard_map/ppermute | solution.py:102
  30.9 7.1 %collective-permute-done.6 = bf16[32,3072]{1,0:T(8,128)(2,1)S(1)} collective-permute-done((bf16[32,3072]{1,0:T(8,128)(2,1)S(1)}, bf16[32,3072]{1,0:T(8,128)(2,1)S(1)}, u32[]{:S(2)}, u32[]{:S(2)}) %collective-permute-start.6) | collective-permute-done | bytes 196640 | tf_op jit(solution)/shard_map/ppermute | solution.py:102
  38.1 1.7 %pad_maximum_fusion = bf16[64,3072]{1,0:T(8,128)(2,1)} fusion(bf16[32,3072]{1,0:T(8,128)(2,1)S(1)} %add_add_fusion, bf16[32,3072]{1,0:T(8,128)(2,1)} %param.4), kind=kLoop, calls=%fused_computation.5 | loop fusion | flops 786432 | bytes 786432 | tf_op jit(solution)/shard_map/concatenate | solution.py:133
  41.1 27.1 %all-gather.2.cloned.1.call-done = bf16[64,12288]{1,0:T(8,128)(2,1)} async-done(((bf16[64,3072]{1,0:T(8,128)(2,1)}), bf16[64,12288]{1,0:T(8,128)(2,1)}) %all-gather.2.cloned.1.call-update) | async-done | bytes 1572880 | tf_op jit(solution)/shard_map/all_gather | solution.py:127
  68.2 2.9 %copy.23 = bf16[8,8,96,128]{3,2,1,0:T(8,128)(2,1)} copy(bf16[8,8,96,128]{3,1,2,0:T(8,128)(2,1)} %bitcast.24) | data formatting | bytes 3145728
  71.0 3.1 %copy.10 = bf16[64,96,128]{1,2,0:T(8,128)(2,1)S(1)} copy(bf16[64,96,128]{2,1,0:T(8,128)(2,1)} %bitcast.26) | data formatting | bytes 3145728 | tf_op jit(solution)/shard_map/reshape | solution.py:38
  74.2 1.9 %fusion = bf16[8,8,96,128]{3,1,2,0:T(8,128)(2,1)S(1)} fusion(bf16[64,12288]{1,0:T(8,128)(2,1)} %all-gather.2.cloned.1.call-done), kind=kLoop, calls=%fused_computation.4 | loop fusion | bytes 3145728
  76.1 1.5 %copy.22 = bf16[8,8,96,128]{3,2,1,0:T(8,128)(2,1)} copy(bf16[8,8,96,128]{3,1,2,0:T(8,128)(2,1)S(1)} %fusion) | data formatting | bytes 3145728
  77.6 1.8 %copy.21 = bf16[64,96,31]{1,2,0:T(8,128)(2,1)S(1)} copy(bf16[64,96,31]{2,1,0:T(8,128)(2,1)} %bitcast.25) | data formatting | bytes 761856
  79.4 2.4 %maximum_bitcast_fusion = bf16[64,96,159,1]{1,2,0,3:T(8,128)(2,1)} fusion(bf16[64,96,128]{1,2,0:T(8,128)(2,1)S(1)} %copy.10, bf16[64,96,31]{1,2,0:T(8,128)(2,1)S(1)} %copy.21), kind=kLoop, calls=%fused_computation.2 | loop fusion | flops 3907584 | bytes 3907584 | tf_op jit(solution)/shard_map/concatenate | solution.py:40
  81.8 5.6 %copy.17 = bf16[64,96,159,1]{2,0,1,3:T(8,128)(2,1)S(1)} copy(bf16[64,96,159,1]{1,2,0,3:T(8,128)(2,1)} %maximum_bitcast_fusion) | data formatting | bytes 3907584 | tf_op jit(solution)/shard_map/concatenate | solution.py:40
  87.4 2.4 %convert_bitcast_fusion = bf16[4,96,64,128]{3,2,1,0:T(8,128)(2,1)S(1)} fusion(bf16[64,96,159,1]{2,0,1,3:T(8,128)(2,1)S(1)} %copy.17, bf16[4,128,159]{2,1,0:T(8,128)(2,1)S(1)} %reshape.32), kind=kOutput, calls=%fused_computation | convolution fusion | flops 1003487232 | bytes 8408064 | tf_op jit(solution)/shard_map/cnu,btu->bnct/dot_general | solution.py:41
  89.7 1.3 fusion.3
  91.1 0.7 pad.11.pp_ref
  91.8 2.4 %pad.10.fw_ref = bf16[4,105,32,128]{3,2,1,0:T(8,128)(2,1)} pad(bf16[4,96,32,128]{3,2,1,0:T(8,128)(2,1)S(1)} %get-tuple-element.6, bf16[]{:T(256)} %constant.4.clone.1), padding=0_0x2_7x0_0x0_0 | pad | bytes 6586370 | tf_op jit(solution)/shard_map/jit(_pad)/pad | solution.py:142
  94.3 26.7 %shard_map.46 = bf16[4,512,256]{2,1,0:T(8,128)(2,1)S(1)} custom-call(s32[1]{0:T(128)} %bitcast.off_ref, bf16[4,105,32,128]{3,2,1,0:T(8,128)(2,1)} %pad.10.fw_ref, bf16[4,101,32,128]{3,2,1,0:T(8,128)(2,1)S(1)} %pad.11.pp_ref), custom_call_target="tpu_custom_call" | custom-call | tf_op jit(solution)/shard_map/pallas_call | solution.py:85
  121.5 3.8 %reshape.35 = bf16[4,16,32,8,2,16]{2,1,5,4,3,0:T(8,128)(2,1)} reshape(bf16[4,512,256]{1,2,0:T(8,128)(2,1)S(1)} %copy.13) | data formatting | bytes 2097152 | tf_op jit(solution)/shard_map/reshape | solution.py:150
  125.3 5.4 %copy.14 = bf16[2,4,16,32,8,16]{3,5,4,2,1,0:T(8,128)(2,1)} copy(bf16[2,4,16,32,8,16]{3,5,2,0,4,1:T(8,128)(2,1)} %bitcast.22) | data formatting | bytes 2097152 | tf_op jit(solution)/shard_map/transpose | solution.py:151
  130.7 4.6 %copy.15 = bf16[2,4,16,32,128]{4,3,2,1,0:T(8,128)(2,1)} copy(bf16[2,4,16,32,128]{3,4,2,1,0:T(8,128)(2,1)} %bitcast.23) | data formatting | bytes 2097152 | tf_op jit(solution)/shard_map/reshape | solution.py:152
  (27 shorter events, 4.2 us)
Async XLA Ops:
  6.5 33.3 %copy-start.1 = (s32[4]{0:T(128)S(1)}, s32[4]{0:T(128)}, u32[]{:S(2)}) copy-start(s32[4]{0:T(128)} %param.6) | copy-start | bytes 52
  6.5 33.3 %copy-start = (f32[4,32]{1,0:T(4,128)S(1)}, f32[4,32]{1,0:T(4,128)}, u32[]{:S(2)}) copy-start(f32[4,32]{1,0:T(4,128)} %param.5) | copy-start | bytes 1540
  6.5 61.6 %all-gather.2.cloned.1.call-start = ((), (), s32[]{:S(2)}) async-start(), calls=%async_computation | async-start | bytes 1966080 | tf_op jit(solution)/shard_map/all_gather | solution.py:127
  8.5 6.3 %collective-permute-start = (bf16[32,3072]{1,0:T(8,128)(2,1)S(1)}, bf16[32,3072]{1,0:T(8,128)(2,1)S(1)}, u32[]{:S(2)}, u32[]{:S(2)}) collective-permute-start(bf16[32,3072]{1,0:T(8,128)(2,1)S(1)} %convolution_convert_fusion), channel_id=1, source_target_pairs={{0,4},{4,0},{8,12},{12,8},{16,20},{20,16},{24,28},{28,24},{32,36},... | collective-permute-start | bytes 589832 | tf_op jit(solution)/shard_map/ppermute | solution.py:102
  14.9 11.5 %collective-permute-start.3 = (bf16[32,3072]{1,0:T(8,128)(2,1)S(1)}, bf16[32,3072]{1,0:T(8,128)(2,1)S(1)}, u32[]{:S(2)}, u32[]{:S(2)}) collective-permute-start(bf16[32,3072]{1,0:T(8,128)(2,1)S(1)} %add.29), channel_id=1, source_target_pairs={{0,24},{4,28},{8,16},{12,20},{16,8},{20,12},{24,0},{28,4},{32,56},... | collective-permute-start | bytes 589832 | tf_op jit(solution)/shard_map/ppermute | solution.py:102
  18.1 8.3 %collective-permute-start.2 = (bf16[32,3072]{1,0:T(8,128)(2,1)S(1)}, bf16[32,3072]{1,0:T(8,128)(2,1)S(1)}, u32[]{:S(2)}, u32[]{:S(2)}) collective-permute-start(bf16[32,3072]{1,0:T(8,128)(2,1)S(1)} %add.29), channel_id=1, source_target_pairs={{0,16},{4,20},{8,24},{12,28},{16,0},{20,4},{24,8},{28,12},{32,48},... | collective-permute-start | bytes 589832 | tf_op jit(solution)/shard_map/ppermute | solution.py:102
  18.4 8.1 %collective-permute-start.1 = (bf16[32,3072]{1,0:T(8,128)(2,1)S(1)}, bf16[32,3072]{1,0:T(8,128)(2,1)S(1)}, u32[]{:S(2)}, u32[]{:S(2)}) collective-permute-start(bf16[32,3072]{1,0:T(8,128)(2,1)S(1)} %add.29), channel_id=1, source_target_pairs={{0,8},{4,12},{8,0},{12,4},{16,24},{20,28},{24,16},{28,20},{32,40},... | collective-permute-start | bytes 589832 | tf_op jit(solution)/shard_map/ppermute | solution.py:102
  26.5 11.5 %collective-permute-start.6 = (bf16[32,3072]{1,0:T(8,128)(2,1)S(1)}, bf16[32,3072]{1,0:T(8,128)(2,1)S(1)}, u32[]{:S(2)}, u32[]{:S(2)}) collective-permute-start(bf16[32,3072]{1,0:T(8,128)(2,1)S(1)} %add_add_fusion.1), channel_id=1, source_target_pairs={{0,96},{4,100},{8,104},{12,108},{16,112},{20,116},{24,120},{28,124... | collective-permute-start | bytes 589832 | tf_op jit(solution)/shard_map/ppermute | solution.py:102
  30.2 7.8 %collective-permute-start.5 = (bf16[32,3072]{1,0:T(8,128)(2,1)S(1)}, bf16[32,3072]{1,0:T(8,128)(2,1)S(1)}, u32[]{:S(2)}, u32[]{:S(2)}) collective-permute-start(bf16[32,3072]{1,0:T(8,128)(2,1)S(1)} %add_add_fusion.1), channel_id=1, source_target_pairs={{0,64},{4,68},{8,72},{12,76},{16,80},{20,84},{24,88},{28,92},{32,9... | collective-permute-start | bytes 589832 | tf_op jit(solution)/shard_map/ppermute | solution.py:102
  30.2 7.8 %collective-permute-start.4 = (bf16[32,3072]{1,0:T(8,128)(2,1)S(1)}, bf16[32,3072]{1,0:T(8,128)(2,1)S(1)}, u32[]{:S(2)}, u32[]{:S(2)}) collective-permute-start(bf16[32,3072]{1,0:T(8,128)(2,1)S(1)} %add_add_fusion.1), channel_id=1, source_target_pairs={{0,32},{4,36},{8,40},{12,44},{16,48},{20,52},{24,56},{28,60},{32,0... | collective-permute-start | bytes 589832 | tf_op jit(solution)/shard_map/ppermute | solution.py:102
Sparse Core Ops, SparseCore 0:
  39.9 28.2 all-gather.1

commit v7 on v5

--- a/solution.py
+++ b/solution.py
@@ -93,7 +93,7 @@
 def summed_over(value, axis):
     count = lax.axis_size(axis)
     bits = max(1, (count - 1).bit_length())
-    rounds = [[0]] + [list(range(b, min(b + 2, bits))) for b in range(1, bits, 2)]
+    rounds = [list(range(b, min(b + 2, bits))) for b in range(1, bits, 2)] + [[0]]
     for group in rounds:
         masks = [
             m for m in range(1, count)

time: 103 us -> 98.1 us (0.952)
  waiting for transfers between devices: 8.33 us -> 5.63 us
  blocking collectives: 24.1 us -> 22.4 us
    ppermute x7, waiting for transfers between devices: 8.33 us -> 5.63 us  [summed_over(): lax.ppermute(value, axis, [(i, i ^ m) for i in range(count)])]
    all_gather x2, blocking collectives: 24.1 us -> 22.4 us  [filtered_of(): rows = lax.all_gather(rows, 'tm', axis=1, tiled=True)]
  transfers between devices with their start and end apart: 7 -> 7, of which waited for: 4 -> 3; matrix products, arithmetic and copies ran while one was open for 9% -> 10% of each run, Pallas kernels for 0% -> 0%
where the time goes in v7:
time: 98.1 us; the launch traced here: 97.7 us
  Pallas kernels  26.7 us (27%)
  local copies, waits for them, and re-layouts  26.3 us (27%)
  blocking collectives  22.4 us (23%)
  starting transfers between devices  9.03 us (9%)
  waiting for transfers between devices  5.63 us (6%)
  other arithmetic  4.29 us (4%)
  matrix products  3.2 us (3%)
    pallas_call x1, Pallas kernels, correlate(): pl.pallas_call(kernel, grid_spec=grid_spec, out_shape=jax.ShapeDtypeStruc...  26.7 us
    all_gather x2, blocking collectives, filtered_of(): rows = lax.all_gather(rows, 'tm', axis=1, tiled=True)  22.4 us
    ppermute x7, starting transfers between devices, summed_over(): lax.ppermute(value, axis, [(i, i ^ m) for i in range(count)])  9.03 us
    ppermute x7, waiting for transfers between devices, summed_over(): lax.ppermute(value, axis, [(i, i ^ m) for i in range(count)])  5.63 us
    transpose x1, local copies, waits for them, and re-layouts, per_device(): out = jnp.transpose(out, (4, 0, 5, 2, 3, 1))  5.38 us
    concatenate x2, local copies, waits for them, and re-layouts, filter_blocks(): pieces = jnp.concatenate([prefix, main], axis=2)  4.7 us
    reshape x1, local copies, waits for them, and re-layouts, per_device(): return out.reshape(ROUNDS, bands, count_src, channels, share)  4.56 us
    reshape x1, local copies, waits for them, and re-layouts, per_device(): out = out.reshape(bands, SHIFTS, channels, groups, ROUNDS, count_src)  3.82 us
  transfers between devices with their start and end apart: 7, of which 3 were waited for; matrix products, arithmetic and copies ran while one was open for 10% of the time, Pallas kernels for 0%

profile of v7, /device:TPU:1, one launch (start us, length us, event | category | flops | bytes accessed | tf_op | source)
XLA Modules:
  0.0 97.7 jit_solution(8078333051367039889)
XLA Ops:
  0.0 0.7 broadcast_subtract_fusion
  0.8 1.2 %convolution_convert_fusion = bf16[32,3072]{1,0:T(8,128)(2,1)S(1)} fusion(bf16[32,3072]{1,0:T(8,128)(2,1)} %param.4, s32[32]{0:T(128)S(1)} %sub.15), kind=kOutput, calls=%fused_computation | convolution fusion | flops 6390784 | bytes 393344 | tf_op jit(solution)/shard_map/dot_general | solution.py:123
  1.9 3.6 %collective-permute-start.2 = (bf16[32,3072]{1,0:T(8,128)(2,1)S(1)}, bf16[32,3072]{1,0:T(8,128)(2,1)S(1)}, u32[]{:S(2)}, u32[]{:S(2)}) collective-permute-start(bf16[32,3072]{1,0:T(8,128)(2,1)S(1)} %convolution_convert_fusion), channel_id=1, source_target_pairs={{0,24},{4,28},{8,16},{12,20},{16,8},{20,12},{24,0},{28,4},{32,56},... | collective-permute-start | bytes 589832 | tf_op jit(solution)/shard_map/ppermute | solution.py:102
  6.2 11.5 %all_gather.6 = bf16[32,12288]{1,0:T(8,128)(2,1)S(1)} all-gather(bf16[32,3072]{1,0:T(8,128)(2,1)} %param.4), channel_id=1, replica_groups=mesh['sta'=32,'tm'=4] {'tm'}, dimensions={1}, use_global_device_ids=true | all-gather | bytes 983040 | tf_op jit(solution)/shard_map/all_gather | solution.py:127
  17.8 0.8 select_convert_fusion
  18.5 0.7 add_add_fusion.1
  19.3 3.8 %collective-permute-start.5 = (bf16[32,3072]{1,0:T(8,128)(2,1)}, bf16[32,3072]{1,0:T(8,128)(2,1)}, u32[]{:S(2)}, u32[]{:S(2)}) collective-permute-start(bf16[32,3072]{1,0:T(8,128)(2,1)} %add_add_fusion.1), channel_id=1, source_target_pairs={{0,96},{4,100},{8,104},{12,108},{16,112},{20,116},{24,120},{28,124... | collective-permute-start | bytes 589832 | tf_op jit(solution)/shard_map/ppermute | solution.py:102
  23.0 0.6 collective-permute-start.3
  24.5 0.6 reshape.39
  25.3 0.7 copy.11
  26.9 2.4 %copy.22 = bf16[32,96,159,1]{2,0,1,3:T(8,128)(2,1)S(1)} copy(bf16[32,96,159,1]{1,2,0,3:T(8,128)(2,1)S(1)} %maximum_bitcast_fusion) | data formatting | bytes 1953792 | tf_op jit(solution)/shard_map/concatenate | solution.py:40
  29.2 3.4 %collective-permute-done.5 = bf16[32,3072]{1,0:T(8,128)(2,1)} collective-permute-done((bf16[32,3072]{1,0:T(8,128)(2,1)}, bf16[32,3072]{1,0:T(8,128)(2,1)}, u32[]{:S(2)}, u32[]{:S(2)}) %collective-permute-start.5) | collective-permute-done | bytes 196640 | tf_op jit(solution)/shard_map/ppermute | solution.py:102
  33.0 1.3 %add_add_fusion = bf16[32,3072]{1,0:T(8,128)(2,1)S(1)} fusion(bf16[32,3072]{1,0:T(8,128)(2,1)} %collective-permute-done.5, bf16[32,3072]{1,0:T(8,128)(2,1)} %collective-permute-done.4, bf16[32,3072]{1,0:T(8,128)(2,1)} %add_add_fusion.1, bf16[32,3072]{1,0:T(8,128)(2,1)} %collective-permute-done.3), kind=kLoop, calls=%fused_computation.11 | loop fusion | flops 294912 | bytes 983040 | tf_op jit(solution)/shard_map/add | solution.py:103
  34.7 1.0 %convert_bitcast_fusion.1 = bf16[4,96,32,128]{3,2,1,0:T(8,128)(2,1)S(1)} fusion(bf16[32,96,159,1]{2,0,1,3:T(8,128)(2,1)S(1)} %copy.22, bf16[4,128,159]{2,1,0:T(8,128)(2,1)S(1)} %reshape.39), kind=kOutput, calls=%fused_computation.2 | convolution fusion | flops 501743616 | bytes 4285440 | tf_op jit(solution)/shard_map/cnu,btu->bnct/dot_general | solution.py:41
  35.7 2.3 %pad.11.fw_ref = bf16[4,105,32,128]{3,2,1,0:T(8,128)(2,1)} pad(bf16[4,96,32,128]{3,2,1,0:T(8,128)(2,1)S(1)} %convert_bitcast_fusion.1, bf16[]{:T(256)} %constant.4.clone.1), padding=0_0x2_7x0_0x0_0 | pad | bytes 6586370 | tf_op jit(solution)/shard_map/jit(_pad)/pad | solution.py:141
  38.0 1.8 %collective-permute-done.6 = bf16[32,3072]{1,0:T(8,128)(2,1)S(1)} collective-permute-done((bf16[32,3072]{1,0:T(8,128)(2,1)S(1)}, bf16[32,3072]{1,0:T(8,128)(2,1)S(1)}, u32[]{:S(2)}, u32[]{:S(2)}) %collective-permute-start.6) | collective-permute-done | bytes 196640 | tf_op jit(solution)/shard_map/ppermute | solution.py:102
  39.9 10.9 %all_gather.7 = bf16[32,12288]{1,0:T(8,128)(2,1)S(1)} all-gather(bf16[32,3072]{1,0:T(8,128)(2,1)S(1)} %add.37), channel_id=1, replica_groups=mesh['sta'=32,'tm'=4] {'tm'}, dimensions={1}, use_global_device_ids=true | all-gather | bytes 983040 | tf_op jit(solution)/shard_map/all_gather | solution.py:127
  51.2 0.7 copy.15
  52.8 2.4 %copy.25 = bf16[32,96,159,1]{2,0,1,3:T(8,128)(2,1)S(1)} copy(bf16[32,96,159,1]{1,2,0,3:T(8,128)(2,1)S(1)} %maximum_bitcast_fusion.1) | data formatting | bytes 1953792 | tf_op jit(solution)/shard_map/concatenate | solution.py:40
  55.1 1.0 %convert_bitcast_fusion = bf16[4,96,32,128]{3,2,1,0:T(8,128)(2,1)S(1)} fusion(bf16[32,96,159,1]{2,0,1,3:T(8,128)(2,1)S(1)} %copy.25, bf16[4,128,159]{2,1,0:T(8,128)(2,1)S(1)} %reshape.39), kind=kOutput, calls=%fused_computation.1 | convolution fusion | flops 501743616 | bytes 4285440 | tf_op jit(solution)/shard_map/cnu,btu->bnct/dot_general | solution.py:41
  56.7 26.7 %shard_map.46 = bf16[4,512,256]{2,1,0:T(8,128)(2,1)S(1)} custom-call(s32[1]{0:T(128)} %bitcast.off_ref, bf16[4,105,32,128]{3,2,1,0:T(8,128)(2,1)} %pad.11.fw_ref, bf16[4,101,32,128]{3,2,1,0:T(8,128)(2,1)S(1)} %pad.12.pp_ref), custom_call_target="tpu_custom_call" | custom-call | tf_op jit(solution)/shard_map/pallas_call | solution.py:85
  84.0 3.8 %reshape.44 = bf16[4,16,32,8,2,16]{2,1,5,4,3,0:T(8,128)(2,1)} reshape(bf16[4,512,256]{1,2,0:T(8,128)(2,1)S(1)} %copy.18) | data formatting | bytes 2097152 | tf_op jit(solution)/shard_map/reshape | solution.py:149
  87.8 5.4 %copy.19 = bf16[2,4,16,32,8,16]{3,5,4,2,1,0:T(8,128)(2,1)} copy(bf16[2,4,16,32,8,16]{3,5,2,0,4,1:T(8,128)(2,1)} %bitcast.36) | data formatting | bytes 2097152 | tf_op jit(solution)/shard_map/transpose | solution.py:150
  93.2 4.6 %copy.20 = bf16[2,4,16,32,128]{4,3,2,1,0:T(8,128)(2,1)} copy(bf16[2,4,16,32,128]{3,4,2,1,0:T(8,128)(2,1)} %bitcast.37) | data formatting | bytes 2097152 | tf_op jit(solution)/shard_map/reshape | solution.py:151
  (28 shorter events, 5.9 us)
Async XLA Ops:
  1.9 16.6 %collective-permute-start.2 = (bf16[32,3072]{1,0:T(8,128)(2,1)S(1)}, bf16[32,3072]{1,0:T(8,128)(2,1)S(1)}, u32[]{:S(2)}, u32[]{:S(2)}) collective-permute-start(bf16[32,3072]{1,0:T(8,128)(2,1)S(1)} %convolution_convert_fusion), channel_id=1, source_target_pairs={{0,24},{4,28},{8,16},{12,20},{16,8},{20,12},{24,0},{28,4},{32,56},... | collective-permute-start | bytes 589832 | tf_op jit(solution)/shard_map/ppermute | solution.py:102
  5.6 13.0 %collective-permute-start.1 = (bf16[32,3072]{1,0:T(8,128)(2,1)S(1)}, bf16[32,3072]{1,0:T(8,128)(2,1)S(1)}, u32[]{:S(2)}, u32[]{:S(2)}) collective-permute-start(bf16[32,3072]{1,0:T(8,128)(2,1)S(1)} %convolution_convert_fusion), channel_id=1, source_target_pairs={{0,16},{4,20},{8,24},{12,28},{16,0},{20,4},{24,8},{28,12},{32,48},... | collective-permute-start | bytes 589832 | tf_op jit(solution)/shard_map/ppermute | solution.py:102
  5.9 12.6 %collective-permute-start = (bf16[32,3072]{1,0:T(8,128)(2,1)S(1)}, bf16[32,3072]{1,0:T(8,128)(2,1)S(1)}, u32[]{:S(2)}, u32[]{:S(2)}) collective-permute-start(bf16[32,3072]{1,0:T(8,128)(2,1)S(1)} %convolution_convert_fusion), channel_id=1, source_target_pairs={{0,8},{4,12},{8,0},{12,4},{16,24},{20,28},{24,16},{28,20},{32,40},... | collective-permute-start | bytes 589832 | tf_op jit(solution)/shard_map/ppermute | solution.py:102
  19.3 13.4 %collective-permute-start.5 = (bf16[32,3072]{1,0:T(8,128)(2,1)}, bf16[32,3072]{1,0:T(8,128)(2,1)}, u32[]{:S(2)}, u32[]{:S(2)}) collective-permute-start(bf16[32,3072]{1,0:T(8,128)(2,1)} %add_add_fusion.1), channel_id=1, source_target_pairs={{0,96},{4,100},{8,104},{12,108},{16,112},{20,116},{24,120},{28,124... | collective-permute-start | bytes 589832 | tf_op jit(solution)/shard_map/ppermute | solution.py:102
  23.0 9.6 %collective-permute-start.4 = (bf16[32,3072]{1,0:T(8,128)(2,1)}, bf16[32,3072]{1,0:T(8,128)(2,1)}, u32[]{:S(2)}, u32[]{:S(2)}) collective-permute-start(bf16[32,3072]{1,0:T(8,128)(2,1)} %add_add_fusion.1), channel_id=1, source_target_pairs={{0,64},{4,68},{8,72},{12,76},{16,80},{20,84},{24,88},{28,92},{32,9... | collective-permute-start | bytes 589832 | tf_op jit(solution)/shard_map/ppermute | solution.py:102
  23.0 10.0 %collective-permute-start.3 = (bf16[32,3072]{1,0:T(8,128)(2,1)}, bf16[32,3072]{1,0:T(8,128)(2,1)}, u32[]{:S(2)}, u32[]{:S(2)}) collective-permute-start(bf16[32,3072]{1,0:T(8,128)(2,1)} %add_add_fusion.1), channel_id=1, source_target_pairs={{0,32},{4,36},{8,40},{12,44},{16,48},{20,52},{24,56},{28,60},{32,0... | collective-permute-start | bytes 589832 | tf_op jit(solution)/shard_map/ppermute | solution.py:102
  34.3 5.5 %collective-permute-start.6 = (bf16[32,3072]{1,0:T(8,128)(2,1)S(1)}, bf16[32,3072]{1,0:T(8,128)(2,1)S(1)}, u32[]{:S(2)}, u32[]{:S(2)}) collective-permute-start(bf16[32,3072]{1,0:T(8,128)(2,1)S(1)} %add_add_fusion), channel_id=1, source_target_pairs={{0,4},{4,0},{8,12},{12,8},{16,20},{20,16},{24,28},{28,24},{32,36},... | collective-permute-start | bytes 589832 | tf_op jit(solution)/shard_map/ppermute | solution.py:102

commit v8 on v7

--- a/solution.py
+++ b/solution.py
@@ -61,7 +61,7 @@
         )
         return carry
 
-    lax.fori_loop(0, chunks, step, 0)
+    lax.fori_loop(0, chunks, step, 0, unroll=True)
     out_ref[0] = (acc_ref[...] * scale).astype(out_ref.dtype)
 
 

time: 98.1 us -> 93.3 us (0.951)
  Pallas kernels: 26.7 us -> 21.9 us
    pallas_call x1, Pallas kernels: 26.7 us -> 21.9 us  [correlate(): pl.pallas_call(kernel, grid_spec=grid_spec, out_shape=jax.ShapeDtypeStruc...]
where the time goes in v8:
time: 93.3 us; the launch traced here: 93 us
  local copies, waits for them, and re-layouts  26.3 us (28%)
  blocking collectives  22.4 us (24%)
  Pallas kernels  21.9 us (23%)
  starting transfers between devices  9.03 us (10%)
  waiting for transfers between devices  5.63 us (6%)
  other arithmetic  4.29 us (5%)
  matrix products  3.2 us (3%)
    all_gather x2, blocking collectives, filtered_of(): rows = lax.all_gather(rows, 'tm', axis=1, tiled=True)  22.4 us
    pallas_call x1, Pallas kernels, correlate(): pl.pallas_call(kernel, grid_spec=grid_spec, out_shape=jax.ShapeDtypeStruc...  21.9 us
    ppermute x7, starting transfers between devices, summed_over(): lax.ppermute(value, axis, [(i, i ^ m) for i in range(count)])  9.03 us
    ppermute x7, waiting for transfers between devices, summed_over(): lax.ppermute(value, axis, [(i, i ^ m) for i in range(count)])  5.63 us
    transpose x1, local copies, waits for them, and re-layouts, per_device(): out = jnp.transpose(out, (4, 0, 5, 2, 3, 1))  5.38 us
    concatenate x2, local copies, waits for them, and re-layouts, filter_blocks(): pieces = jnp.concatenate([prefix, main], axis=2)  4.7 us
    reshape x1, local copies, waits for them, and re-layouts, per_device(): return out.reshape(ROUNDS, bands, count_src, channels, share)  4.56 us
    reshape x1, local copies, waits for them, and re-layouts, per_device(): out = out.reshape(bands, SHIFTS, channels, groups, ROUNDS, count_src)  3.82 us
  transfers between devices with their start and end apart: 7, of which 3 were waited for; matrix products, arithmetic and copies ran while one was open for 10% of the time, Pallas kernels for 0%

profile of v8, /device:TPU:1, one launch (start us, length us, event | category | flops | bytes accessed | tf_op | source)
XLA Modules:
  0.0 93.0 jit_solution(3589120434032322301)
XLA Ops:
  0.0 0.7 broadcast_subtract_fusion
  0.8 1.2 %convolution_convert_fusion = bf16[32,3072]{1,0:T(8,128)(2,1)S(1)} fusion(bf16[32,3072]{1,0:T(8,128)(2,1)} %param.4, s32[32]{0:T(128)S(1)} %sub.15), kind=kOutput, calls=%fused_computation | convolution fusion | flops 6390784 | bytes 393344 | tf_op jit(solution)/shard_map/dot_general | solution.py:123
  1.9 3.6 %collective-permute-start.2 = (bf16[32,3072]{1,0:T(8,128)(2,1)S(1)}, bf16[32,3072]{1,0:T(8,128)(2,1)S(1)}, u32[]{:S(2)}, u32[]{:S(2)}) collective-permute-start(bf16[32,3072]{1,0:T(8,128)(2,1)S(1)} %convolution_convert_fusion), channel_id=1, source_target_pairs={{0,24},{4,28},{8,16},{12,20},{16,8},{20,12},{24,0},{28,4},{32,56},... | collective-permute-start | bytes 589832 | tf_op jit(solution)/shard_map/ppermute | solution.py:102
  6.2 11.5 %all_gather.6 = bf16[32,12288]{1,0:T(8,128)(2,1)S(1)} all-gather(bf16[32,3072]{1,0:T(8,128)(2,1)} %param.4), channel_id=1, replica_groups=mesh['sta'=32,'tm'=4] {'tm'}, dimensions={1}, use_global_device_ids=true | all-gather | bytes 983040 | tf_op jit(solution)/shard_map/all_gather | solution.py:127
  17.8 0.8 select_convert_fusion
  18.5 0.7 add_add_fusion.1
  19.3 3.8 %collective-permute-start.5 = (bf16[32,3072]{1,0:T(8,128)(2,1)}, bf16[32,3072]{1,0:T(8,128)(2,1)}, u32[]{:S(2)}, u32[]{:S(2)}) collective-permute-start(bf16[32,3072]{1,0:T(8,128)(2,1)} %add_add_fusion.1), channel_id=1, source_target_pairs={{0,96},{4,100},{8,104},{12,108},{16,112},{20,116},{24,120},{28,124... | collective-permute-start | bytes 589832 | tf_op jit(solution)/shard_map/ppermute | solution.py:102
  23.0 0.6 collective-permute-start.3
  24.5 0.6 reshape.39
  25.3 0.7 copy.11
  26.9 2.4 %copy.22 = bf16[32,96,159,1]{2,0,1,3:T(8,128)(2,1)S(1)} copy(bf16[32,96,159,1]{1,2,0,3:T(8,128)(2,1)S(1)} %maximum_bitcast_fusion) | data formatting | bytes 1953792 | tf_op jit(solution)/shard_map/concatenate | solution.py:40
  29.2 3.4 %collective-permute-done.5 = bf16[32,3072]{1,0:T(8,128)(2,1)} collective-permute-done((bf16[32,3072]{1,0:T(8,128)(2,1)}, bf16[32,3072]{1,0:T(8,128)(2,1)}, u32[]{:S(2)}, u32[]{:S(2)}) %collective-permute-start.5) | collective-permute-done | bytes 196640 | tf_op jit(solution)/shard_map/ppermute | solution.py:102
  33.0 1.3 %add_add_fusion = bf16[32,3072]{1,0:T(8,128)(2,1)S(1)} fusion(bf16[32,3072]{1,0:T(8,128)(2,1)} %collective-permute-done.5, bf16[32,3072]{1,0:T(8,128)(2,1)} %collective-permute-done.4, bf16[32,3072]{1,0:T(8,128)(2,1)} %add_add_fusion.1, bf16[32,3072]{1,0:T(8,128)(2,1)} %collective-permute-done.3), kind=kLoop, calls=%fused_computation.11 | loop fusion | flops 294912 | bytes 983040 | tf_op jit(solution)/shard_map/add | solution.py:103
  34.7 1.0 %convert_bitcast_fusion.1 = bf16[4,96,32,128]{3,2,1,0:T(8,128)(2,1)S(1)} fusion(bf16[32,96,159,1]{2,0,1,3:T(8,128)(2,1)S(1)} %copy.22, bf16[4,128,159]{2,1,0:T(8,128)(2,1)S(1)} %reshape.39), kind=kOutput, calls=%fused_computation.2 | convolution fusion | flops 501743616 | bytes 4285440 | tf_op jit(solution)/shard_map/cnu,btu->bnct/dot_general | solution.py:41
  35.7 2.3 %pad.11.fw_ref = bf16[4,105,32,128]{3,2,1,0:T(8,128)(2,1)} pad(bf16[4,96,32,128]{3,2,1,0:T(8,128)(2,1)S(1)} %convert_bitcast_fusion.1, bf16[]{:T(256)} %constant.4.clone.1), padding=0_0x2_7x0_0x0_0 | pad | bytes 6586370 | tf_op jit(solution)/shard_map/jit(_pad)/pad | solution.py:141
  38.0 1.8 %collective-permute-done.6 = bf16[32,3072]{1,0:T(8,128)(2,1)S(1)} collective-permute-done((bf16[32,3072]{1,0:T(8,128)(2,1)S(1)}, bf16[32,3072]{1,0:T(8,128)(2,1)S(1)}, u32[]{:S(2)}, u32[]{:S(2)}) %collective-permute-start.6) | collective-permute-done | bytes 196640 | tf_op jit(solution)/shard_map/ppermute | solution.py:102
  39.9 10.9 %all_gather.7 = bf16[32,12288]{1,0:T(8,128)(2,1)S(1)} all-gather(bf16[32,3072]{1,0:T(8,128)(2,1)S(1)} %add.37), channel_id=1, replica_groups=mesh['sta'=32,'tm'=4] {'tm'}, dimensions={1}, use_global_device_ids=true | all-gather | bytes 983040 | tf_op jit(solution)/shard_map/all_gather | solution.py:127
  51.2 0.7 copy.15
  52.8 2.4 %copy.25 = bf16[32,96,159,1]{2,0,1,3:T(8,128)(2,1)S(1)} copy(bf16[32,96,159,1]{1,2,0,3:T(8,128)(2,1)S(1)} %maximum_bitcast_fusion.1) | data formatting | bytes 1953792 | tf_op jit(solution)/shard_map/concatenate | solution.py:40
  55.1 1.0 %convert_bitcast_fusion = bf16[4,96,32,128]{3,2,1,0:T(8,128)(2,1)S(1)} fusion(bf16[32,96,159,1]{2,0,1,3:T(8,128)(2,1)S(1)} %copy.25, bf16[4,128,159]{2,1,0:T(8,128)(2,1)S(1)} %reshape.39), kind=kOutput, calls=%fused_computation.1 | convolution fusion | flops 501743616 | bytes 4285440 | tf_op jit(solution)/shard_map/cnu,btu->bnct/dot_general | solution.py:41
  56.7 21.9 %shard_map.46 = bf16[4,512,256]{2,1,0:T(8,128)(2,1)S(1)} custom-call(s32[1]{0:T(128)} %bitcast.off_ref, bf16[4,105,32,128]{3,2,1,0:T(8,128)(2,1)} %pad.11.fw_ref, bf16[4,101,32,128]{3,2,1,0:T(8,128)(2,1)S(1)} %pad.12.pp_ref), custom_call_target="tpu_custom_call" | custom-call | tf_op jit(solution)/shard_map/pallas_call | solution.py:85
  79.2 3.8 %reshape.44 = bf16[4,16,32,8,2,16]{2,1,5,4,3,0:T(8,128)(2,1)} reshape(bf16[4,512,256]{1,2,0:T(8,128)(2,1)S(1)} %copy.18) | data formatting | bytes 2097152 | tf_op jit(solution)/shard_map/reshape | solution.py:149
  83.0 5.4 %copy.19 = bf16[2,4,16,32,8,16]{3,5,4,2,1,0:T(8,128)(2,1)} copy(bf16[2,4,16,32,8,16]{3,5,2,0,4,1:T(8,128)(2,1)} %bitcast.36) | data formatting | bytes 2097152 | tf_op jit(solution)/shard_map/transpose | solution.py:150
  88.4 4.6 %copy.20 = bf16[2,4,16,32,128]{4,3,2,1,0:T(8,128)(2,1)} copy(bf16[2,4,16,32,128]{3,4,2,1,0:T(8,128)(2,1)} %bitcast.37) | data formatting | bytes 2097152 | tf_op jit(solution)/shard_map/reshape | solution.py:151
  (28 shorter events, 5.9 us)
Async XLA Ops:
  1.9 16.6 %collective-permute-start.2 = (bf16[32,3072]{1,0:T(8,128)(2,1)S(1)}, bf16[32,3072]{1,0:T(8,128)(2,1)S(1)}, u32[]{:S(2)}, u32[]{:S(2)}) collective-permute-start(bf16[32,3072]{1,0:T(8,128)(2,1)S(1)} %convolution_convert_fusion), channel_id=1, source_target_pairs={{0,24},{4,28},{8,16},{12,20},{16,8},{20,12},{24,0},{28,4},{32,56},... | collective-permute-start | bytes 589832 | tf_op jit(solution)/shard_map/ppermute | solution.py:102
  5.6 13.0 %collective-permute-start.1 = (bf16[32,3072]{1,0:T(8,128)(2,1)S(1)}, bf16[32,3072]{1,0:T(8,128)(2,1)S(1)}, u32[]{:S(2)}, u32[]{:S(2)}) collective-permute-start(bf16[32,3072]{1,0:T(8,128)(2,1)S(1)} %convolution_convert_fusion), channel_id=1, source_target_pairs={{0,16},{4,20},{8,24},{12,28},{16,0},{20,4},{24,8},{28,12},{32,48},... | collective-permute-start | bytes 589832 | tf_op jit(solution)/shard_map/ppermute | solution.py:102
  5.9 12.6 %collective-permute-start = (bf16[32,3072]{1,0:T(8,128)(2,1)S(1)}, bf16[32,3072]{1,0:T(8,128)(2,1)S(1)}, u32[]{:S(2)}, u32[]{:S(2)}) collective-permute-start(bf16[32,3072]{1,0:T(8,128)(2,1)S(1)} %convolution_convert_fusion), channel_id=1, source_target_pairs={{0,8},{4,12},{8,0},{12,4},{16,24},{20,28},{24,16},{28,20},{32,40},... | collective-permute-start | bytes 589832 | tf_op jit(solution)/shard_map/ppermute | solution.py:102
  19.3 13.4 %collective-permute-start.5 = (bf16[32,3072]{1,0:T(8,128)(2,1)}, bf16[32,3072]{1,0:T(8,128)(2,1)}, u32[]{:S(2)}, u32[]{:S(2)}) collective-permute-start(bf16[32,3072]{1,0:T(8,128)(2,1)} %add_add_fusion.1), channel_id=1, source_target_pairs={{0,96},{4,100},{8,104},{12,108},{16,112},{20,116},{24,120},{28,124... | collective-permute-start | bytes 589832 | tf_op jit(solution)/shard_map/ppermute | solution.py:102
  23.0 9.6 %collective-permute-start.4 = (bf16[32,3072]{1,0:T(8,128)(2,1)}, bf16[32,3072]{1,0:T(8,128)(2,1)}, u32[]{:S(2)}, u32[]{:S(2)}) collective-permute-start(bf16[32,3072]{1,0:T(8,128)(2,1)} %add_add_fusion.1), channel_id=1, source_target_pairs={{0,64},{4,68},{8,72},{12,76},{16,80},{20,84},{24,88},{28,92},{32,9... | collective-permute-start | bytes 589832 | tf_op jit(solution)/shard_map/ppermute | solution.py:102
  23.0 10.0 %collective-permute-start.3 = (bf16[32,3072]{1,0:T(8,128)(2,1)}, bf16[32,3072]{1,0:T(8,128)(2,1)}, u32[]{:S(2)}, u32[]{:S(2)}) collective-permute-start(bf16[32,3072]{1,0:T(8,128)(2,1)} %add_add_fusion.1), channel_id=1, source_target_pairs={{0,32},{4,36},{8,40},{12,44},{16,48},{20,52},{24,56},{28,60},{32,0... | collective-permute-start | bytes 589832 | tf_op jit(solution)/shard_map/ppermute | solution.py:102
  34.3 5.5 %collective-permute-start.6 = (bf16[32,3072]{1,0:T(8,128)(2,1)S(1)}, bf16[32,3072]{1,0:T(8,128)(2,1)S(1)}, u32[]{:S(2)}, u32[]{:S(2)}) collective-permute-start(bf16[32,3072]{1,0:T(8,128)(2,1)S(1)} %add_add_fusion), channel_id=1, source_target_pairs={{0,4},{4,0},{8,12},{12,8},{16,20},{20,16},{24,28},{28,24},{32,36},... | collective-permute-start | bytes 589832 | tf_op jit(solution)/shard_map/ppermute | solution.py:102

commit v9 on v8

--- a/solution.py
+++ b/solution.py
@@ -62,7 +62,13 @@
         return carry
 
     lax.fori_loop(0, chunks, step, 0, unroll=True)
-    out_ref[0] = (acc_ref[...] * scale).astype(out_ref.dtype)
+    rounded = (acc_ref[...] * scale).astype(jnp.bfloat16)
+    n = rounded.shape[1]
+    rows_p = n // groups
+    src = lax.broadcasted_iota(jnp.int32, (n, n), 0)
+    dst = lax.broadcasted_iota(jnp.int32, (n, n), 1)
+    perm = ((src % rows_p) * groups + src // rows_p == dst).astype(jnp.bfloat16)
+    out_ref[0] = jnp.dot(rounded, perm, preferred_element_type=jnp.float32).astype(out_ref.dtype)
 
 
 def correlate(offset, f_blocks, p_blocks, lags, chunks, scale):
@@ -146,8 +152,8 @@
 
     out = correlate(offset, f_blocks, p_blocks, share, chunks, norm_scale)
     bands = out.shape[0]
-    out = out.reshape(bands, SHIFTS, channels, groups, ROUNDS, count_src)
-    out = jnp.transpose(out, (4, 0, 5, 2, 3, 1))
+    out = out.reshape(bands, SHIFTS, channels, ROUNDS, count_src, groups)
+    out = jnp.transpose(out, (3, 0, 4, 2, 5, 1))
     return out.reshape(ROUNDS, bands, count_src, channels, share)
 
 

time: 93.3 us -> 88.2 us (0.945)
  local copies, waits for them, and re-layouts: 26.3 us -> 20.9 us
    transpose x1 -> x0, local copies, waits for them, and re-layouts: 5.38 us -> none  [per_device(): out = jnp.transpose(out, (4, 0, 5, 2, 3, 1))]
  transfers between devices with their start and end apart: 7 -> 7, of which waited for: 3 -> 3; matrix products, arithmetic and copies ran while one was open for 10% -> 11% of each run, Pallas kernels for 0% -> 0%
where the time goes in v9:
time: 88.2 us; the launch traced here: 87.9 us
  blocking collectives  22.4 us (25%)
  Pallas kernels  22.2 us (25%)
  local copies, waits for them, and re-layouts  20.9 us (24%)
  starting transfers between devices  9.03 us (10%)
  waiting for transfers between devices  5.63 us (6%)
  other arithmetic  4.29 us (5%)
  matrix products  3.2 us (4%)
    all_gather x2, blocking collectives, filtered_of(): rows = lax.all_gather(rows, 'tm', axis=1, tiled=True)  22.4 us
    pallas_call x1, Pallas kernels, correlate(): pl.pallas_call(kernel, grid_spec=grid_spec, out_shape=jax.ShapeDtypeStruc...  22.2 us
    ppermute x7, starting transfers between devices, summed_over(): lax.ppermute(value, axis, [(i, i ^ m) for i in range(count)])  9.03 us
    ppermute x7, waiting for transfers between devices, summed_over(): lax.ppermute(value, axis, [(i, i ^ m) for i in range(count)])  5.63 us
    concatenate x2, local copies, waits for them, and re-layouts, filter_blocks(): pieces = jnp.concatenate([prefix, main], axis=2)  4.7 us
    reshape x1, local copies, waits for them, and re-layouts, per_device(): return out.reshape(ROUNDS, bands, count_src, channels, share)  4.56 us
    reshape x1, local copies, waits for them, and re-layouts, per_device(): out = out.reshape(bands, SHIFTS, channels, ROUNDS, count_src, groups)  3.82 us
    pad x1, local copies, waits for them, and re-layouts, per_device(): jnp.pad(f_loc, ((0, 0), (f_front, blocks + lag_count // 128 - data_blocks...  2.3 us
  transfers between devices with their start and end apart: 7, of which 3 were waited for; matrix products, arithmetic and copies ran while one was open for 11% of the time, Pallas kernels for 0%

profile of v9, /device:TPU:1, one launch (start us, length us, event | category | flops | bytes accessed | tf_op | source)
XLA Modules:
  0.0 87.9 jit_solution(16059767271378898650)
XLA Ops:
  0.0 0.7 broadcast_subtract_fusion
  0.8 1.2 %convolution_convert_fusion = bf16[32,3072]{1,0:T(8,128)(2,1)S(1)} fusion(bf16[32,3072]{1,0:T(8,128)(2,1)} %param.4, s32[32]{0:T(128)S(1)} %sub.15), kind=kOutput, calls=%fused_computation | convolution fusion | flops 6390784 | bytes 393344 | tf_op jit(solution)/shard_map/dot_general | solution.py:129
  1.9 3.6 %collective-permute-start.2 = (bf16[32,3072]{1,0:T(8,128)(2,1)S(1)}, bf16[32,3072]{1,0:T(8,128)(2,1)S(1)}, u32[]{:S(2)}, u32[]{:S(2)}) collective-permute-start(bf16[32,3072]{1,0:T(8,128)(2,1)S(1)} %convolution_convert_fusion), channel_id=1, source_target_pairs={{0,24},{4,28},{8,16},{12,20},{16,8},{20,12},{24,0},{28,4},{32,56},... | collective-permute-start | bytes 589832 | tf_op jit(solution)/shard_map/ppermute | solution.py:108
  6.2 11.5 %all_gather.6 = bf16[32,12288]{1,0:T(8,128)(2,1)S(1)} all-gather(bf16[32,3072]{1,0:T(8,128)(2,1)} %param.4), channel_id=1, replica_groups=mesh['sta'=32,'tm'=4] {'tm'}, dimensions={1}, use_global_device_ids=true | all-gather | bytes 983040 | tf_op jit(solution)/shard_map/all_gather | solution.py:133
  17.8 0.8 select_convert_fusion
  18.5 0.7 add_add_fusion.1
  19.3 3.8 %collective-permute-start.5 = (bf16[32,3072]{1,0:T(8,128)(2,1)}, bf16[32,3072]{1,0:T(8,128)(2,1)}, u32[]{:S(2)}, u32[]{:S(2)}) collective-permute-start(bf16[32,3072]{1,0:T(8,128)(2,1)} %add_add_fusion.1), channel_id=1, source_target_pairs={{0,96},{4,100},{8,104},{12,108},{16,112},{20,116},{24,120},{28,124... | collective-permute-start | bytes 589832 | tf_op jit(solution)/shard_map/ppermute | solution.py:108
  23.0 0.6 collective-permute-start.3
  24.5 0.6 reshape.39
  25.3 0.7 copy.11
  26.9 2.4 %copy.22 = bf16[32,96,159,1]{2,0,1,3:T(8,128)(2,1)S(1)} copy(bf16[32,96,159,1]{1,2,0,3:T(8,128)(2,1)S(1)} %maximum_bitcast_fusion) | data formatting | bytes 1953792 | tf_op jit(solution)/shard_map/concatenate | solution.py:40
  29.2 3.4 %collective-permute-done.5 = bf16[32,3072]{1,0:T(8,128)(2,1)} collective-permute-done((bf16[32,3072]{1,0:T(8,128)(2,1)}, bf16[32,3072]{1,0:T(8,128)(2,1)}, u32[]{:S(2)}, u32[]{:S(2)}) %collective-permute-start.5) | collective-permute-done | bytes 196640 | tf_op jit(solution)/shard_map/ppermute | solution.py:108
  33.0 1.3 %add_add_fusion = bf16[32,3072]{1,0:T(8,128)(2,1)S(1)} fusion(bf16[32,3072]{1,0:T(8,128)(2,1)} %collective-permute-done.5, bf16[32,3072]{1,0:T(8,128)(2,1)} %collective-permute-done.4, bf16[32,3072]{1,0:T(8,128)(2,1)} %add_add_fusion.1, bf16[32,3072]{1,0:T(8,128)(2,1)} %collective-permute-done.3), kind=kLoop, calls=%fused_computation.11 | loop fusion | flops 294912 | bytes 983040 | tf_op jit(solution)/shard_map/add | solution.py:109
  34.7 1.0 %convert_bitcast_fusion.1 = bf16[4,96,32,128]{3,2,1,0:T(8,128)(2,1)S(1)} fusion(bf16[32,96,159,1]{2,0,1,3:T(8,128)(2,1)S(1)} %copy.22, bf16[4,128,159]{2,1,0:T(8,128)(2,1)S(1)} %reshape.39), kind=kOutput, calls=%fused_computation.2 | convolution fusion | flops 501743616 | bytes 4285440 | tf_op jit(solution)/shard_map/cnu,btu->bnct/dot_general | solution.py:41
  35.7 2.3 %pad.11.fw_ref = bf16[4,105,32,128]{3,2,1,0:T(8,128)(2,1)} pad(bf16[4,96,32,128]{3,2,1,0:T(8,128)(2,1)S(1)} %convert_bitcast_fusion.1, bf16[]{:T(256)} %constant.4.clone.1), padding=0_0x2_7x0_0x0_0 | pad | bytes 6586370 | tf_op jit(solution)/shard_map/jit(_pad)/pad | solution.py:147
  38.0 1.8 %collective-permute-done.6 = bf16[32,3072]{1,0:T(8,128)(2,1)S(1)} collective-permute-done((bf16[32,3072]{1,0:T(8,128)(2,1)S(1)}, bf16[32,3072]{1,0:T(8,128)(2,1)S(1)}, u32[]{:S(2)}, u32[]{:S(2)}) %collective-permute-start.6) | collective-permute-done | bytes 196640 | tf_op jit(solution)/shard_map/ppermute | solution.py:108
  39.9 10.9 %all_gather.7 = bf16[32,12288]{1,0:T(8,128)(2,1)S(1)} all-gather(bf16[32,3072]{1,0:T(8,128)(2,1)S(1)} %add.37), channel_id=1, replica_groups=mesh['sta'=32,'tm'=4] {'tm'}, dimensions={1}, use_global_device_ids=true | all-gather | bytes 983040 | tf_op jit(solution)/shard_map/all_gather | solution.py:133
  51.2 0.7 copy.15
  52.8 2.4 %copy.25 = bf16[32,96,159,1]{2,0,1,3:T(8,128)(2,1)S(1)} copy(bf16[32,96,159,1]{1,2,0,3:T(8,128)(2,1)S(1)} %maximum_bitcast_fusion.1) | data formatting | bytes 1953792 | tf_op jit(solution)/shard_map/concatenate | solution.py:40
  55.1 1.0 %convert_bitcast_fusion = bf16[4,96,32,128]{3,2,1,0:T(8,128)(2,1)S(1)} fusion(bf16[32,96,159,1]{2,0,1,3:T(8,128)(2,1)S(1)} %copy.25, bf16[4,128,159]{2,1,0:T(8,128)(2,1)S(1)} %reshape.39), kind=kOutput, calls=%fused_computation.1 | convolution fusion | flops 501743616 | bytes 4285440 | tf_op jit(solution)/shard_map/cnu,btu->bnct/dot_general | solution.py:41
  56.2 0.6 pad.12.pp_ref
  56.7 22.2 %shard_map.46 = bf16[4,512,256]{2,1,0:T(8,128)(2,1)S(1)} custom-call(s32[1]{0:T(128)} %bitcast.off_ref, bf16[4,105,32,128]{3,2,1,0:T(8,128)(2,1)} %pad.11.fw_ref, bf16[4,101,32,128]{3,2,1,0:T(8,128)(2,1)S(1)} %pad.12.pp_ref), custom_call_target="tpu_custom_call" | custom-call | tf_op jit(solution)/shard_map/pallas_call | solution.py:91
  79.5 3.8 %reshape.44 = bf16[4,16,32,2,16,8]{2,1,5,4,3,0:T(8,128)(2,1)} reshape(bf16[4,512,256]{1,2,0:T(8,128)(2,1)S(1)} %copy.18) | data formatting | bytes 2097152 | tf_op jit(solution)/shard_map/reshape | solution.py:155
  83.3 4.6 %copy.20 = bf16[2,4,16,32,128]{4,3,2,1,0:T(8,128)(2,1)} copy(bf16[2,4,16,32,128]{3,4,2,0,1:T(8,128)(2,1)} %bitcast.37) | data formatting | bytes 2097152 | tf_op jit(solution)/shard_map/reshape | solution.py:157
  (27 shorter events, 5.3 us)
Async XLA Ops:
  1.9 16.6 %collective-permute-start.2 = (bf16[32,3072]{1,0:T(8,128)(2,1)S(1)}, bf16[32,3072]{1,0:T(8,128)(2,1)S(1)}, u32[]{:S(2)}, u32[]{:S(2)}) collective-permute-start(bf16[32,3072]{1,0:T(8,128)(2,1)S(1)} %convolution_convert_fusion), channel_id=1, source_target_pairs={{0,24},{4,28},{8,16},{12,20},{16,8},{20,12},{24,0},{28,4},{32,56},... | collective-permute-start | bytes 589832 | tf_op jit(solution)/shard_map/ppermute | solution.py:108
  5.6 13.0 %collective-permute-start.1 = (bf16[32,3072]{1,0:T(8,128)(2,1)S(1)}, bf16[32,3072]{1,0:T(8,128)(2,1)S(1)}, u32[]{:S(2)}, u32[]{:S(2)}) collective-permute-start(bf16[32,3072]{1,0:T(8,128)(2,1)S(1)} %convolution_convert_fusion), channel_id=1, source_target_pairs={{0,16},{4,20},{8,24},{12,28},{16,0},{20,4},{24,8},{28,12},{32,48},... | collective-permute-start | bytes 589832 | tf_op jit(solution)/shard_map/ppermute | solution.py:108
  5.9 12.6 %collective-permute-start = (bf16[32,3072]{1,0:T(8,128)(2,1)S(1)}, bf16[32,3072]{1,0:T(8,128)(2,1)S(1)}, u32[]{:S(2)}, u32[]{:S(2)}) collective-permute-start(bf16[32,3072]{1,0:T(8,128)(2,1)S(1)} %convolution_convert_fusion), channel_id=1, source_target_pairs={{0,8},{4,12},{8,0},{12,4},{16,24},{20,28},{24,16},{28,20},{32,40},... | collective-permute-start | bytes 589832 | tf_op jit(solution)/shard_map/ppermute | solution.py:108
  19.3 13.4 %collective-permute-start.5 = (bf16[32,3072]{1,0:T(8,128)(2,1)}, bf16[32,3072]{1,0:T(8,128)(2,1)}, u32[]{:S(2)}, u32[]{:S(2)}) collective-permute-start(bf16[32,3072]{1,0:T(8,128)(2,1)} %add_add_fusion.1), channel_id=1, source_target_pairs={{0,96},{4,100},{8,104},{12,108},{16,112},{20,116},{24,120},{28,124... | collective-permute-start | bytes 589832 | tf_op jit(solution)/shard_map/ppermute | solution.py:108
  23.0 9.6 %collective-permute-start.4 = (bf16[32,3072]{1,0:T(8,128)(2,1)}, bf16[32,3072]{1,0:T(8,128)(2,1)}, u32[]{:S(2)}, u32[]{:S(2)}) collective-permute-start(bf16[32,3072]{1,0:T(8,128)(2,1)} %add_add_fusion.1), channel_id=1, source_target_pairs={{0,64},{4,68},{8,72},{12,76},{16,80},{20,84},{24,88},{28,92},{32,9... | collective-permute-start | bytes 589832 | tf_op jit(solution)/shard_map/ppermute | solution.py:108
  23.0 10.0 %collective-permute-start.3 = (bf16[32,3072]{1,0:T(8,128)(2,1)}, bf16[32,3072]{1,0:T(8,128)(2,1)}, u32[]{:S(2)}, u32[]{:S(2)}) collective-permute-start(bf16[32,3072]{1,0:T(8,128)(2,1)} %add_add_fusion.1), channel_id=1, source_target_pairs={{0,32},{4,36},{8,40},{12,44},{16,48},{20,52},{24,56},{28,60},{32,0... | collective-permute-start | bytes 589832 | tf_op jit(solution)/shard_map/ppermute | solution.py:108
  34.3 5.5 %collective-permute-start.6 = (bf16[32,3072]{1,0:T(8,128)(2,1)S(1)}, bf16[32,3072]{1,0:T(8,128)(2,1)S(1)}, u32[]{:S(2)}, u32[]{:S(2)}) collective-permute-start(bf16[32,3072]{1,0:T(8,128)(2,1)S(1)} %add_add_fusion), channel_id=1, source_target_pairs={{0,4},{4,0},{8,12},{12,8},{16,20},{20,16},{24,28},{28,24},{32,36},... | collective-permute-start | bytes 589832 | tf_op jit(solution)/shard_map/ppermute | solution.py:108

commit v10 on v9

--- a/solution.py
+++ b/solution.py
@@ -10,7 +10,7 @@
 ROUNDS = 2
 MAXLAG = 256
 SHIFTS = 16
-CHUNK = 2560
+CHUNK = 3200
 
 
 def skew(values, count_rows):

time: 88.2 us -> 88.2 us (level)
  no operation moved by 1% of the time
where the time goes in v10:
time: 88.2 us; the launch traced here: 87.8 us
  blocking collectives  22.4 us (25%)
  Pallas kernels  22.2 us (25%)
  local copies, waits for them, and re-layouts  20.9 us (24%)
  starting transfers between devices  9.03 us (10%)
  waiting for transfers between devices  5.63 us (6%)
  other arithmetic  4.29 us (5%)
  matrix products  3.2 us (4%)
    all_gather x2, blocking collectives, filtered_of(): rows = lax.all_gather(rows, 'tm', axis=1, tiled=True)  22.4 us
    pallas_call x1, Pallas kernels, correlate(): pl.pallas_call(kernel, grid_spec=grid_spec, out_shape=jax.ShapeDtypeStruc...  22.2 us
    ppermute x7, starting transfers between devices, summed_over(): lax.ppermute(value, axis, [(i, i ^ m) for i in range(count)])  9.03 us
    ppermute x7, waiting for transfers between devices, summed_over(): lax.ppermute(value, axis, [(i, i ^ m) for i in range(count)])  5.63 us
    concatenate x2, local copies, waits for them, and re-layouts, filter_blocks(): pieces = jnp.concatenate([prefix, main], axis=2)  4.7 us
    reshape x1, local copies, waits for them, and re-layouts, per_device(): return out.reshape(ROUNDS, bands, count_src, channels, share)  4.56 us
    reshape x1, local copies, waits for them, and re-layouts, per_device(): out = out.reshape(bands, SHIFTS, channels, ROUNDS, count_src, groups)  3.82 us
    pad x1, local copies, waits for them, and re-layouts, per_device(): jnp.pad(f_loc, ((0, 0), (f_front, blocks + lag_count // 128 - data_blocks...  2.3 us
  transfers between devices with their start and end apart: 7, of which 3 were waited for; matrix products, arithmetic and copies ran while one was open for 11% of the time, Pallas kernels for 0%

profile of v10, /device:TPU:1, one launch (start us, length us, event | category | flops | bytes accessed | tf_op | source)
XLA Modules:
  0.0 87.8 jit_solution(1145277853374142171)
XLA Ops:
  0.0 0.7 broadcast_subtract_fusion
  0.8 1.2 %convolution_convert_fusion = bf16[32,3072]{1,0:T(8,128)(2,1)S(1)} fusion(bf16[32,3072]{1,0:T(8,128)(2,1)} %param.4, s32[32]{0:T(128)S(1)} %sub.15), kind=kOutput, calls=%fused_computation | convolution fusion | flops 6390784 | bytes 393344 | tf_op jit(solution)/shard_map/dot_general | solution.py:129
  1.9 3.6 %collective-permute-start.2 = (bf16[32,3072]{1,0:T(8,128)(2,1)S(1)}, bf16[32,3072]{1,0:T(8,128)(2,1)S(1)}, u32[]{:S(2)}, u32[]{:S(2)}) collective-permute-start(bf16[32,3072]{1,0:T(8,128)(2,1)S(1)} %convolution_convert_fusion), channel_id=1, source_target_pairs={{0,24},{4,28},{8,16},{12,20},{16,8},{20,12},{24,0},{28,4},{32,56},... | collective-permute-start | bytes 589832 | tf_op jit(solution)/shard_map/ppermute | solution.py:108
  6.2 11.5 %all_gather.6 = bf16[32,12288]{1,0:T(8,128)(2,1)S(1)} all-gather(bf16[32,3072]{1,0:T(8,128)(2,1)} %param.4), channel_id=1, replica_groups=mesh['sta'=32,'tm'=4] {'tm'}, dimensions={1}, use_global_device_ids=true | all-gather | bytes 983040 | tf_op jit(solution)/shard_map/all_gather | solution.py:133
  17.8 0.8 select_convert_fusion
  18.5 0.7 add_add_fusion.1
  19.3 3.8 %collective-permute-start.5 = (bf16[32,3072]{1,0:T(8,128)(2,1)}, bf16[32,3072]{1,0:T(8,128)(2,1)}, u32[]{:S(2)}, u32[]{:S(2)}) collective-permute-start(bf16[32,3072]{1,0:T(8,128)(2,1)} %add_add_fusion.1), channel_id=1, source_target_pairs={{0,96},{4,100},{8,104},{12,108},{16,112},{20,116},{24,120},{28,124... | collective-permute-start | bytes 589832 | tf_op jit(solution)/shard_map/ppermute | solution.py:108
  23.0 0.6 collective-permute-start.3
  24.5 0.6 reshape.39
  25.3 0.7 copy.11
  26.9 2.4 %copy.22 = bf16[32,96,159,1]{2,0,1,3:T(8,128)(2,1)S(1)} copy(bf16[32,96,159,1]{1,2,0,3:T(8,128)(2,1)S(1)} %maximum_bitcast_fusion) | data formatting | bytes 1953792 | tf_op jit(solution)/shard_map/concatenate | solution.py:40
  29.2 3.4 %collective-permute-done.5 = bf16[32,3072]{1,0:T(8,128)(2,1)} collective-permute-done((bf16[32,3072]{1,0:T(8,128)(2,1)}, bf16[32,3072]{1,0:T(8,128)(2,1)}, u32[]{:S(2)}, u32[]{:S(2)}) %collective-permute-start.5) | collective-permute-done | bytes 196640 | tf_op jit(solution)/shard_map/ppermute | solution.py:108
  33.0 1.3 %add_add_fusion = bf16[32,3072]{1,0:T(8,128)(2,1)S(1)} fusion(bf16[32,3072]{1,0:T(8,128)(2,1)} %collective-permute-done.5, bf16[32,3072]{1,0:T(8,128)(2,1)} %collective-permute-done.4, bf16[32,3072]{1,0:T(8,128)(2,1)} %add_add_fusion.1, bf16[32,3072]{1,0:T(8,128)(2,1)} %collective-permute-done.3), kind=kLoop, calls=%fused_computation.11 | loop fusion | flops 294912 | bytes 983040 | tf_op jit(solution)/shard_map/add | solution.py:109
  34.7 1.0 %convert_bitcast_fusion.1 = bf16[4,96,32,128]{3,2,1,0:T(8,128)(2,1)S(1)} fusion(bf16[32,96,159,1]{2,0,1,3:T(8,128)(2,1)S(1)} %copy.22, bf16[4,128,159]{2,1,0:T(8,128)(2,1)S(1)} %reshape.39), kind=kOutput, calls=%fused_computation.2 | convolution fusion | flops 501743616 | bytes 4285440 | tf_op jit(solution)/shard_map/cnu,btu->bnct/dot_general | solution.py:41
  35.7 2.3 %pad.11.fw_ref = bf16[4,105,32,128]{3,2,1,0:T(8,128)(2,1)} pad(bf16[4,96,32,128]{3,2,1,0:T(8,128)(2,1)S(1)} %convert_bitcast_fusion.1, bf16[]{:T(256)} %constant.4.clone.1), padding=0_0x2_7x0_0x0_0 | pad | bytes 6586370 | tf_op jit(solution)/shard_map/jit(_pad)/pad | solution.py:147
  38.0 1.8 %collective-permute-done.6 = bf16[32,3072]{1,0:T(8,128)(2,1)S(1)} collective-permute-done((bf16[32,3072]{1,0:T(8,128)(2,1)S(1)}, bf16[32,3072]{1,0:T(8,128)(2,1)S(1)}, u32[]{:S(2)}, u32[]{:S(2)}) %collective-permute-start.6) | collective-permute-done | bytes 196640 | tf_op jit(solution)/shard_map/ppermute | solution.py:108
  39.9 10.9 %all_gather.7 = bf16[32,12288]{1,0:T(8,128)(2,1)S(1)} all-gather(bf16[32,3072]{1,0:T(8,128)(2,1)S(1)} %add.37), channel_id=1, replica_groups=mesh['sta'=32,'tm'=4] {'tm'}, dimensions={1}, use_global_device_ids=true | all-gather | bytes 983040 | tf_op jit(solution)/shard_map/all_gather | solution.py:133
  51.2 0.7 copy.15
  52.8 2.4 %copy.25 = bf16[32,96,159,1]{2,0,1,3:T(8,128)(2,1)S(1)} copy(bf16[32,96,159,1]{1,2,0,3:T(8,128)(2,1)S(1)} %maximum_bitcast_fusion.1) | data formatting | bytes 1953792 | tf_op jit(solution)/shard_map/concatenate | solution.py:40
  55.1 1.0 %convert_bitcast_fusion = bf16[4,96,32,128]{3,2,1,0:T(8,128)(2,1)S(1)} fusion(bf16[32,96,159,1]{2,0,1,3:T(8,128)(2,1)S(1)} %copy.25, bf16[4,128,159]{2,1,0:T(8,128)(2,1)S(1)} %reshape.39), kind=kOutput, calls=%fused_computation.1 | convolution fusion | flops 501743616 | bytes 4285440 | tf_op jit(solution)/shard_map/cnu,btu->bnct/dot_general | solution.py:41
  56.2 0.6 pad.12.pp_ref
  56.7 22.2 %shard_map.46 = bf16[4,512,256]{2,1,0:T(8,128)(2,1)S(1)} custom-call(s32[1]{0:T(128)} %bitcast.off_ref, bf16[4,105,32,128]{3,2,1,0:T(8,128)(2,1)} %pad.11.fw_ref, bf16[4,101,32,128]{3,2,1,0:T(8,128)(2,1)S(1)} %pad.12.pp_ref), custom_call_target="tpu_custom_call" | custom-call | tf_op jit(solution)/shard_map/pallas_call | solution.py:91
  79.5 3.8 %reshape.44 = bf16[4,16,32,2,16,8]{2,1,5,4,3,0:T(8,128)(2,1)} reshape(bf16[4,512,256]{1,2,0:T(8,128)(2,1)S(1)} %copy.18) | data formatting | bytes 2097152 | tf_op jit(solution)/shard_map/reshape | solution.py:155
  83.3 4.6 %copy.20 = bf16[2,4,16,32,128]{4,3,2,1,0:T(8,128)(2,1)} copy(bf16[2,4,16,32,128]{3,4,2,0,1:T(8,128)(2,1)} %bitcast.37) | data formatting | bytes 2097152 | tf_op jit(solution)/shard_map/reshape | solution.py:157
  (27 shorter events, 5.3 us)
Async XLA Ops:
  1.9 16.6 %collective-permute-start.2 = (bf16[32,3072]{1,0:T(8,128)(2,1)S(1)}, bf16[32,3072]{1,0:T(8,128)(2,1)S(1)}, u32[]{:S(2)}, u32[]{:S(2)}) collective-permute-start(bf16[32,3072]{1,0:T(8,128)(2,1)S(1)} %convolution_convert_fusion), channel_id=1, source_target_pairs={{0,24},{4,28},{8,16},{12,20},{16,8},{20,12},{24,0},{28,4},{32,56},... | collective-permute-start | bytes 589832 | tf_op jit(solution)/shard_map/ppermute | solution.py:108
  5.6 13.0 %collective-permute-start.1 = (bf16[32,3072]{1,0:T(8,128)(2,1)S(1)}, bf16[32,3072]{1,0:T(8,128)(2,1)S(1)}, u32[]{:S(2)}, u32[]{:S(2)}) collective-permute-start(bf16[32,3072]{1,0:T(8,128)(2,1)S(1)} %convolution_convert_fusion), channel_id=1, source_target_pairs={{0,16},{4,20},{8,24},{12,28},{16,0},{20,4},{24,8},{28,12},{32,48},... | collective-permute-start | bytes 589832 | tf_op jit(solution)/shard_map/ppermute | solution.py:108
  5.9 12.6 %collective-permute-start = (bf16[32,3072]{1,0:T(8,128)(2,1)S(1)}, bf16[32,3072]{1,0:T(8,128)(2,1)S(1)}, u32[]{:S(2)}, u32[]{:S(2)}) collective-permute-start(bf16[32,3072]{1,0:T(8,128)(2,1)S(1)} %convolution_convert_fusion), channel_id=1, source_target_pairs={{0,8},{4,12},{8,0},{12,4},{16,24},{20,28},{24,16},{28,20},{32,40},... | collective-permute-start | bytes 589832 | tf_op jit(solution)/shard_map/ppermute | solution.py:108
  19.3 13.4 %collective-permute-start.5 = (bf16[32,3072]{1,0:T(8,128)(2,1)}, bf16[32,3072]{1,0:T(8,128)(2,1)}, u32[]{:S(2)}, u32[]{:S(2)}) collective-permute-start(bf16[32,3072]{1,0:T(8,128)(2,1)} %add_add_fusion.1), channel_id=1, source_target_pairs={{0,96},{4,100},{8,104},{12,108},{16,112},{20,116},{24,120},{28,124... | collective-permute-start | bytes 589832 | tf_op jit(solution)/shard_map/ppermute | solution.py:108
  23.0 9.6 %collective-permute-start.4 = (bf16[32,3072]{1,0:T(8,128)(2,1)}, bf16[32,3072]{1,0:T(8,128)(2,1)}, u32[]{:S(2)}, u32[]{:S(2)}) collective-permute-start(bf16[32,3072]{1,0:T(8,128)(2,1)} %add_add_fusion.1), channel_id=1, source_target_pairs={{0,64},{4,68},{8,72},{12,76},{16,80},{20,84},{24,88},{28,92},{32,9... | collective-permute-start | bytes 589832 | tf_op jit(solution)/shard_map/ppermute | solution.py:108
  23.0 10.0 %collective-permute-start.3 = (bf16[32,3072]{1,0:T(8,128)(2,1)}, bf16[32,3072]{1,0:T(8,128)(2,1)}, u32[]{:S(2)}, u32[]{:S(2)}) collective-permute-start(bf16[32,3072]{1,0:T(8,128)(2,1)} %add_add_fusion.1), channel_id=1, source_target_pairs={{0,32},{4,36},{8,40},{12,44},{16,48},{20,52},{24,56},{28,60},{32,0... | collective-permute-start | bytes 589832 | tf_op jit(solution)/shard_map/ppermute | solution.py:108
  34.3 5.5 %collective-permute-start.6 = (bf16[32,3072]{1,0:T(8,128)(2,1)S(1)}, bf16[32,3072]{1,0:T(8,128)(2,1)S(1)}, u32[]{:S(2)}, u32[]{:S(2)}) collective-permute-start(bf16[32,3072]{1,0:T(8,128)(2,1)S(1)} %add_add_fusion), channel_id=1, source_target_pairs={{0,4},{4,0},{8,12},{12,8},{16,20},{20,16},{24,28},{28,24},{32,36},... | collective-permute-start | bytes 589832 | tf_op jit(solution)/shard_map/ppermute | solution.py:108

commit v11 on v9

--- a/solution.py
+++ b/solution.py
@@ -13,33 +13,21 @@
 CHUNK = 2560
 
 
-def skew(values, count_rows):
-    leading = values.shape[:-1]
-    length = values.shape[-1]
-    row_width = length + count_rows
-    padded = jnp.concatenate([values, jnp.zeros(leading + (count_rows,), values.dtype)], axis=-1)
-    repeated = jnp.tile(padded, (1,) * len(leading) + (count_rows,))
-    return repeated[..., : count_rows * (row_width - 1)].reshape(
-        leading + (count_rows, row_width - 1)
-    )
-
-
-def band_matrix(fir, taps, count_rows):
+def filter_in_blocks(rows, fir, taps):
+    count, length = rows.shape
     tap_limit = fir.shape[1]
+    blocks = jnp.transpose(rows.reshape(count, length // 128, 128), (1, 0, 2))
+    before = jnp.pad(blocks[:-1], ((1, 0), (0, 0), (0, 0)))
+    pieces = jnp.concatenate([before, blocks], axis=2)
     active = jnp.arange(tap_limit, dtype=jnp.int32)[None, :] < taps[:, None]
     coefficients = jnp.where(active, fir, 0.0).astype(jnp.bfloat16)
-    return skew(coefficients[:, ::-1], count_rows)
-
-
-def filter_blocks(extended, fir, taps, length, block):
-    tap_limit = fir.shape[1]
-    channels = extended.shape[0]
-    count = length // block
-    main = extended[:, tap_limit - 1 :].reshape(channels, count, block)
-    prefix = extended[:, :length].reshape(channels, count, block)[:, :, : tap_limit - 1]
-    pieces = jnp.concatenate([prefix, main], axis=2)
+    lag = 128 + lax.broadcasted_iota(jnp.int32, (128, 256), 0) - lax.broadcasted_iota(
+        jnp.int32, (128, 256), 1
+    )
+    inside = (lag >= 0) & (lag < tap_limit)
+    banded = jnp.where(inside[None], coefficients[:, jnp.clip(lag, 0, tap_limit - 1)], 0.0)
     return jnp.einsum(
-        "cnu,btu->bnct", pieces, band_matrix(fir, taps, block), preferred_element_type=jnp.float32
+        "nru,btu->bnrt", pieces, banded.astype(jnp.bfloat16), preferred_element_type=jnp.float32
     )
 
 
@@ -112,7 +100,6 @@
 
 def per_device(signal, fir, taps, sources):
     channels = signal.shape[0]
-    tap_limit = fir.shape[1]
     shards = lax.axis_size("tm")
     samples_all = signal.shape[1] * shards
     lag_count = 2 * MAXLAG
@@ -131,10 +118,7 @@
 
     def filtered_of(rows):
         rows = lax.all_gather(rows, "tm", axis=1, tiled=True)
-        extended = jnp.concatenate(
-            [jnp.zeros((rows.shape[0], tap_limit - 1), rows.dtype), rows], axis=1
-        )
-        return filter_blocks(extended, fir, taps, samples_all, 128).astype(jnp.bfloat16)
+        return filter_in_blocks(rows, fir, taps).astype(jnp.bfloat16)
 
     f_loc = filtered_of(signal)
     p_src = filtered_of(picks)

time: 88.2 us -> 210 us (2.38)
  local copies, waits for them, and re-layouts: 20.9 us -> 135 us
  waiting for transfers between devices: 5.63 us -> 11.9 us
    gather x0 -> x2, local copies, waits for them, and re-layouts: none -> 122 us  [filter_in_blocks(): coefficients[:, jnp.clip(lag, 0, tap_limit - 1)]]
    ppermute x7, waiting for transfers between devices: 5.63 us -> 11.9 us  [summed_over(): lax.ppermute(value, axis, [(i, i ^ m) for i in range(count)])]
    concatenate x3 -> x0, local copies, waits for them, and re-layouts: 4.71 us -> none  [the longest x2 4.7 us: filter_blocks(): pieces = jnp.concatenate([prefix, main], axis=2)]
  transfers between devices with their start and end apart: 7 -> 7, of which waited for: 3 -> 4; matrix products, arithmetic and copies ran while one was open for 11% -> 61% of each run, Pallas kernels for 0% -> 0%
where the time goes in v11:
time: 210 us
  local copies, waits for them, and re-layouts  135 us (64%)
  blocking collectives  22.9 us (11%)
  Pallas kernels  22.2 us (11%)
  waiting for transfers between devices  11.9 us (6%)
  starting transfers between devices  10.2 us (5%)
  matrix products  4.65 us (2%)
  other arithmetic  2.9 us (1%)
    gather x2, local copies, waits for them, and re-layouts, filter_in_blocks(): coefficients[:, jnp.clip(lag, 0, tap_limit - 1)]  122 us
    all_gather x2, blocking collectives, filtered_of(): rows = lax.all_gather(rows, 'tm', axis=1, tiled=True)  22.9 us
    pallas_call x1, Pallas kernels, correlate(): pl.pallas_call(kernel, grid_spec=grid_spec, out_shape=jax.ShapeDtypeStruc...  22.2 us
    ppermute x7, waiting for transfers between devices, summed_over(): lax.ppermute(value, axis, [(i, i ^ m) for i in range(count)])  11.9 us
    ppermute x7, starting transfers between devices, summed_over(): lax.ppermute(value, axis, [(i, i ^ m) for i in range(count)])  10.2 us
    reshape x1, local copies, waits for them, and re-layouts, per_device(): return out.reshape(ROUNDS, bands, count_src, channels, share)  4.56 us
  transfers between devices with their start and end apart: 7, of which 4 were waited for; matrix products, arithmetic and copies ran while one was open for 61% of the time, Pallas kernels for 0%

profile of v11, /device:TPU:1, one launch (start us, length us, event | category | flops | bytes accessed | tf_op | source)
XLA Modules:
  0.0 209.9 jit_solution(18016364037409492067)
XLA Ops:
  0.0 0.7 broadcast_subtract_fusion
  0.8 1.2 convolution_convert_fusion
  1.9 2.2 %collective-permute-start = (bf16[32,3072]{1,0:T(8,128)(2,1)S(1)}, bf16[32,3072]{1,0:T(8,128)(2,1)S(1)}, u32[]{:S(2)}, u32[]{:S(2)}) collective-permute-start(bf16[32,3072]{1,0:T(8,128)(2,1)S(1)} %convolution_convert_fusion), channel_id=1, source_target_pairs={{0,8},{4,12},{8,0},{12,4},{16,24},{20,28},{24,16},{28,20},{32,40},... | collective-permute-start | bytes 589832 | tf_op jit(solution)/shard_map/ppermute | solution.py:96
  4.1 2.6 %collective-permute-start.1 = (bf16[32,3072]{1,0:T(8,128)(2,1)S(1)}, bf16[32,3072]{1,0:T(8,128)(2,1)S(1)}, u32[]{:S(2)}, u32[]{:S(2)}) collective-permute-start(bf16[32,3072]{1,0:T(8,128)(2,1)S(1)} %convolution_convert_fusion), channel_id=1, source_target_pairs={{0,16},{4,20},{8,24},{12,28},{16,0},{20,4},{24,8},{28,12},{32,48},... | collective-permute-start | bytes 589832 | tf_op jit(solution)/shard_map/ppermute | solution.py:96
  6.8 11.6 %all_gather.6 = bf16[32,12288]{1,0:T(8,128)(2,1)S(1)} all-gather(bf16[32,3072]{1,0:T(8,128)(2,1)} %param.4), channel_id=1, replica_groups=mesh['sta'=32,'tm'=4] {'tm'}, dimensions={1}, use_global_device_ids=true | all-gather | bytes 983040 | tf_op jit(solution)/shard_map/all_gather | solution.py:120
  18.6 0.8 copy.10
  19.4 0.7 select_convert_fusion
  20.0 115.0 %gather_fusion = bf16[32768,4]{1,0:T(8,128)(2,1)} fusion(bf16[4,32]{0,1:T(8,128)(2,1)S(1)} %select_convert_fusion, s32[32768]{0:T(1024)S(1)} %broadcast_clamp_fusion), kind=kCustom, calls=%fused_computation | custom fusion | bytes 655360 | tf_op jit(solution)/shard_map/gather | solution.py:28
  135.0 7.1 %copy.11 = bf16[128,256,4]{1,0,2:T(8,128)(2,1)S(1)} copy(bf16[128,256,4]{2,1,0:T(8,128)(2,1)} %bitcast.40) | data formatting | bytes 524288 | tf_op jit(solution)/shard_map/gather | solution.py:28
  142.2 0.6 fusion.3
  142.9 1.7 collective-permute-start.3
  144.6 3.3 %collective-permute-start.4 = (bf16[32,3072]{1,0:T(8,128)(2,1)S(1)}, bf16[32,3072]{1,0:T(8,128)(2,1)S(1)}, u32[]{:S(2)}, u32[]{:S(2)}) collective-permute-start(bf16[32,3072]{1,0:T(8,128)(2,1)S(1)} %add_add_fusion.1), channel_id=1, source_target_pairs={{0,64},{4,68},{8,72},{12,76},{16,80},{20,84},{24,88},{28,92},{32,9... | collective-permute-start | bytes 589832 | tf_op jit(solution)/shard_map/ppermute | solution.py:96
  148.0 1.6 collective-permute-done.3
  149.7 7.4 %collective-permute-done.4 = bf16[32,3072]{1,0:T(8,128)(2,1)S(1)} collective-permute-done((bf16[32,3072]{1,0:T(8,128)(2,1)S(1)}, bf16[32,3072]{1,0:T(8,128)(2,1)S(1)}, u32[]{:S(2)}, u32[]{:S(2)}) %collective-permute-start.4) | collective-permute-done | bytes 196640 | tf_op jit(solution)/shard_map/ppermute | solution.py:96
  157.0 2.2 %collective-permute-done.5 = bf16[32,3072]{1,0:T(8,128)(2,1)S(1)} collective-permute-done((bf16[32,3072]{1,0:T(8,128)(2,1)S(1)}, bf16[32,3072]{1,0:T(8,128)(2,1)S(1)}, u32[]{:S(2)}, u32[]{:S(2)}) %collective-permute-start.5) | collective-permute-done | bytes 196640 | tf_op jit(solution)/shard_map/ppermute | solution.py:96
  159.7 1.7 convert_bitcast_fusion.1
  161.4 2.3 %pad.16.fw_ref = bf16[4,105,32,128]{3,2,1,0:T(8,128)(2,1)} pad(bf16[4,96,32,128]{3,2,1,0:T(8,128)(2,1)S(1)} %convert_bitcast_fusion.1, bf16[]{:T(256)} %constant.21.clone.1), padding=0_0x2_7x0_0x0_0 | pad | bytes 6586370 | tf_op jit(solution)/shard_map/jit(_pad)/pad | solution.py:131
  163.7 0.7 collective-permute-done.6
  164.4 11.2 %all_gather.7 = bf16[32,12288]{1,0:T(8,128)(2,1)S(1)} all-gather(bf16[32,3072]{1,0:T(8,128)(2,1)S(1)} %add.55), channel_id=1, replica_groups=mesh['sta'=32,'tm'=4] {'tm'}, dimensions={1}, use_global_device_ids=true | all-gather | bytes 983040 | tf_op jit(solution)/shard_map/all_gather | solution.py:120
  175.8 0.6 fusion.5
  176.4 1.7 convert_bitcast_fusion
  178.7 22.2 %shard_map.46 = bf16[4,512,256]{2,1,0:T(8,128)(2,1)S(1)} custom-call(s32[1]{0:T(128)} %bitcast.off_ref, bf16[4,105,32,128]{3,2,1,0:T(8,128)(2,1)} %pad.16.fw_ref, bf16[4,101,32,128]{3,2,1,0:T(8,128)(2,1)S(1)} %pad.18.pp_ref), custom_call_target="tpu_custom_call" | custom-call | tf_op jit(solution)/shard_map/pallas_call | solution.py:79
  201.5 3.8 %reshape.82 = bf16[4,16,32,2,16,8]{2,1,5,4,3,0:T(8,128)(2,1)} reshape(bf16[4,512,256]{1,2,0:T(8,128)(2,1)S(1)} %copy.14) | data formatting | bytes 2097152 | tf_op jit(solution)/shard_map/reshape | solution.py:139
  205.3 4.6 %copy.16 = bf16[2,4,16,32,128]{4,3,2,1,0:T(8,128)(2,1)} copy(bf16[2,4,16,32,128]{3,4,2,0,1:T(8,128)(2,1)} %bitcast.39) | data formatting | bytes 2097152 | tf_op jit(solution)/shard_map/reshape | solution.py:141
  (19 shorter events, 2.3 us)
Async XLA Ops:
  1.9 140.9 %collective-permute-start = (bf16[32,3072]{1,0:T(8,128)(2,1)S(1)}, bf16[32,3072]{1,0:T(8,128)(2,1)S(1)}, u32[]{:S(2)}, u32[]{:S(2)}) collective-permute-start(bf16[32,3072]{1,0:T(8,128)(2,1)S(1)} %convolution_convert_fusion), channel_id=1, source_target_pairs={{0,8},{4,12},{8,0},{12,4},{16,24},{20,28},{24,16},{28,20},{32,40},... | collective-permute-start | bytes 589832 | tf_op jit(solution)/shard_map/ppermute | solution.py:96
  4.1 138.7 %collective-permute-start.1 = (bf16[32,3072]{1,0:T(8,128)(2,1)S(1)}, bf16[32,3072]{1,0:T(8,128)(2,1)S(1)}, u32[]{:S(2)}, u32[]{:S(2)}) collective-permute-start(bf16[32,3072]{1,0:T(8,128)(2,1)S(1)} %convolution_convert_fusion), channel_id=1, source_target_pairs={{0,16},{4,20},{8,24},{12,28},{16,0},{20,4},{24,8},{28,12},{32,48},... | collective-permute-start | bytes 589832 | tf_op jit(solution)/shard_map/ppermute | solution.py:96
  6.8 136.1 %collective-permute-start.2 = (bf16[32,3072]{1,0:T(8,128)(2,1)S(1)}, bf16[32,3072]{1,0:T(8,128)(2,1)S(1)}, u32[]{:S(2)}, u32[]{:S(2)}) collective-permute-start(bf16[32,3072]{1,0:T(8,128)(2,1)S(1)} %convolution_convert_fusion), channel_id=1, source_target_pairs={{0,24},{4,28},{8,16},{12,20},{16,8},{20,12},{24,0},{28,4},{32,56},... | collective-permute-start | bytes 589832 | tf_op jit(solution)/shard_map/ppermute | solution.py:96
  142.9 6.7 %collective-permute-start.3 = (bf16[32,3072]{1,0:T(8,128)(2,1)S(1)}, bf16[32,3072]{1,0:T(8,128)(2,1)S(1)}, u32[]{:S(2)}, u32[]{:S(2)}) collective-permute-start(bf16[32,3072]{1,0:T(8,128)(2,1)S(1)} %add_add_fusion.1), channel_id=1, source_target_pairs={{0,32},{4,36},{8,40},{12,44},{16,48},{20,52},{24,56},{28,60},{32,0... | collective-permute-start | bytes 589832 | tf_op jit(solution)/shard_map/ppermute | solution.py:96
  144.6 12.4 %collective-permute-start.4 = (bf16[32,3072]{1,0:T(8,128)(2,1)S(1)}, bf16[32,3072]{1,0:T(8,128)(2,1)S(1)}, u32[]{:S(2)}, u32[]{:S(2)}) collective-permute-start(bf16[32,3072]{1,0:T(8,128)(2,1)S(1)} %add_add_fusion.1), channel_id=1, source_target_pairs={{0,64},{4,68},{8,72},{12,76},{16,80},{20,84},{24,88},{28,92},{32,9... | collective-permute-start | bytes 589832 | tf_op jit(solution)/shard_map/ppermute | solution.py:96
  147.9 11.3 %collective-permute-start.5 = (bf16[32,3072]{1,0:T(8,128)(2,1)S(1)}, bf16[32,3072]{1,0:T(8,128)(2,1)S(1)}, u32[]{:S(2)}, u32[]{:S(2)}) collective-permute-start(bf16[32,3072]{1,0:T(8,128)(2,1)S(1)} %add_add_fusion.1), channel_id=1, source_target_pairs={{0,96},{4,100},{8,104},{12,108},{16,112},{20,116},{24,120},{28,124... | collective-permute-start | bytes 589832 | tf_op jit(solution)/shard_map/ppermute | solution.py:96
  159.3 5.1 %collective-permute-start.6 = (bf16[32,3072]{1,0:T(8,128)(2,1)S(1)}, bf16[32,3072]{1,0:T(8,128)(2,1)S(1)}, u32[]{:S(2)}, u32[]{:S(2)}) collective-permute-start(bf16[32,3072]{1,0:T(8,128)(2,1)S(1)} %add_add_fusion), channel_id=1, source_target_pairs={{0,4},{4,0},{8,12},{12,8},{16,20},{20,16},{24,28},{28,24},{32,36},... | collective-permute-start | bytes 589832 | tf_op jit(solution)/shard_map/ppermute | solution.py:96

commit v12 on v9

--- a/solution.py
+++ b/solution.py
@@ -31,15 +31,15 @@
     return skew(coefficients[:, ::-1], count_rows)
 
 
-def filter_blocks(extended, fir, taps, length, block):
+def filter_in_blocks(rows, fir, taps):
+    count, length = rows.shape
     tap_limit = fir.shape[1]
-    channels = extended.shape[0]
-    count = length // block
-    main = extended[:, tap_limit - 1 :].reshape(channels, count, block)
-    prefix = extended[:, :length].reshape(channels, count, block)[:, :, : tap_limit - 1]
-    pieces = jnp.concatenate([prefix, main], axis=2)
+    blocks = jnp.transpose(rows.reshape(count, length // 128, 128), (1, 0, 2))
+    before = jnp.pad(blocks[:-1], ((1, 0), (0, 0), (0, 0)))
+    pieces = jnp.concatenate([before, blocks], axis=2)
+    banded = jnp.pad(band_matrix(fir, taps, 128), ((0, 0), (0, 0), (129 - tap_limit, 0)))
     return jnp.einsum(
-        "cnu,btu->bnct", pieces, band_matrix(fir, taps, block), preferred_element_type=jnp.float32
+        "nru,btu->bnrt", pieces, banded, preferred_element_type=jnp.float32
     )
 
 
@@ -112,7 +112,6 @@
 
 def per_device(signal, fir, taps, sources):
     channels = signal.shape[0]
-    tap_limit = fir.shape[1]
     shards = lax.axis_size("tm")
     samples_all = signal.shape[1] * shards
     lag_count = 2 * MAXLAG
@@ -131,10 +130,7 @@
 
     def filtered_of(rows):
         rows = lax.all_gather(rows, "tm", axis=1, tiled=True)
-        extended = jnp.concatenate(
-            [jnp.zeros((rows.shape[0], tap_limit - 1), rows.dtype), rows], axis=1
-        )
-        return filter_blocks(extended, fir, taps, samples_all, 128).astype(jnp.bfloat16)
+        return filter_in_blocks(rows, fir, taps).astype(jnp.bfloat16)
 
     f_loc = filtered_of(signal)
     p_src = filtered_of(picks)

time: 88.2 us -> 82.5 us (0.935)
  local copies, waits for them, and re-layouts: 20.9 us -> 13.3 us
  waiting for transfers between devices: 5.63 us -> 8.13 us
  other arithmetic: 4.29 us -> 2.12 us
  matrix products: 3.2 us -> 4.64 us
    concatenate x2 -> x0, local copies, waits for them, and re-layouts: 4.7 us -> none  [filter_blocks(): pieces = jnp.concatenate([prefix, main], axis=2)]
    ppermute x7, waiting for transfers between devices: 5.63 us -> 8.13 us  [summed_over(): lax.ppermute(value, axis, [(i, i ^ m) for i in range(count)])]
    add x3, other arithmetic: 2.02 us -> 0.13 us  [summed_over(): value = sum(parts, value)]
    unnamed x8 -> x6, local copies, waits for them, and re-layouts: 1.83 us -> 0.29 us
    dot_general x2, matrix products: 2.03 us -> 3.47 us  [filter_in_blocks(): jnp.einsum('nru,btu->bnrt', pieces, banded, preferred_element_type=jnp.fl...]
    reshape x2 -> x0, local copies, waits for them, and re-layouts: 1.31 us -> none  [filter_blocks(): main = extended[:, tap_limit - 1:].reshape(channels, count, block)]
  transfers between devices with their start and end apart: 7 -> 7, of which waited for: 3 -> 3; matrix products, arithmetic and copies ran while one was open for 11% -> 7% of each run, Pallas kernels for 0% -> 0%
where the time goes in v12:
time: 82.5 us; the launch traced here: 82.2 us
  blocking collectives  22.4 us (27%)
  Pallas kernels  22.2 us (27%)
  local copies, waits for them, and re-layouts  13.3 us (16%)
  starting transfers between devices  9.2 us (11%)
  waiting for transfers between devices  8.13 us (10%)
  matrix products  4.64 us (6%)
  other arithmetic  2.12 us (3%)
    all_gather x2, blocking collectives, filtered_of(): rows = lax.all_gather(rows, 'tm', axis=1, tiled=True)  22.4 us
    pallas_call x1, Pallas kernels, correlate(): pl.pallas_call(kernel, grid_spec=grid_spec, out_shape=jax.ShapeDtypeStruc...  22.2 us
    ppermute x7, starting transfers between devices, summed_over(): lax.ppermute(value, axis, [(i, i ^ m) for i in range(count)])  9.2 us
    ppermute x7, waiting for transfers between devices, summed_over(): lax.ppermute(value, axis, [(i, i ^ m) for i in range(count)])  8.13 us
    reshape x1, local copies, waits for them, and re-layouts, per_device(): return out.reshape(ROUNDS, bands, count_src, channels, share)  4.56 us
    reshape x1, local copies, waits for them, and re-layouts, per_device(): out = out.reshape(bands, SHIFTS, channels, ROUNDS, count_src, groups)  3.8 us
    dot_general x2, matrix products, filter_in_blocks(): jnp.einsum('nru,btu->bnrt', pieces, banded, preferred_element_type=jnp.fl...  3.47 us
    pad x1, local copies, waits for them, and re-layouts, per_device(): jnp.pad(f_loc, ((0, 0), (f_front, blocks + lag_count // 128 - data_blocks...  2.29 us
  transfers between devices with their start and end apart: 7, of which 3 were waited for; matrix products, arithmetic and copies ran while one was open for 7% of the time, Pallas kernels for 0%

profile of v12, /device:TPU:1, one launch (start us, length us, event | category | flops | bytes accessed | tf_op | source)
XLA Modules:
  0.0 82.2 jit_solution(12804002361614258415)
XLA Ops:
  0.0 0.7 broadcast_subtract_fusion
  0.8 1.2 %convolution_convert_fusion = bf16[32,3072]{1,0:T(8,128)(2,1)S(1)} fusion(bf16[32,3072]{1,0:T(8,128)(2,1)} %param.4, s32[32]{0:T(128)S(1)} %sub.15), kind=kOutput, calls=%fused_computation | convolution fusion | flops 6390784 | bytes 393344 | tf_op jit(solution)/shard_map/dot_general | solution.py:128
  2.0 3.6 %collective-permute-start.2 = (bf16[32,3072]{1,0:T(8,128)(2,1)S(1)}, bf16[32,3072]{1,0:T(8,128)(2,1)S(1)}, u32[]{:S(2)}, u32[]{:S(2)}) collective-permute-start(bf16[32,3072]{1,0:T(8,128)(2,1)S(1)} %convolution_convert_fusion), channel_id=1, source_target_pairs={{0,24},{4,28},{8,16},{12,20},{16,8},{20,12},{24,0},{28,4},{32,56},... | collective-permute-start | bytes 589832 | tf_op jit(solution)/shard_map/ppermute | solution.py:108
  5.6 0.3 collective-permute-start.1
  6.3 11.5 %all_gather.6 = bf16[32,12288]{1,0:T(8,128)(2,1)S(1)} all-gather(bf16[32,3072]{1,0:T(8,128)(2,1)} %param.4), channel_id=1, replica_groups=mesh['sta'=32,'tm'=4] {'tm'}, dimensions={1}, use_global_device_ids=true | all-gather | bytes 983040 | tf_op jit(solution)/shard_map/all_gather | solution.py:132
  17.9 3.8 %collective-permute-start.5 = (bf16[32,3072]{1,0:T(8,128)(2,1)S(1)}, bf16[32,3072]{1,0:T(8,128)(2,1)S(1)}, u32[]{:S(2)}, u32[]{:S(2)}) collective-permute-start(bf16[32,3072]{1,0:T(8,128)(2,1)S(1)} %add_add_fusion.1), channel_id=1, source_target_pairs={{0,96},{4,100},{8,104},{12,108},{16,112},{20,116},{24,120},{28,124... | collective-permute-start | bytes 589832 | tf_op jit(solution)/shard_map/ppermute | solution.py:108
  21.7 0.7 collective-permute-start.3
  22.6 0.4 tile.5
  23.0 0.6 reshape.33
  23.8 0.6 fusion.3
  24.4 6.6 %collective-permute-done.5 = bf16[32,3072]{1,0:T(8,128)(2,1)S(1)} collective-permute-done((bf16[32,3072]{1,0:T(8,128)(2,1)S(1)}, bf16[32,3072]{1,0:T(8,128)(2,1)S(1)}, u32[]{:S(2)}, u32[]{:S(2)}) %collective-permute-start.5) | collective-permute-done | bytes 196640 | tf_op jit(solution)/shard_map/ppermute | solution.py:108
  31.0 0.5 collective-permute-done.3
  31.5 0.4 collective-permute-start.6
  31.9 1.7 %convert_bitcast_fusion.1 = bf16[4,96,32,128]{3,2,1,0:T(8,128)(2,1)S(1)} fusion(bf16[96,32,256,1]{2,0,1,3:T(8,128)(2,1)S(1)} %fusion.3, bf16[4,128,159]{2,1,0:T(8,128)(2,1)S(1)} %reshape.33), kind=kOutput, calls=%fused_computation.5 | convolution fusion | flops 806879232 | bytes 4881408 | tf_op jit(solution)/shard_map/nru,btu->bnrt/dot_general | solution.py:41
  33.7 2.3 %pad.23.fw_ref = bf16[4,105,32,128]{3,2,1,0:T(8,128)(2,1)} pad(bf16[4,96,32,128]{3,2,1,0:T(8,128)(2,1)S(1)} %convert_bitcast_fusion.1, bf16[]{:T(256)} %constant.5.clone.1), padding=0_0x2_7x0_0x0_0 | pad | bytes 6586370 | tf_op jit(solution)/shard_map/jit(_pad)/pad | solution.py:143
  35.9 1.1 %collective-permute-done.6 = bf16[32,3072]{1,0:T(8,128)(2,1)S(1)} collective-permute-done((bf16[32,3072]{1,0:T(8,128)(2,1)S(1)}, bf16[32,3072]{1,0:T(8,128)(2,1)S(1)}, u32[]{:S(2)}, u32[]{:S(2)}) %collective-permute-start.6) | collective-permute-done | bytes 196640 | tf_op jit(solution)/shard_map/ppermute | solution.py:108
  37.1 10.9 %all_gather.7 = bf16[32,12288]{1,0:T(8,128)(2,1)S(1)} all-gather(bf16[32,3072]{1,0:T(8,128)(2,1)S(1)} %add.39), channel_id=1, replica_groups=mesh['sta'=32,'tm'=4] {'tm'}, dimensions={1}, use_global_device_ids=true | all-gather | bytes 983040 | tf_op jit(solution)/shard_map/all_gather | solution.py:132
  48.1 0.6 fusion.5
  48.8 1.7 %convert_bitcast_fusion = bf16[4,96,32,128]{3,2,1,0:T(8,128)(2,1)S(1)} fusion(bf16[96,32,256,1]{2,0,1,3:T(8,128)(2,1)S(1)} %fusion.5, bf16[4,128,159]{2,1,0:T(8,128)(2,1)S(1)} %reshape.33), kind=kOutput, calls=%fused_computation.4 | convolution fusion | flops 806879232 | bytes 4881408 | tf_op jit(solution)/shard_map/nru,btu->bnrt/dot_general | solution.py:41
  50.5 0.6 pad.25.pp_ref
  51.1 22.2 %shard_map.46 = bf16[4,512,256]{2,1,0:T(8,128)(2,1)S(1)} custom-call(s32[1]{0:T(128)} %bitcast.off_ref, bf16[4,105,32,128]{3,2,1,0:T(8,128)(2,1)} %pad.23.fw_ref, bf16[4,101,32,128]{3,2,1,0:T(8,128)(2,1)S(1)} %pad.25.pp_ref), custom_call_target="tpu_custom_call" | custom-call | tf_op jit(solution)/shard_map/pallas_call | solution.py:91
  73.3 0.5 copy.10
  73.8 3.8 %reshape.36 = bf16[4,16,32,2,16,8]{2,1,5,4,3,0:T(8,128)(2,1)} reshape(bf16[4,512,256]{1,2,0:T(8,128)(2,1)S(1)} %copy.10) | data formatting | bytes 2097152 | tf_op jit(solution)/shard_map/reshape | solution.py:151
  77.6 4.6 %copy.12 = bf16[2,4,16,32,128]{4,3,2,1,0:T(8,128)(2,1)} copy(bf16[2,4,16,32,128]{3,4,2,0,1:T(8,128)(2,1)} %bitcast.32) | data formatting | bytes 2097152 | tf_op jit(solution)/shard_map/reshape | solution.py:153
  (21 shorter events, 1.1 us)
Async XLA Ops:
  0.0 22.4 %copy-start.1 = (s32[4]{0:T(128)S(1)}, s32[4]{0:T(128)}, u32[]{:S(2)}) copy-start(s32[4]{0:T(128)} %param.6) | copy-start | bytes 52
  0.0 22.4 %copy-start = (f32[4,32]{1,0:T(4,128)S(1)}, f32[4,32]{1,0:T(4,128)}, u32[]{:S(2)}) copy-start(f32[4,32]{1,0:T(4,128)} %param.5) | copy-start | bytes 1540
  2.0 15.8 %collective-permute-start.2 = (bf16[32,3072]{1,0:T(8,128)(2,1)S(1)}, bf16[32,3072]{1,0:T(8,128)(2,1)S(1)}, u32[]{:S(2)}, u32[]{:S(2)}) collective-permute-start(bf16[32,3072]{1,0:T(8,128)(2,1)S(1)} %convolution_convert_fusion), channel_id=1, source_target_pairs={{0,24},{4,28},{8,16},{12,20},{16,8},{20,12},{24,0},{28,4},{32,56},... | collective-permute-start | bytes 589832 | tf_op jit(solution)/shard_map/ppermute | solution.py:108
  5.6 12.2 %collective-permute-start.1 = (bf16[32,3072]{1,0:T(8,128)(2,1)S(1)}, bf16[32,3072]{1,0:T(8,128)(2,1)S(1)}, u32[]{:S(2)}, u32[]{:S(2)}) collective-permute-start(bf16[32,3072]{1,0:T(8,128)(2,1)S(1)} %convolution_convert_fusion), channel_id=1, source_target_pairs={{0,16},{4,20},{8,24},{12,28},{16,0},{20,4},{24,8},{28,12},{32,48},... | collective-permute-start | bytes 589832 | tf_op jit(solution)/shard_map/ppermute | solution.py:108
  6.0 11.9 %collective-permute-start = (bf16[32,3072]{1,0:T(8,128)(2,1)S(1)}, bf16[32,3072]{1,0:T(8,128)(2,1)S(1)}, u32[]{:S(2)}, u32[]{:S(2)}) collective-permute-start(bf16[32,3072]{1,0:T(8,128)(2,1)S(1)} %convolution_convert_fusion), channel_id=1, source_target_pairs={{0,8},{4,12},{8,0},{12,4},{16,24},{20,28},{24,16},{28,20},{32,40},... | collective-permute-start | bytes 589832 | tf_op jit(solution)/shard_map/ppermute | solution.py:108
  17.9 13.1 %collective-permute-start.5 = (bf16[32,3072]{1,0:T(8,128)(2,1)S(1)}, bf16[32,3072]{1,0:T(8,128)(2,1)S(1)}, u32[]{:S(2)}, u32[]{:S(2)}) collective-permute-start(bf16[32,3072]{1,0:T(8,128)(2,1)S(1)} %add_add_fusion.1), channel_id=1, source_target_pairs={{0,96},{4,100},{8,104},{12,108},{16,112},{20,116},{24,120},{28,124... | collective-permute-start | bytes 589832 | tf_op jit(solution)/shard_map/ppermute | solution.py:108
  21.7 9.3 %collective-permute-start.4 = (bf16[32,3072]{1,0:T(8,128)(2,1)S(1)}, bf16[32,3072]{1,0:T(8,128)(2,1)S(1)}, u32[]{:S(2)}, u32[]{:S(2)}) collective-permute-start(bf16[32,3072]{1,0:T(8,128)(2,1)S(1)} %add_add_fusion.1), channel_id=1, source_target_pairs={{0,64},{4,68},{8,72},{12,76},{16,80},{20,84},{24,88},{28,92},{32,9... | collective-permute-start | bytes 589832 | tf_op jit(solution)/shard_map/ppermute | solution.py:108
  21.7 9.8 %collective-permute-start.3 = (bf16[32,3072]{1,0:T(8,128)(2,1)S(1)}, bf16[32,3072]{1,0:T(8,128)(2,1)S(1)}, u32[]{:S(2)}, u32[]{:S(2)}) collective-permute-start(bf16[32,3072]{1,0:T(8,128)(2,1)S(1)} %add_add_fusion.1), channel_id=1, source_target_pairs={{0,32},{4,36},{8,40},{12,44},{16,48},{20,52},{24,56},{28,60},{32,0... | collective-permute-start | bytes 589832 | tf_op jit(solution)/shard_map/ppermute | solution.py:108
  31.5 5.5 %collective-permute-start.6 = (bf16[32,3072]{1,0:T(8,128)(2,1)S(1)}, bf16[32,3072]{1,0:T(8,128)(2,1)S(1)}, u32[]{:S(2)}, u32[]{:S(2)}) collective-permute-start(bf16[32,3072]{1,0:T(8,128)(2,1)S(1)} %add_add_fusion), channel_id=1, source_target_pairs={{0,4},{4,0},{8,12},{12,8},{16,20},{20,16},{24,28},{28,24},{32,36},... | collective-permute-start | bytes 589832 | tf_op jit(solution)/shard_map/ppermute | solution.py:108

commit v13 on v12

--- a/solution.py
+++ b/solution.py
@@ -31,12 +31,13 @@
     return skew(coefficients[:, ::-1], count_rows)
 
 
-def filter_in_blocks(rows, fir, taps):
+def filter_in_blocks(rows, fir, taps, front, back):
     count, length = rows.shape
     tap_limit = fir.shape[1]
     blocks = jnp.transpose(rows.reshape(count, length // 128, 128), (1, 0, 2))
     before = jnp.pad(blocks[:-1], ((1, 0), (0, 0), (0, 0)))
     pieces = jnp.concatenate([before, blocks], axis=2)
+    pieces = jnp.pad(pieces, ((front, back), (0, 0), (0, 0)))
     banded = jnp.pad(band_matrix(fir, taps, 128), ((0, 0), (0, 0), (129 - tap_limit, 0)))
     return jnp.einsum(
         "nru,btu->bnrt", pieces, banded, preferred_element_type=jnp.float32
@@ -128,22 +129,20 @@
     picks = jnp.dot(onehot, signal, preferred_element_type=jnp.float32).astype(jnp.bfloat16)
     picks = summed_over(picks, "sta")
 
-    def filtered_of(rows):
-        rows = lax.all_gather(rows, "tm", axis=1, tiled=True)
-        return filter_in_blocks(rows, fir, taps).astype(jnp.bfloat16)
-
-    f_loc = filtered_of(signal)
-    p_src = filtered_of(picks)
-
     span = samples_all + (groups - 1) * SHIFTS
     chunks = -(-span // CHUNK)
     blocks = chunks * CHUNK // 128 + 1
     data_blocks = samples_all // 128
     f_front = MAXLAG // 128
-    f_blocks = jnp.pad(
-        f_loc, ((0, 0), (f_front, blocks + lag_count // 128 - data_blocks - f_front), (0, 0), (0, 0))
-    )
-    p_blocks = jnp.pad(p_src, ((0, 0), (1, blocks - data_blocks - 1), (0, 0), (0, 0)))
+    f_back = blocks + lag_count // 128 - data_blocks - f_front
+    p_back = blocks - data_blocks - 1
+
+    def filtered_of(rows, front, back):
+        rows = lax.all_gather(rows, "tm", axis=1, tiled=True)
+        return filter_in_blocks(rows, fir, taps, front, back).astype(jnp.bfloat16)
+
+    f_blocks = filtered_of(signal, f_front, f_back)
+    p_blocks = filtered_of(picks, 1, p_back)
     offset = (lax.axis_index("tm") * (share // 128)).astype(jnp.int32).reshape(1)
 
     out = correlate(offset, f_blocks, p_blocks, share, chunks, norm_scale)

time: 82.5 us -> 82.6 us (level)
  no operation moved by 1% of the time
where the time goes in v13:
time: 82.6 us; the launch traced here: 82.4 us
  blocking collectives  22.4 us (27%)
  Pallas kernels  22.2 us (27%)
  local copies, waits for them, and re-layouts  12.6 us (15%)
  starting transfers between devices  9.2 us (11%)
  waiting for transfers between devices  8.42 us (10%)
  matrix products  5.2 us (6%)
  other arithmetic  2.12 us (3%)
    all_gather x2, blocking collectives, filtered_of(): rows = lax.all_gather(rows, 'tm', axis=1, tiled=True)  22.4 us
    pallas_call x1, Pallas kernels, correlate(): pl.pallas_call(kernel, grid_spec=grid_spec, out_shape=jax.ShapeDtypeStruc...  22.2 us
    ppermute x7, starting transfers between devices, summed_over(): lax.ppermute(value, axis, [(i, i ^ m) for i in range(count)])  9.2 us
    ppermute x7, waiting for transfers between devices, summed_over(): lax.ppermute(value, axis, [(i, i ^ m) for i in range(count)])  8.42 us
    reshape x1, local copies, waits for them, and re-layouts, per_device(): return out.reshape(ROUNDS, bands, count_src, channels, share)  4.56 us
    dot_general x2, matrix products, filter_in_blocks(): jnp.einsum('nru,btu->bnrt', pieces, banded, preferred_element_type=jnp.fl...  4.03 us
    reshape x1, local copies, waits for them, and re-layouts, per_device(): out = out.reshape(bands, SHIFTS, channels, ROUNDS, count_src, groups)  3.8 us
    pad x2, local copies, waits for them, and re-layouts, filter_in_blocks(): pieces = jnp.pad(pieces, ((front, back), (0, 0), (0, 0)))  2.16 us
  transfers between devices with their start and end apart: 7, of which 3 were waited for; matrix products, arithmetic and copies ran while one was open for 7% of the time, Pallas kernels for 0%

profile of v13, /device:TPU:1, one launch (start us, length us, event | category | flops | bytes accessed | tf_op | source)
XLA Modules:
  0.0 82.4 jit_solution(14056336444727865200)
XLA Ops:
  0.0 0.7 broadcast_subtract_fusion
  0.8 1.2 %convolution_convert_fusion = bf16[32,3072]{1,0:T(8,128)(2,1)S(1)} fusion(bf16[32,3072]{1,0:T(8,128)(2,1)} %param.4, s32[32]{0:T(128)S(1)} %sub.15), kind=kOutput, calls=%fused_computation.1 | convolution fusion | flops 6390784 | bytes 393344 | tf_op jit(solution)/shard_map/dot_general | solution.py:129
  2.0 3.6 %collective-permute-start.2 = (bf16[32,3072]{1,0:T(8,128)(2,1)S(1)}, bf16[32,3072]{1,0:T(8,128)(2,1)S(1)}, u32[]{:S(2)}, u32[]{:S(2)}) collective-permute-start(bf16[32,3072]{1,0:T(8,128)(2,1)S(1)} %convolution_convert_fusion), channel_id=1, source_target_pairs={{0,24},{4,28},{8,16},{12,20},{16,8},{20,12},{24,0},{28,4},{32,56},... | collective-permute-start | bytes 589832 | tf_op jit(solution)/shard_map/ppermute | solution.py:109
  5.6 0.3 collective-permute-start.1
  6.3 11.5 %all_gather.6 = bf16[32,12288]{1,0:T(8,128)(2,1)S(1)} all-gather(bf16[32,3072]{1,0:T(8,128)(2,1)} %param.4), channel_id=1, replica_groups=mesh['sta'=32,'tm'=4] {'tm'}, dimensions={1}, use_global_device_ids=true | all-gather | bytes 983040 | tf_op jit(solution)/shard_map/all_gather | solution.py:141
  18.1 3.8 %collective-permute-start.5 = (bf16[32,3072]{1,0:T(8,128)(2,1)S(1)}, bf16[32,3072]{1,0:T(8,128)(2,1)S(1)}, u32[]{:S(2)}, u32[]{:S(2)}) collective-permute-start(bf16[32,3072]{1,0:T(8,128)(2,1)S(1)} %add_add_fusion.1), channel_id=1, source_target_pairs={{0,96},{4,100},{8,104},{12,108},{16,112},{20,116},{24,120},{28,124... | collective-permute-start | bytes 589832 | tf_op jit(solution)/shard_map/ppermute | solution.py:109
  21.9 0.7 collective-permute-start.3
  22.6 0.6 fusion.4
  23.4 0.4 tile.5
  23.8 0.6 reshape.33
  24.4 1.1 %pad_bitcast_fusion = bf16[105,32,256,1]{2,0,1,3:T(8,128)(2,1)S(1)} fusion(bf16[96,32,256]{2,0,1:T(8,128)(2,1)S(1)} %fusion.4), kind=kLoop, calls=%fused_computation.6 | loop fusion | bytes 3293184 | tf_op jit(solution)/shard_map/jit(_pad)/pad | solution.py:40
  25.5 5.7 %collective-permute-done.5 = bf16[32,3072]{1,0:T(8,128)(2,1)S(1)} collective-permute-done((bf16[32,3072]{1,0:T(8,128)(2,1)S(1)}, bf16[32,3072]{1,0:T(8,128)(2,1)S(1)}, u32[]{:S(2)}, u32[]{:S(2)}) %collective-permute-start.5) | collective-permute-done | bytes 196640 | tf_op jit(solution)/shard_map/ppermute | solution.py:109
  31.2 0.5 collective-permute-done.3
  31.8 0.4 collective-permute-start.6
  32.2 2.9 %convert_bitcast_fusion.fw_ref = bf16[4,105,32,128]{3,2,1,0:T(8,128)(2,1)} fusion(bf16[105,32,256,1]{2,0,1,3:T(8,128)(2,1)S(1)} %pad_bitcast_fusion, bf16[4,128,159]{2,1,0:T(8,128)(2,1)S(1)} %reshape.33), kind=kOutput, calls=%fused_computation | convolution fusion | flops 882524160 | bytes 5323776 | tf_op jit(solution)/shard_map/nru,btu->bnrt/dot_general | solution.py:42
  35.0 2.2 %collective-permute-done.6 = bf16[32,3072]{1,0:T(8,128)(2,1)S(1)} collective-permute-done((bf16[32,3072]{1,0:T(8,128)(2,1)S(1)}, bf16[32,3072]{1,0:T(8,128)(2,1)S(1)}, u32[]{:S(2)}, u32[]{:S(2)}) %collective-permute-start.6) | collective-permute-done | bytes 196640 | tf_op jit(solution)/shard_map/ppermute | solution.py:109
  37.3 10.9 %all_gather.7 = bf16[32,12288]{1,0:T(8,128)(2,1)S(1)} all-gather(bf16[32,3072]{1,0:T(8,128)(2,1)S(1)} %add.39), channel_id=1, replica_groups=mesh['sta'=32,'tm'=4] {'tm'}, dimensions={1}, use_global_device_ids=true | all-gather | bytes 983040 | tf_op jit(solution)/shard_map/all_gather | solution.py:141
  48.4 0.6 fusion.5
  49.0 1.1 %pad_bitcast_fusion.1 = bf16[101,32,256,1]{2,0,1,3:T(8,128)(2,1)S(1)} fusion(bf16[96,32,256]{2,0,1:T(8,128)(2,1)S(1)} %fusion.5), kind=kLoop, calls=%fused_computation.8 | loop fusion | bytes 3227648 | tf_op jit(solution)/shard_map/jit(_pad)/pad | solution.py:40
  50.1 1.1 %convert_bitcast_fusion.1.pp_ref = bf16[4,101,32,128]{3,2,1,0:T(8,128)(2,1)S(1)} fusion(bf16[101,32,256,1]{2,0,1,3:T(8,128)(2,1)S(1)} %pad_bitcast_fusion.1, bf16[4,128,159]{2,1,0:T(8,128)(2,1)S(1)} %reshape.33), kind=kOutput, calls=%fused_computation.2 | convolution fusion | flops 848904192 | bytes 5127168 | tf_op jit(solution)/shard_map/nru,btu->bnrt/dot_general | solution.py:42
  51.2 22.2 %shard_map.46 = bf16[4,512,256]{2,1,0:T(8,128)(2,1)S(1)} custom-call(s32[1]{0:T(128)} %bitcast.off_ref, bf16[4,105,32,128]{3,2,1,0:T(8,128)(2,1)} %convert_bitcast_fusion.fw_ref, bf16[4,101,32,128]{3,2,1,0:T(8,128)(2,1)S(1)} %convert_bitcast_fusion.1.pp_ref), custom_call_target="tpu_custom_call" | custom-call | tf_op jit(solution)/shard_map/pallas_call | solution.py:92
  73.5 0.5 copy.10
  74.0 3.8 %reshape.36 = bf16[4,16,32,2,16,8]{2,1,5,4,3,0:T(8,128)(2,1)} reshape(bf16[4,512,256]{1,2,0:T(8,128)(2,1)S(1)} %copy.10) | data formatting | bytes 2097152 | tf_op jit(solution)/shard_map/reshape | solution.py:150
  77.8 4.6 %copy.12 = bf16[2,4,16,32,128]{4,3,2,1,0:T(8,128)(2,1)} copy(bf16[2,4,16,32,128]{3,4,2,0,1:T(8,128)(2,1)} %bitcast.32) | data formatting | bytes 2097152 | tf_op jit(solution)/shard_map/reshape | solution.py:152
  (21 shorter events, 1.1 us)
Async XLA Ops:
  0.0 18.0 %copy-start.1 = (s32[4]{0:T(128)S(1)}, s32[4]{0:T(128)}, u32[]{:S(2)}) copy-start(s32[4]{0:T(128)} %param.6) | copy-start | bytes 52
  0.0 18.0 %copy-start = (f32[4,32]{1,0:T(4,128)S(1)}, f32[4,32]{1,0:T(4,128)}, u32[]{:S(2)}) copy-start(f32[4,32]{1,0:T(4,128)} %param.5) | copy-start | bytes 1540
  2.0 16.1 %collective-permute-start.2 = (bf16[32,3072]{1,0:T(8,128)(2,1)S(1)}, bf16[32,3072]{1,0:T(8,128)(2,1)S(1)}, u32[]{:S(2)}, u32[]{:S(2)}) collective-permute-start(bf16[32,3072]{1,0:T(8,128)(2,1)S(1)} %convolution_convert_fusion), channel_id=1, source_target_pairs={{0,24},{4,28},{8,16},{12,20},{16,8},{20,12},{24,0},{28,4},{32,56},... | collective-permute-start | bytes 589832 | tf_op jit(solution)/shard_map/ppermute | solution.py:109
  5.6 12.4 %collective-permute-start.1 = (bf16[32,3072]{1,0:T(8,128)(2,1)S(1)}, bf16[32,3072]{1,0:T(8,128)(2,1)S(1)}, u32[]{:S(2)}, u32[]{:S(2)}) collective-permute-start(bf16[32,3072]{1,0:T(8,128)(2,1)S(1)} %convolution_convert_fusion), channel_id=1, source_target_pairs={{0,16},{4,20},{8,24},{12,28},{16,0},{20,4},{24,8},{28,12},{32,48},... | collective-permute-start | bytes 589832 | tf_op jit(solution)/shard_map/ppermute | solution.py:109
  6.0 12.1 %collective-permute-start = (bf16[32,3072]{1,0:T(8,128)(2,1)S(1)}, bf16[32,3072]{1,0:T(8,128)(2,1)S(1)}, u32[]{:S(2)}, u32[]{:S(2)}) collective-permute-start(bf16[32,3072]{1,0:T(8,128)(2,1)S(1)} %convolution_convert_fusion), channel_id=1, source_target_pairs={{0,8},{4,12},{8,0},{12,4},{16,24},{20,28},{24,16},{28,20},{32,40},... | collective-permute-start | bytes 589832 | tf_op jit(solution)/shard_map/ppermute | solution.py:109
  18.1 13.1 %collective-permute-start.5 = (bf16[32,3072]{1,0:T(8,128)(2,1)S(1)}, bf16[32,3072]{1,0:T(8,128)(2,1)S(1)}, u32[]{:S(2)}, u32[]{:S(2)}) collective-permute-start(bf16[32,3072]{1,0:T(8,128)(2,1)S(1)} %add_add_fusion.1), channel_id=1, source_target_pairs={{0,96},{4,100},{8,104},{12,108},{16,112},{20,116},{24,120},{28,124... | collective-permute-start | bytes 589832 | tf_op jit(solution)/shard_map/ppermute | solution.py:109
  21.9 9.3 %collective-permute-start.4 = (bf16[32,3072]{1,0:T(8,128)(2,1)S(1)}, bf16[32,3072]{1,0:T(8,128)(2,1)S(1)}, u32[]{:S(2)}, u32[]{:S(2)}) collective-permute-start(bf16[32,3072]{1,0:T(8,128)(2,1)S(1)} %add_add_fusion.1), channel_id=1, source_target_pairs={{0,64},{4,68},{8,72},{12,76},{16,80},{20,84},{24,88},{28,92},{32,9... | collective-permute-start | bytes 589832 | tf_op jit(solution)/shard_map/ppermute | solution.py:109
  21.9 9.8 %collective-permute-start.3 = (bf16[32,3072]{1,0:T(8,128)(2,1)S(1)}, bf16[32,3072]{1,0:T(8,128)(2,1)S(1)}, u32[]{:S(2)}, u32[]{:S(2)}) collective-permute-start(bf16[32,3072]{1,0:T(8,128)(2,1)S(1)} %add_add_fusion.1), channel_id=1, source_target_pairs={{0,32},{4,36},{8,40},{12,44},{16,48},{20,52},{24,56},{28,60},{32,0... | collective-permute-start | bytes 589832 | tf_op jit(solution)/shard_map/ppermute | solution.py:109
  31.8 5.5 %collective-permute-start.6 = (bf16[32,3072]{1,0:T(8,128)(2,1)S(1)}, bf16[32,3072]{1,0:T(8,128)(2,1)S(1)}, u32[]{:S(2)}, u32[]{:S(2)}) collective-permute-start(bf16[32,3072]{1,0:T(8,128)(2,1)S(1)} %add_add_fusion), channel_id=1, source_target_pairs={{0,4},{4,0},{8,12},{12,8},{16,20},{20,16},{24,28},{28,24},{32,36},... | collective-permute-start | bytes 589832 | tf_op jit(solution)/shard_map/ppermute | solution.py:109

commit v14 on v12

--- a/solution.py
+++ b/solution.py
@@ -96,18 +96,20 @@
     )(offset, f_blocks, p_blocks)
 
 
-def summed_over(value, axis):
+def summed_over(value, axis, companion):
     count = lax.axis_size(axis)
     bits = max(1, (count - 1).bit_length())
     rounds = [list(range(b, min(b + 2, bits))) for b in range(1, bits, 2)] + [[0]]
-    for group in rounds:
+    for index, group in enumerate(rounds):
         masks = [
             m for m in range(1, count)
             if all((m >> b) & 1 == 0 for b in range(bits) if b not in group)
         ]
         parts = [lax.ppermute(value, axis, [(i, i ^ m) for i in range(count)]) for m in masks]
         value = sum(parts, value)
-    return value
+        if index == 0:
+            value, companion = lax.optimization_barrier((value, companion))
+    return value, companion
 
 
 def per_device(signal, fir, taps, sources):
@@ -126,7 +128,7 @@
         jnp.bfloat16
     )
     picks = jnp.dot(onehot, signal, preferred_element_type=jnp.float32).astype(jnp.bfloat16)
-    picks = summed_over(picks, "sta")
+    picks, signal = summed_over(picks, "sta", signal)
 
     def filtered_of(rows):
         rows = lax.all_gather(rows, "tm", axis=1, tiled=True)

time: 82.5 us -> 83.6 us (1.013)
  transfers between devices with their start and end apart: 7 -> 7, of which waited for: 3 -> 3; matrix products, arithmetic and copies ran while one was open for 7% -> 8% of each run, Pallas kernels for 0% -> 0%
where the time goes in v14:
time: 83.6 us; the launch traced here: 83.3 us
  blocking collectives  22.5 us (27%)
  Pallas kernels  22.2 us (27%)
  local copies, waits for them, and re-layouts  13.3 us (16%)
  starting transfers between devices  9.1 us (11%)
  waiting for transfers between devices  8.58 us (10%)
  matrix products  4.64 us (6%)
  other arithmetic  2.81 us (3%)
    all_gather x2, blocking collectives, filtered_of(): rows = lax.all_gather(rows, 'tm', axis=1, tiled=True)  22.5 us
    pallas_call x1, Pallas kernels, correlate(): pl.pallas_call(kernel, grid_spec=grid_spec, out_shape=jax.ShapeDtypeStruc...  22.2 us
    ppermute x7, starting transfers between devices, summed_over(): lax.ppermute(value, axis, [(i, i ^ m) for i in range(count)])  9.1 us
    ppermute x7, waiting for transfers between devices, summed_over(): lax.ppermute(value, axis, [(i, i ^ m) for i in range(count)])  8.58 us
    reshape x1, local copies, waits for them, and re-layouts, per_device(): return out.reshape(ROUNDS, bands, count_src, channels, share)  4.56 us
    reshape x1, local copies, waits for them, and re-layouts, per_device(): out = out.reshape(bands, SHIFTS, channels, ROUNDS, count_src, groups)  3.81 us
    dot_general x2, matrix products, filter_in_blocks(): jnp.einsum('nru,btu->bnrt', pieces, banded, preferred_element_type=jnp.fl...  3.47 us
    pad x1, local copies, waits for them, and re-layouts, per_device(): jnp.pad(f_loc, ((0, 0), (f_front, blocks + lag_count // 128 - data_blocks...  2.3 us
  transfers between devices with their start and end apart: 7, of which 3 were waited for; matrix products, arithmetic and copies ran while one was open for 8% of the time, Pallas kernels for 0%

profile of v14, /device:TPU:1, one launch (start us, length us, event | category | flops | bytes accessed | tf_op | source)
XLA Modules:
  0.0 83.3 jit_solution(1083807183614786100)
XLA Ops:
  0.0 0.7 broadcast_subtract_fusion
  0.8 1.2 %convolution_convert_fusion = bf16[32,3072]{1,0:T(8,128)(2,1)S(1)} fusion(bf16[32,3072]{1,0:T(8,128)(2,1)} %param.4, s32[32]{0:T(128)S(1)} %sub.15), kind=kOutput, calls=%fused_computation | convolution fusion | flops 6390784 | bytes 393344 | tf_op jit(solution)/shard_map/dot_general | solution.py:130
  2.0 3.6 %collective-permute-start.2 = (bf16[32,3072]{1,0:T(8,128)(2,1)S(1)}, bf16[32,3072]{1,0:T(8,128)(2,1)S(1)}, u32[]{:S(2)}, u32[]{:S(2)}) collective-permute-start(bf16[32,3072]{1,0:T(8,128)(2,1)S(1)} %convolution_convert_fusion), channel_id=1, source_target_pairs={{0,24},{4,28},{8,16},{12,20},{16,8},{20,12},{24,0},{28,4},{32,56},... | collective-permute-start | bytes 589832 | tf_op jit(solution)/shard_map/ppermute | solution.py:108
  6.3 0.8 select_convert_fusion
  7.2 0.4 tile.5
  7.6 0.6 reshape.33
  8.3 5.8 %collective-permute-done.2 = bf16[32,3072]{1,0:T(8,128)(2,1)S(1)} collective-permute-done((bf16[32,3072]{1,0:T(8,128)(2,1)S(1)}, bf16[32,3072]{1,0:T(8,128)(2,1)S(1)}, u32[]{:S(2)}, u32[]{:S(2)}) %collective-permute-start.2) | collective-permute-done | bytes 196640 | tf_op jit(solution)/shard_map/ppermute | solution.py:108
  14.1 0.8 collective-permute-done
  14.9 3.7 %collective-permute-start.5 = (bf16[32,3072]{1,0:T(8,128)(2,1)S(1)}, bf16[32,3072]{1,0:T(8,128)(2,1)S(1)}, u32[]{:S(2)}, u32[]{:S(2)}) collective-permute-start(bf16[32,3072]{1,0:T(8,128)(2,1)S(1)} %add_add_fusion.1), channel_id=1, source_target_pairs={{0,96},{4,100},{8,104},{12,108},{16,112},{20,116},{24,120},{28,124... | collective-permute-start | bytes 589832 | tf_op jit(solution)/shard_map/ppermute | solution.py:108
  18.7 0.7 collective-permute-start.3
  19.3 12.1 %all_gather.6 = bf16[32,12288]{1,0:T(8,128)(2,1)S(1)} all-gather(bf16[32,3072]{1,0:T(8,128)(2,1)S(1)} %copy-done), channel_id=1, replica_groups=mesh['sta'=32,'tm'=4] {'tm'}, dimensions={1}, use_global_device_ids=true | all-gather | bytes 983040 | tf_op jit(solution)/shard_map/all_gather | solution.py:134
  31.6 0.6 fusion.3
  32.3 0.4 collective-permute-start.6
  32.7 1.7 %convert_bitcast_fusion.1 = bf16[4,96,32,128]{3,2,1,0:T(8,128)(2,1)S(1)} fusion(bf16[96,32,256,1]{2,0,1,3:T(8,128)(2,1)S(1)} %fusion.3, bf16[4,128,159]{2,1,0:T(8,128)(2,1)S(1)} %reshape.33), kind=kOutput, calls=%fused_computation.5 | convolution fusion | flops 806879232 | bytes 4881408 | tf_op jit(solution)/shard_map/nru,btu->bnrt/dot_general | solution.py:41
  34.4 2.3 %pad.23.fw_ref = bf16[4,105,32,128]{3,2,1,0:T(8,128)(2,1)} pad(bf16[4,96,32,128]{3,2,1,0:T(8,128)(2,1)S(1)} %convert_bitcast_fusion.1, bf16[]{:T(256)} %constant.5.clone.1), padding=0_0x2_7x0_0x0_0 | pad | bytes 6586370 | tf_op jit(solution)/shard_map/jit(_pad)/pad | solution.py:145
  36.7 2.0 %collective-permute-done.6 = bf16[32,3072]{1,0:T(8,128)(2,1)S(1)} collective-permute-done((bf16[32,3072]{1,0:T(8,128)(2,1)S(1)}, bf16[32,3072]{1,0:T(8,128)(2,1)S(1)}, u32[]{:S(2)}, u32[]{:S(2)}) %collective-permute-start.6) | collective-permute-done | bytes 196640 | tf_op jit(solution)/shard_map/ppermute | solution.py:108
  38.7 10.4 %all_gather.7 = bf16[32,12288]{1,0:T(8,128)(2,1)S(1)} all-gather(bf16[32,3072]{1,0:T(8,128)(2,1)S(1)} %add.39), channel_id=1, replica_groups=mesh['sta'=32,'tm'=4] {'tm'}, dimensions={1}, use_global_device_ids=true | all-gather | bytes 983040 | tf_op jit(solution)/shard_map/all_gather | solution.py:134
  49.3 0.6 fusion.5
  49.9 1.7 %convert_bitcast_fusion = bf16[4,96,32,128]{3,2,1,0:T(8,128)(2,1)S(1)} fusion(bf16[96,32,256,1]{2,0,1,3:T(8,128)(2,1)S(1)} %fusion.5, bf16[4,128,159]{2,1,0:T(8,128)(2,1)S(1)} %reshape.33), kind=kOutput, calls=%fused_computation.4 | convolution fusion | flops 806879232 | bytes 4881408 | tf_op jit(solution)/shard_map/nru,btu->bnrt/dot_general | solution.py:41
  51.6 0.6 pad.25.pp_ref
  52.2 22.2 %shard_map.46 = bf16[4,512,256]{2,1,0:T(8,128)(2,1)S(1)} custom-call(s32[1]{0:T(128)} %bitcast.off_ref, bf16[4,105,32,128]{3,2,1,0:T(8,128)(2,1)} %pad.23.fw_ref, bf16[4,101,32,128]{3,2,1,0:T(8,128)(2,1)S(1)} %pad.25.pp_ref), custom_call_target="tpu_custom_call" | custom-call | tf_op jit(solution)/shard_map/pallas_call | solution.py:91
  74.4 0.5 copy.10
  75.0 3.8 %reshape.36 = bf16[4,16,32,2,16,8]{2,1,5,4,3,0:T(8,128)(2,1)} reshape(bf16[4,512,256]{1,2,0:T(8,128)(2,1)S(1)} %copy.10) | data formatting | bytes 2097152 | tf_op jit(solution)/shard_map/reshape | solution.py:153
  78.8 4.6 %copy.12 = bf16[2,4,16,32,128]{4,3,2,1,0:T(8,128)(2,1)} copy(bf16[2,4,16,32,128]{3,4,2,0,1:T(8,128)(2,1)} %bitcast.32) | data formatting | bytes 2097152 | tf_op jit(solution)/shard_map/reshape | solution.py:155
  (19 shorter events, 1.4 us)
Async XLA Ops:
  0.0 19.3 %copy-start = (bf16[32,3072]{1,0:T(8,128)(2,1)S(1)}, bf16[32,3072]{1,0:T(8,128)(2,1)}, u32[]{:S(2)}) copy-start(bf16[32,3072]{1,0:T(8,128)(2,1)} %param.4) | copy-start | bytes 589828
  2.0 12.1 %collective-permute-start.2 = (bf16[32,3072]{1,0:T(8,128)(2,1)S(1)}, bf16[32,3072]{1,0:T(8,128)(2,1)S(1)}, u32[]{:S(2)}, u32[]{:S(2)}) collective-permute-start(bf16[32,3072]{1,0:T(8,128)(2,1)S(1)} %convolution_convert_fusion), channel_id=1, source_target_pairs={{0,24},{4,28},{8,16},{12,20},{16,8},{20,12},{24,0},{28,4},{32,56},... | collective-permute-start | bytes 589832 | tf_op jit(solution)/shard_map/ppermute | solution.py:108
  5.6 8.4 %collective-permute-start.1 = (bf16[32,3072]{1,0:T(8,128)(2,1)S(1)}, bf16[32,3072]{1,0:T(8,128)(2,1)S(1)}, u32[]{:S(2)}, u32[]{:S(2)}) collective-permute-start(bf16[32,3072]{1,0:T(8,128)(2,1)S(1)} %convolution_convert_fusion), channel_id=1, source_target_pairs={{0,16},{4,20},{8,24},{12,28},{16,0},{20,4},{24,8},{28,12},{32,48},... | collective-permute-start | bytes 589832 | tf_op jit(solution)/shard_map/ppermute | solution.py:108
  6.0 8.9 %collective-permute-start = (bf16[32,3072]{1,0:T(8,128)(2,1)S(1)}, bf16[32,3072]{1,0:T(8,128)(2,1)S(1)}, u32[]{:S(2)}, u32[]{:S(2)}) collective-permute-start(bf16[32,3072]{1,0:T(8,128)(2,1)S(1)} %convolution_convert_fusion), channel_id=1, source_target_pairs={{0,8},{4,12},{8,0},{12,4},{16,24},{20,28},{24,16},{28,20},{32,40},... | collective-permute-start | bytes 589832 | tf_op jit(solution)/shard_map/ppermute | solution.py:108
  14.9 17.3 %collective-permute-start.5 = (bf16[32,3072]{1,0:T(8,128)(2,1)S(1)}, bf16[32,3072]{1,0:T(8,128)(2,1)S(1)}, u32[]{:S(2)}, u32[]{:S(2)}) collective-permute-start(bf16[32,3072]{1,0:T(8,128)(2,1)S(1)} %add_add_fusion.1), channel_id=1, source_target_pairs={{0,96},{4,100},{8,104},{12,108},{16,112},{20,116},{24,120},{28,124... | collective-permute-start | bytes 589832 | tf_op jit(solution)/shard_map/ppermute | solution.py:108
  18.7 13.6 %collective-permute-start.4 = (bf16[32,3072]{1,0:T(8,128)(2,1)S(1)}, bf16[32,3072]{1,0:T(8,128)(2,1)S(1)}, u32[]{:S(2)}, u32[]{:S(2)}) collective-permute-start(bf16[32,3072]{1,0:T(8,128)(2,1)S(1)} %add_add_fusion.1), channel_id=1, source_target_pairs={{0,64},{4,68},{8,72},{12,76},{16,80},{20,84},{24,88},{28,92},{32,9... | collective-permute-start | bytes 589832 | tf_op jit(solution)/shard_map/ppermute | solution.py:108
  18.7 13.6 %collective-permute-start.3 = (bf16[32,3072]{1,0:T(8,128)(2,1)S(1)}, bf16[32,3072]{1,0:T(8,128)(2,1)S(1)}, u32[]{:S(2)}, u32[]{:S(2)}) collective-permute-start(bf16[32,3072]{1,0:T(8,128)(2,1)S(1)} %add_add_fusion.1), channel_id=1, source_target_pairs={{0,32},{4,36},{8,40},{12,44},{16,48},{20,52},{24,56},{28,60},{32,0... | collective-permute-start | bytes 589832 | tf_op jit(solution)/shard_map/ppermute | solution.py:108
  32.3 6.4 %collective-permute-start.6 = (bf16[32,3072]{1,0:T(8,128)(2,1)S(1)}, bf16[32,3072]{1,0:T(8,128)(2,1)S(1)}, u32[]{:S(2)}, u32[]{:S(2)}) collective-permute-start(bf16[32,3072]{1,0:T(8,128)(2,1)S(1)} %add_add_fusion), channel_id=1, source_target_pairs={{0,4},{4,0},{8,12},{12,8},{16,20},{20,16},{24,28},{28,24},{32,36},... | collective-permute-start | bytes 589832 | tf_op jit(solution)/shard_map/ppermute | solution.py:108

commit v15 on v12

--- a/solution.py
+++ b/solution.py
@@ -99,7 +99,7 @@
 def summed_over(value, axis):
     count = lax.axis_size(axis)
     bits = max(1, (count - 1).bit_length())
-    rounds = [list(range(b, min(b + 2, bits))) for b in range(1, bits, 2)] + [[0]]
+    rounds = [list(range(b, min(b + 2, bits))) for b in range(1, bits, 2)][::-1] + [[0]]
     for group in rounds:
         masks = [
             m for m in range(1, count)

time: 82.5 us -> 82.3 us (level)
  no operation moved by 1% of the time
where the time goes in v15:
time: 82.3 us; the launch traced here: 82.1 us
  blocking collectives  22.5 us (27%)
  Pallas kernels  22.2 us (27%)
  local copies, waits for them, and re-layouts  13.3 us (16%)
  starting transfers between devices  9.19 us (11%)
  waiting for transfers between devices  7.91 us (10%)
  matrix products  4.64 us (6%)
  other arithmetic  2.12 us (3%)
    all_gather x2, blocking collectives, filtered_of(): rows = lax.all_gather(rows, 'tm', axis=1, tiled=True)  22.5 us
    pallas_call x1, Pallas kernels, correlate(): pl.pallas_call(kernel, grid_spec=grid_spec, out_shape=jax.ShapeDtypeStruc...  22.2 us
    ppermute x7, starting transfers between devices, summed_over(): lax.ppermute(value, axis, [(i, i ^ m) for i in range(count)])  9.19 us
    ppermute x7, waiting for transfers between devices, summed_over(): lax.ppermute(value, axis, [(i, i ^ m) for i in range(count)])  7.91 us
    reshape x1, local copies, waits for them, and re-layouts, per_device(): return out.reshape(ROUNDS, bands, count_src, channels, share)  4.56 us
    reshape x1, local copies, waits for them, and re-layouts, per_device(): out = out.reshape(bands, SHIFTS, channels, ROUNDS, count_src, groups)  3.8 us
    dot_general x2, matrix products, filter_in_blocks(): jnp.einsum('nru,btu->bnrt', pieces, banded, preferred_element_type=jnp.fl...  3.47 us
    pad x1, local copies, waits for them, and re-layouts, per_device(): jnp.pad(f_loc, ((0, 0), (f_front, blocks + lag_count // 128 - data_blocks...  2.29 us
  transfers between devices with their start and end apart: 7, of which 3 were waited for; matrix products, arithmetic and copies ran while one was open for 7% of the time, Pallas kernels for 0%

profile of v15, /device:TPU:1, one launch (start us, length us, event | category | flops | bytes accessed | tf_op | source)
XLA Modules:
  0.0 82.1 jit_solution(16012030583457302773)
XLA Ops:
  0.0 0.7 broadcast_subtract_fusion
  0.8 1.2 %convolution_convert_fusion = bf16[32,3072]{1,0:T(8,128)(2,1)S(1)} fusion(bf16[32,3072]{1,0:T(8,128)(2,1)} %param.4, s32[32]{0:T(128)S(1)} %sub.15), kind=kOutput, calls=%fused_computation | convolution fusion | flops 6390784 | bytes 393344 | tf_op jit(solution)/shard_map/dot_general | solution.py:128
  2.0 4.7 %collective-permute-start.2 = (bf16[32,3072]{1,0:T(8,128)(2,1)S(1)}, bf16[32,3072]{1,0:T(8,128)(2,1)S(1)}, u32[]{:S(2)}, u32[]{:S(2)}) collective-permute-start(bf16[32,3072]{1,0:T(8,128)(2,1)S(1)} %convolution_convert_fusion), channel_id=1, source_target_pairs={{0,96},{4,100},{8,104},{12,108},{16,112},{20,116},{24,120},{28,124... | collective-permute-start | bytes 589832 | tf_op jit(solution)/shard_map/ppermute | solution.py:108
  6.6 0.7 collective-permute-start
  7.3 11.4 %all_gather.6 = bf16[32,12288]{1,0:T(8,128)(2,1)S(1)} all-gather(bf16[32,3072]{1,0:T(8,128)(2,1)} %param.4), channel_id=1, replica_groups=mesh['sta'=32,'tm'=4] {'tm'}, dimensions={1}, use_global_device_ids=true | all-gather | bytes 983040 | tf_op jit(solution)/shard_map/all_gather | solution.py:132
  18.8 2.8 %collective-permute-start.5 = (bf16[32,3072]{1,0:T(8,128)(2,1)S(1)}, bf16[32,3072]{1,0:T(8,128)(2,1)S(1)}, u32[]{:S(2)}, u32[]{:S(2)}) collective-permute-start(bf16[32,3072]{1,0:T(8,128)(2,1)S(1)} %add_add_fusion.1), channel_id=1, source_target_pairs={{0,24},{4,28},{8,16},{12,20},{16,8},{20,12},{24,0},{28,4},{32,56},... | collective-permute-start | bytes 589832 | tf_op jit(solution)/shard_map/ppermute | solution.py:108
  21.6 0.3 collective-permute-start.4
  22.5 0.4 tile.5
  22.9 0.6 reshape.33
  23.7 0.6 fusion.3
  24.3 6.1 %collective-permute-done.5 = bf16[32,3072]{1,0:T(8,128)(2,1)S(1)} collective-permute-done((bf16[32,3072]{1,0:T(8,128)(2,1)S(1)}, bf16[32,3072]{1,0:T(8,128)(2,1)S(1)}, u32[]{:S(2)}, u32[]{:S(2)}) %collective-permute-start.5) | collective-permute-done | bytes 196640 | tf_op jit(solution)/shard_map/ppermute | solution.py:108
  30.5 0.8 collective-permute-done.3
  31.3 0.4 collective-permute-start.6
  31.6 1.7 %convert_bitcast_fusion.1 = bf16[4,96,32,128]{3,2,1,0:T(8,128)(2,1)S(1)} fusion(bf16[96,32,256,1]{2,0,1,3:T(8,128)(2,1)S(1)} %fusion.3, bf16[4,128,159]{2,1,0:T(8,128)(2,1)S(1)} %reshape.33), kind=kOutput, calls=%fused_computation.5 | convolution fusion | flops 806879232 | bytes 4881408 | tf_op jit(solution)/shard_map/nru,btu->bnrt/dot_general | solution.py:41
  33.4 2.3 %pad.23.fw_ref = bf16[4,105,32,128]{3,2,1,0:T(8,128)(2,1)} pad(bf16[4,96,32,128]{3,2,1,0:T(8,128)(2,1)S(1)} %convert_bitcast_fusion.1, bf16[]{:T(256)} %constant.5.clone.1), padding=0_0x2_7x0_0x0_0 | pad | bytes 6586370 | tf_op jit(solution)/shard_map/jit(_pad)/pad | solution.py:143
  35.7 1.0 %collective-permute-done.6 = bf16[32,3072]{1,0:T(8,128)(2,1)S(1)} collective-permute-done((bf16[32,3072]{1,0:T(8,128)(2,1)S(1)}, bf16[32,3072]{1,0:T(8,128)(2,1)S(1)}, u32[]{:S(2)}, u32[]{:S(2)}) %collective-permute-start.6) | collective-permute-done | bytes 196640 | tf_op jit(solution)/shard_map/ppermute | solution.py:108
  36.7 11.2 %all_gather.7 = bf16[32,12288]{1,0:T(8,128)(2,1)S(1)} all-gather(bf16[32,3072]{1,0:T(8,128)(2,1)S(1)} %add.39), channel_id=1, replica_groups=mesh['sta'=32,'tm'=4] {'tm'}, dimensions={1}, use_global_device_ids=true | all-gather | bytes 983040 | tf_op jit(solution)/shard_map/all_gather | solution.py:132
  48.0 0.6 fusion.5
  48.6 1.7 %convert_bitcast_fusion = bf16[4,96,32,128]{3,2,1,0:T(8,128)(2,1)S(1)} fusion(bf16[96,32,256,1]{2,0,1,3:T(8,128)(2,1)S(1)} %fusion.5, bf16[4,128,159]{2,1,0:T(8,128)(2,1)S(1)} %reshape.33), kind=kOutput, calls=%fused_computation.4 | convolution fusion | flops 806879232 | bytes 4881408 | tf_op jit(solution)/shard_map/nru,btu->bnrt/dot_general | solution.py:41
  50.4 0.6 pad.25.pp_ref
  50.9 22.2 %shard_map.46 = bf16[4,512,256]{2,1,0:T(8,128)(2,1)S(1)} custom-call(s32[1]{0:T(128)} %bitcast.off_ref, bf16[4,105,32,128]{3,2,1,0:T(8,128)(2,1)} %pad.23.fw_ref, bf16[4,101,32,128]{3,2,1,0:T(8,128)(2,1)S(1)} %pad.25.pp_ref), custom_call_target="tpu_custom_call" | custom-call | tf_op jit(solution)/shard_map/pallas_call | solution.py:91
  73.1 0.5 copy.10
  73.7 3.8 %reshape.36 = bf16[4,16,32,2,16,8]{2,1,5,4,3,0:T(8,128)(2,1)} reshape(bf16[4,512,256]{1,2,0:T(8,128)(2,1)S(1)} %copy.10) | data formatting | bytes 2097152 | tf_op jit(solution)/shard_map/reshape | solution.py:151
  77.5 4.6 %copy.12 = bf16[2,4,16,32,128]{4,3,2,1,0:T(8,128)(2,1)} copy(bf16[2,4,16,32,128]{3,4,2,0,1:T(8,128)(2,1)} %bitcast.32) | data formatting | bytes 2097152 | tf_op jit(solution)/shard_map/reshape | solution.py:153
  (21 shorter events, 1.1 us)
Async XLA Ops:
  0.0 22.3 %copy-start.1 = (s32[4]{0:T(128)S(1)}, s32[4]{0:T(128)}, u32[]{:S(2)}) copy-start(s32[4]{0:T(128)} %param.6) | copy-start | bytes 52
  0.0 22.3 %copy-start = (f32[4,32]{1,0:T(4,128)S(1)}, f32[4,32]{1,0:T(4,128)}, u32[]{:S(2)}) copy-start(f32[4,32]{1,0:T(4,128)} %param.5) | copy-start | bytes 1540
  2.0 16.7 %collective-permute-start.2 = (bf16[32,3072]{1,0:T(8,128)(2,1)S(1)}, bf16[32,3072]{1,0:T(8,128)(2,1)S(1)}, u32[]{:S(2)}, u32[]{:S(2)}) collective-permute-start(bf16[32,3072]{1,0:T(8,128)(2,1)S(1)} %convolution_convert_fusion), channel_id=1, source_target_pairs={{0,96},{4,100},{8,104},{12,108},{16,112},{20,116},{24,120},{28,124... | collective-permute-start | bytes 589832 | tf_op jit(solution)/shard_map/ppermute | solution.py:108
  6.6 12.1 %collective-permute-start.1 = (bf16[32,3072]{1,0:T(8,128)(2,1)S(1)}, bf16[32,3072]{1,0:T(8,128)(2,1)S(1)}, u32[]{:S(2)}, u32[]{:S(2)}) collective-permute-start(bf16[32,3072]{1,0:T(8,128)(2,1)S(1)} %convolution_convert_fusion), channel_id=1, source_target_pairs={{0,64},{4,68},{8,72},{12,76},{16,80},{20,84},{24,88},{28,92},{32,9... | collective-permute-start | bytes 589832 | tf_op jit(solution)/shard_map/ppermute | solution.py:108
  6.6 12.1 %collective-permute-start = (bf16[32,3072]{1,0:T(8,128)(2,1)S(1)}, bf16[32,3072]{1,0:T(8,128)(2,1)S(1)}, u32[]{:S(2)}, u32[]{:S(2)}) collective-permute-start(bf16[32,3072]{1,0:T(8,128)(2,1)S(1)} %convolution_convert_fusion), channel_id=1, source_target_pairs={{0,32},{4,36},{8,40},{12,44},{16,48},{20,52},{24,56},{28,60},{32,0... | collective-permute-start | bytes 589832 | tf_op jit(solution)/shard_map/ppermute | solution.py:108
  18.8 11.7 %collective-permute-start.5 = (bf16[32,3072]{1,0:T(8,128)(2,1)S(1)}, bf16[32,3072]{1,0:T(8,128)(2,1)S(1)}, u32[]{:S(2)}, u32[]{:S(2)}) collective-permute-start(bf16[32,3072]{1,0:T(8,128)(2,1)S(1)} %add_add_fusion.1), channel_id=1, source_target_pairs={{0,24},{4,28},{8,16},{12,20},{16,8},{20,12},{24,0},{28,4},{32,56},... | collective-permute-start | bytes 589832 | tf_op jit(solution)/shard_map/ppermute | solution.py:108
  21.6 8.9 %collective-permute-start.4 = (bf16[32,3072]{1,0:T(8,128)(2,1)S(1)}, bf16[32,3072]{1,0:T(8,128)(2,1)S(1)}, u32[]{:S(2)}, u32[]{:S(2)}) collective-permute-start(bf16[32,3072]{1,0:T(8,128)(2,1)S(1)} %add_add_fusion.1), channel_id=1, source_target_pairs={{0,16},{4,20},{8,24},{12,28},{16,0},{20,4},{24,8},{28,12},{32,48},... | collective-permute-start | bytes 589832 | tf_op jit(solution)/shard_map/ppermute | solution.py:108
  21.9 9.3 %collective-permute-start.3 = (bf16[32,3072]{1,0:T(8,128)(2,1)S(1)}, bf16[32,3072]{1,0:T(8,128)(2,1)S(1)}, u32[]{:S(2)}, u32[]{:S(2)}) collective-permute-start(bf16[32,3072]{1,0:T(8,128)(2,1)S(1)} %add_add_fusion.1), channel_id=1, source_target_pairs={{0,8},{4,12},{8,0},{12,4},{16,24},{20,28},{24,16},{28,20},{32,40},... | collective-permute-start | bytes 589832 | tf_op jit(solution)/shard_map/ppermute | solution.py:108
  31.3 5.4 %collective-permute-start.6 = (bf16[32,3072]{1,0:T(8,128)(2,1)S(1)}, bf16[32,3072]{1,0:T(8,128)(2,1)S(1)}, u32[]{:S(2)}, u32[]{:S(2)}) collective-permute-start(bf16[32,3072]{1,0:T(8,128)(2,1)S(1)} %add_add_fusion), channel_id=1, source_target_pairs={{0,4},{4,0},{8,12},{12,8},{16,20},{20,16},{24,28},{28,24},{32,36},... | collective-permute-start | bytes 589832 | tf_op jit(solution)/shard_map/ppermute | solution.py:108

commit v16 on v15

--- a/solution.py
+++ b/solution.py
@@ -43,25 +43,23 @@
     )
 
 
-def corr_kernel(off_ref, fw_ref, pp_ref, out_ref, acc_ref, *, chunks, groups, scale):
+def corr_kernel(off_ref, fw_ref, pp_ref, out_ref, acc_ref, *, widths, groups, scale):
     acc_ref[...] = jnp.zeros_like(acc_ref)
-    per = CHUNK // 128
     off = off_ref[0]
-
-    def step(k, carry):
-        first = k * per
+    first = 0
+    for width in widths:
+        per = width // 128
         fa = jnp.concatenate([fw_ref[0, off + first + i] for i in range(per + 1)], axis=1)
         pa = jnp.concatenate([pp_ref[0, first + i] for i in range(per + 1)], axis=1)
-        lhs = jnp.concatenate([fa[:, q : q + CHUNK] for q in range(SHIFTS)], axis=0)
+        lhs = jnp.concatenate([fa[:, q : q + width] for q in range(SHIFTS)], axis=0)
         rhs = jnp.concatenate(
-            [pa[:, 128 - g * SHIFTS : 128 - g * SHIFTS + CHUNK] for g in range(groups)], axis=0
+            [pa[:, 128 - g * SHIFTS : 128 - g * SHIFTS + width] for g in range(groups)], axis=0
         )
         acc_ref[...] += lax.dot_general(
             lhs, rhs, (((1,), (1,)), ((), ())), preferred_element_type=jnp.float32
         )
-        return carry
+        first += per
 
-    lax.fori_loop(0, chunks, step, 0, unroll=True)
     rounded = (acc_ref[...] * scale).astype(jnp.bfloat16)
     n = rounded.shape[1]
     rows_p = n // groups
@@ -71,11 +69,13 @@
     out_ref[0] = jnp.dot(rounded, perm, preferred_element_type=jnp.float32).astype(out_ref.dtype)
 
 
-def correlate(offset, f_blocks, p_blocks, lags, chunks, scale):
+def correlate(offset, f_blocks, p_blocks, lags, chunks, scale, span):
     bands, nf, rows_f, _ = f_blocks.shape
     np_, rows_p = p_blocks.shape[1], p_blocks.shape[2]
     groups = lags // SHIFTS
-    kernel = functools.partial(corr_kernel, chunks=chunks, groups=groups, scale=scale)
+    needed = -(-span // 128) * 128
+    widths = tuple([CHUNK] * (chunks - 1) + [needed - (chunks - 1) * CHUNK])
+    kernel = functools.partial(corr_kernel, widths=widths, groups=groups, scale=scale)
     m = SHIFTS * rows_f
     n = groups * rows_p
     grid_spec = pltpu.PrefetchScalarGridSpec(
@@ -146,7 +146,7 @@
     p_blocks = jnp.pad(p_src, ((0, 0), (1, blocks - data_blocks - 1), (0, 0), (0, 0)))
     offset = (lax.axis_index("tm") * (share // 128)).astype(jnp.int32).reshape(1)
 
-    out = correlate(offset, f_blocks, p_blocks, share, chunks, norm_scale)
+    out = correlate(offset, f_blocks, p_blocks, share, chunks, norm_scale, span)
     bands = out.shape[0]
     out = out.reshape(bands, SHIFTS, channels, ROUNDS, count_src, groups)
     out = jnp.transpose(out, (3, 0, 4, 2, 5, 1))

time: 82.3 us -> 82.1 us (level)
  no operation moved by 1% of the time
where the time goes in v16:
time: 82.1 us; the launch traced here: 81.8 us
  blocking collectives  22.5 us (27%)
  Pallas kernels  22 us (27%)
  local copies, waits for them, and re-layouts  13.3 us (16%)
  starting transfers between devices  9.19 us (11%)
  waiting for transfers between devices  7.91 us (10%)
  matrix products  4.64 us (6%)
  other arithmetic  2.12 us (3%)
    all_gather x2, blocking collectives, filtered_of(): rows = lax.all_gather(rows, 'tm', axis=1, tiled=True)  22.5 us
    pallas_call x1, Pallas kernels, correlate(): pl.pallas_call(kernel, grid_spec=grid_spec, out_shape=jax.ShapeDtypeStruc...  22 us
    ppermute x7, starting transfers between devices, summed_over(): lax.ppermute(value, axis, [(i, i ^ m) for i in range(count)])  9.19 us
    ppermute x7, waiting for transfers between devices, summed_over(): lax.ppermute(value, axis, [(i, i ^ m) for i in range(count)])  7.91 us
    reshape x1, local copies, waits for them, and re-layouts, per_device(): return out.reshape(ROUNDS, bands, count_src, channels, share)  4.56 us
    reshape x1, local copies, waits for them, and re-layouts, per_device(): out = out.reshape(bands, SHIFTS, channels, ROUNDS, count_src, groups)  3.8 us
    dot_general x2, matrix products, filter_in_blocks(): jnp.einsum('nru,btu->bnrt', pieces, banded, preferred_element_type=jnp.fl...  3.47 us
    pad x1, local copies, waits for them, and re-layouts, per_device(): jnp.pad(f_loc, ((0, 0), (f_front, blocks + lag_count // 128 - data_blocks...  2.29 us
  transfers between devices with their start and end apart: 7, of which 3 were waited for; matrix products, arithmetic and copies ran while one was open for 7% of the time, Pallas kernels for 0%

profile of v16, /device:TPU:1, one launch (start us, length us, event | category | flops | bytes accessed | tf_op | source)
XLA Modules:
  0.0 81.8 jit_solution(1060514295928009389)
XLA Ops:
  0.0 0.7 broadcast_subtract_fusion
  0.8 1.2 %convolution_convert_fusion = bf16[32,3072]{1,0:T(8,128)(2,1)S(1)} fusion(bf16[32,3072]{1,0:T(8,128)(2,1)} %param.4, s32[32]{0:T(128)S(1)} %sub.15), kind=kOutput, calls=%fused_computation | convolution fusion | flops 6390784 | bytes 393344 | tf_op jit(solution)/shard_map/dot_general | solution.py:128
  2.0 4.7 %collective-permute-start.2 = (bf16[32,3072]{1,0:T(8,128)(2,1)S(1)}, bf16[32,3072]{1,0:T(8,128)(2,1)S(1)}, u32[]{:S(2)}, u32[]{:S(2)}) collective-permute-start(bf16[32,3072]{1,0:T(8,128)(2,1)S(1)} %convolution_convert_fusion), channel_id=1, source_target_pairs={{0,96},{4,100},{8,104},{12,108},{16,112},{20,116},{24,120},{28,124... | collective-permute-start | bytes 589832 | tf_op jit(solution)/shard_map/ppermute | solution.py:108
  6.6 0.7 collective-permute-start
  7.3 11.4 %all_gather.6 = bf16[32,12288]{1,0:T(8,128)(2,1)S(1)} all-gather(bf16[32,3072]{1,0:T(8,128)(2,1)} %param.4), channel_id=1, replica_groups=mesh['sta'=32,'tm'=4] {'tm'}, dimensions={1}, use_global_device_ids=true | all-gather | bytes 983040 | tf_op jit(solution)/shard_map/all_gather | solution.py:132
  18.8 2.8 %collective-permute-start.5 = (bf16[32,3072]{1,0:T(8,128)(2,1)S(1)}, bf16[32,3072]{1,0:T(8,128)(2,1)S(1)}, u32[]{:S(2)}, u32[]{:S(2)}) collective-permute-start(bf16[32,3072]{1,0:T(8,128)(2,1)S(1)} %add_add_fusion.1), channel_id=1, source_target_pairs={{0,24},{4,28},{8,16},{12,20},{16,8},{20,12},{24,0},{28,4},{32,56},... | collective-permute-start | bytes 589832 | tf_op jit(solution)/shard_map/ppermute | solution.py:108
  21.6 0.3 collective-permute-start.4
  22.5 0.4 tile.5
  22.9 0.6 reshape.33
  23.7 0.6 fusion.3
  24.3 6.1 %collective-permute-done.5 = bf16[32,3072]{1,0:T(8,128)(2,1)S(1)} collective-permute-done((bf16[32,3072]{1,0:T(8,128)(2,1)S(1)}, bf16[32,3072]{1,0:T(8,128)(2,1)S(1)}, u32[]{:S(2)}, u32[]{:S(2)}) %collective-permute-start.5) | collective-permute-done | bytes 196640 | tf_op jit(solution)/shard_map/ppermute | solution.py:108
  30.5 0.8 collective-permute-done.3
  31.3 0.4 collective-permute-start.6
  31.6 1.7 %convert_bitcast_fusion.1 = bf16[4,96,32,128]{3,2,1,0:T(8,128)(2,1)S(1)} fusion(bf16[96,32,256,1]{2,0,1,3:T(8,128)(2,1)S(1)} %fusion.3, bf16[4,128,159]{2,1,0:T(8,128)(2,1)S(1)} %reshape.33), kind=kOutput, calls=%fused_computation.5 | convolution fusion | flops 806879232 | bytes 4881408 | tf_op jit(solution)/shard_map/nru,btu->bnrt/dot_general | solution.py:41
  33.4 2.3 %pad.23.fw_ref = bf16[4,105,32,128]{3,2,1,0:T(8,128)(2,1)} pad(bf16[4,96,32,128]{3,2,1,0:T(8,128)(2,1)S(1)} %convert_bitcast_fusion.1, bf16[]{:T(256)} %constant.5.clone.1), padding=0_0x2_7x0_0x0_0 | pad | bytes 6586370 | tf_op jit(solution)/shard_map/jit(_pad)/pad | solution.py:143
  35.7 1.0 %collective-permute-done.6 = bf16[32,3072]{1,0:T(8,128)(2,1)S(1)} collective-permute-done((bf16[32,3072]{1,0:T(8,128)(2,1)S(1)}, bf16[32,3072]{1,0:T(8,128)(2,1)S(1)}, u32[]{:S(2)}, u32[]{:S(2)}) %collective-permute-start.6) | collective-permute-done | bytes 196640 | tf_op jit(solution)/shard_map/ppermute | solution.py:108
  36.7 11.2 %all_gather.7 = bf16[32,12288]{1,0:T(8,128)(2,1)S(1)} all-gather(bf16[32,3072]{1,0:T(8,128)(2,1)S(1)} %add.39), channel_id=1, replica_groups=mesh['sta'=32,'tm'=4] {'tm'}, dimensions={1}, use_global_device_ids=true | all-gather | bytes 983040 | tf_op jit(solution)/shard_map/all_gather | solution.py:132
  48.0 0.6 fusion.5
  48.6 1.7 %convert_bitcast_fusion = bf16[4,96,32,128]{3,2,1,0:T(8,128)(2,1)S(1)} fusion(bf16[96,32,256,1]{2,0,1,3:T(8,128)(2,1)S(1)} %fusion.5, bf16[4,128,159]{2,1,0:T(8,128)(2,1)S(1)} %reshape.33), kind=kOutput, calls=%fused_computation.4 | convolution fusion | flops 806879232 | bytes 4881408 | tf_op jit(solution)/shard_map/nru,btu->bnrt/dot_general | solution.py:41
  50.4 0.6 pad.25.pp_ref
  50.9 22.0 %shard_map.46 = bf16[4,512,256]{2,1,0:T(8,128)(2,1)S(1)} custom-call(s32[1]{0:T(128)} %bitcast.off_ref, bf16[4,105,32,128]{3,2,1,0:T(8,128)(2,1)} %pad.23.fw_ref, bf16[4,101,32,128]{3,2,1,0:T(8,128)(2,1)S(1)} %pad.25.pp_ref), custom_call_target="tpu_custom_call" | custom-call | tf_op jit(solution)/shard_map/pallas_call | solution.py:91
  72.9 0.5 copy.10
  73.5 3.8 %reshape.36 = bf16[4,16,32,2,16,8]{2,1,5,4,3,0:T(8,128)(2,1)} reshape(bf16[4,512,256]{1,2,0:T(8,128)(2,1)S(1)} %copy.10) | data formatting | bytes 2097152 | tf_op jit(solution)/shard_map/reshape | solution.py:151
  77.3 4.6 %copy.12 = bf16[2,4,16,32,128]{4,3,2,1,0:T(8,128)(2,1)} copy(bf16[2,4,16,32,128]{3,4,2,0,1:T(8,128)(2,1)} %bitcast.32) | data formatting | bytes 2097152 | tf_op jit(solution)/shard_map/reshape | solution.py:153
  (21 shorter events, 1.1 us)
Async XLA Ops:
  0.0 22.3 %copy-start.1 = (s32[4]{0:T(128)S(1)}, s32[4]{0:T(128)}, u32[]{:S(2)}) copy-start(s32[4]{0:T(128)} %param.6) | copy-start | bytes 52
  0.0 22.3 %copy-start = (f32[4,32]{1,0:T(4,128)S(1)}, f32[4,32]{1,0:T(4,128)}, u32[]{:S(2)}) copy-start(f32[4,32]{1,0:T(4,128)} %param.5) | copy-start | bytes 1540
  2.0 16.7 %collective-permute-start.2 = (bf16[32,3072]{1,0:T(8,128)(2,1)S(1)}, bf16[32,3072]{1,0:T(8,128)(2,1)S(1)}, u32[]{:S(2)}, u32[]{:S(2)}) collective-permute-start(bf16[32,3072]{1,0:T(8,128)(2,1)S(1)} %convolution_convert_fusion), channel_id=1, source_target_pairs={{0,96},{4,100},{8,104},{12,108},{16,112},{20,116},{24,120},{28,124... | collective-permute-start | bytes 589832 | tf_op jit(solution)/shard_map/ppermute | solution.py:108
  6.6 12.1 %collective-permute-start.1 = (bf16[32,3072]{1,0:T(8,128)(2,1)S(1)}, bf16[32,3072]{1,0:T(8,128)(2,1)S(1)}, u32[]{:S(2)}, u32[]{:S(2)}) collective-permute-start(bf16[32,3072]{1,0:T(8,128)(2,1)S(1)} %convolution_convert_fusion), channel_id=1, source_target_pairs={{0,64},{4,68},{8,72},{12,76},{16,80},{20,84},{24,88},{28,92},{32,9... | collective-permute-start | bytes 589832 | tf_op jit(solution)/shard_map/ppermute | solution.py:108
  6.6 12.1 %collective-permute-start = (bf16[32,3072]{1,0:T(8,128)(2,1)S(1)}, bf16[32,3072]{1,0:T(8,128)(2,1)S(1)}, u32[]{:S(2)}, u32[]{:S(2)}) collective-permute-start(bf16[32,3072]{1,0:T(8,128)(2,1)S(1)} %convolution_convert_fusion), channel_id=1, source_target_pairs={{0,32},{4,36},{8,40},{12,44},{16,48},{20,52},{24,56},{28,60},{32,0... | collective-permute-start | bytes 589832 | tf_op jit(solution)/shard_map/ppermute | solution.py:108
  18.8 11.7 %collective-permute-start.5 = (bf16[32,3072]{1,0:T(8,128)(2,1)S(1)}, bf16[32,3072]{1,0:T(8,128)(2,1)S(1)}, u32[]{:S(2)}, u32[]{:S(2)}) collective-permute-start(bf16[32,3072]{1,0:T(8,128)(2,1)S(1)} %add_add_fusion.1), channel_id=1, source_target_pairs={{0,24},{4,28},{8,16},{12,20},{16,8},{20,12},{24,0},{28,4},{32,56},... | collective-permute-start | bytes 589832 | tf_op jit(solution)/shard_map/ppermute | solution.py:108
  21.6 8.9 %collective-permute-start.4 = (bf16[32,3072]{1,0:T(8,128)(2,1)S(1)}, bf16[32,3072]{1,0:T(8,128)(2,1)S(1)}, u32[]{:S(2)}, u32[]{:S(2)}) collective-permute-start(bf16[32,3072]{1,0:T(8,128)(2,1)S(1)} %add_add_fusion.1), channel_id=1, source_target_pairs={{0,16},{4,20},{8,24},{12,28},{16,0},{20,4},{24,8},{28,12},{32,48},... | collective-permute-start | bytes 589832 | tf_op jit(solution)/shard_map/ppermute | solution.py:108
  21.9 9.3 %collective-permute-start.3 = (bf16[32,3072]{1,0:T(8,128)(2,1)S(1)}, bf16[32,3072]{1,0:T(8,128)(2,1)S(1)}, u32[]{:S(2)}, u32[]{:S(2)}) collective-permute-start(bf16[32,3072]{1,0:T(8,128)(2,1)S(1)} %add_add_fusion.1), channel_id=1, source_target_pairs={{0,8},{4,12},{8,0},{12,4},{16,24},{20,28},{24,16},{28,20},{32,40},... | collective-permute-start | bytes 589832 | tf_op jit(solution)/shard_map/ppermute | solution.py:108
  31.3 5.4 %collective-permute-start.6 = (bf16[32,3072]{1,0:T(8,128)(2,1)S(1)}, bf16[32,3072]{1,0:T(8,128)(2,1)S(1)}, u32[]{:S(2)}, u32[]{:S(2)}) collective-permute-start(bf16[32,3072]{1,0:T(8,128)(2,1)S(1)} %add_add_fusion), channel_id=1, source_target_pairs={{0,4},{4,0},{8,12},{12,8},{16,20},{20,16},{24,28},{28,24},{32,36},... | collective-permute-start | bytes 589832 | tf_op jit(solution)/shard_map/ppermute | solution.py:108

commit v17 on v16

--- a/solution.py
+++ b/solution.py
@@ -10,7 +10,7 @@
 ROUNDS = 2
 MAXLAG = 256
 SHIFTS = 16
-CHUNK = 2560
+CHUNK = 3200
 
 
 def skew(values, count_rows):
@@ -73,8 +73,9 @@
     bands, nf, rows_f, _ = f_blocks.shape
     np_, rows_p = p_blocks.shape[1], p_blocks.shape[2]
     groups = lags // SHIFTS
-    needed = -(-span // 128) * 128
-    widths = tuple([CHUNK] * (chunks - 1) + [needed - (chunks - 1) * CHUNK])
+    needed = -(-span // 128)
+    base, extra = divmod(needed, chunks)
+    widths = tuple((base + (i >= chunks - extra)) * 128 for i in range(chunks))
     kernel = functools.partial(corr_kernel, widths=widths, groups=groups, scale=scale)
     m = SHIFTS * rows_f
     n = groups * rows_p

time: 82.1 us -> 82 us (level)
  no operation moved by 1% of the time
where the time goes in v17:
time: 82 us; the launch traced here: 81.8 us
  blocking collectives  22.5 us (27%)
  Pallas kernels  21.9 us (27%)
  local copies, waits for them, and re-layouts  13.3 us (16%)
  starting transfers between devices  9.19 us (11%)
  waiting for transfers between devices  7.91 us (10%)
  matrix products  4.64 us (6%)
  other arithmetic  2.12 us (3%)
    all_gather x2, blocking collectives, filtered_of(): rows = lax.all_gather(rows, 'tm', axis=1, tiled=True)  22.5 us
    pallas_call x1, Pallas kernels, correlate(): pl.pallas_call(kernel, grid_spec=grid_spec, out_shape=jax.ShapeDtypeStruc...  21.9 us
    ppermute x7, starting transfers between devices, summed_over(): lax.ppermute(value, axis, [(i, i ^ m) for i in range(count)])  9.19 us
    ppermute x7, waiting for transfers between devices, summed_over(): lax.ppermute(value, axis, [(i, i ^ m) for i in range(count)])  7.91 us
    reshape x1, local copies, waits for them, and re-layouts, per_device(): return out.reshape(ROUNDS, bands, count_src, channels, share)  4.56 us
    reshape x1, local copies, waits for them, and re-layouts, per_device(): out = out.reshape(bands, SHIFTS, channels, ROUNDS, count_src, groups)  3.8 us
    dot_general x2, matrix products, filter_in_blocks(): jnp.einsum('nru,btu->bnrt', pieces, banded, preferred_element_type=jnp.fl...  3.47 us
    pad x1, local copies, waits for them, and re-layouts, per_device(): jnp.pad(f_loc, ((0, 0), (f_front, blocks + lag_count // 128 - data_blocks...  2.29 us
  transfers between devices with their start and end apart: 7, of which 3 were waited for; matrix products, arithmetic and copies ran while one was open for 7% of the time, Pallas kernels for 0%

profile of v17, /device:TPU:1, one launch (start us, length us, event | category | flops | bytes accessed | tf_op | source)
XLA Modules:
  0.0 81.8 jit_solution(11177154302236093911)
XLA Ops:
  0.0 0.7 broadcast_subtract_fusion
  0.8 1.2 %convolution_convert_fusion = bf16[32,3072]{1,0:T(8,128)(2,1)S(1)} fusion(bf16[32,3072]{1,0:T(8,128)(2,1)} %param.4, s32[32]{0:T(128)S(1)} %sub.15), kind=kOutput, calls=%fused_computation | convolution fusion | flops 6390784 | bytes 393344 | tf_op jit(solution)/shard_map/dot_general | solution.py:129
  2.0 4.7 %collective-permute-start.2 = (bf16[32,3072]{1,0:T(8,128)(2,1)S(1)}, bf16[32,3072]{1,0:T(8,128)(2,1)S(1)}, u32[]{:S(2)}, u32[]{:S(2)}) collective-permute-start(bf16[32,3072]{1,0:T(8,128)(2,1)S(1)} %convolution_convert_fusion), channel_id=1, source_target_pairs={{0,96},{4,100},{8,104},{12,108},{16,112},{20,116},{24,120},{28,124... | collective-permute-start | bytes 589832 | tf_op jit(solution)/shard_map/ppermute | solution.py:109
  6.6 0.7 collective-permute-start
  7.3 11.4 %all_gather.6 = bf16[32,12288]{1,0:T(8,128)(2,1)S(1)} all-gather(bf16[32,3072]{1,0:T(8,128)(2,1)} %param.4), channel_id=1, replica_groups=mesh['sta'=32,'tm'=4] {'tm'}, dimensions={1}, use_global_device_ids=true | all-gather | bytes 983040 | tf_op jit(solution)/shard_map/all_gather | solution.py:133
  18.8 2.8 %collective-permute-start.5 = (bf16[32,3072]{1,0:T(8,128)(2,1)S(1)}, bf16[32,3072]{1,0:T(8,128)(2,1)S(1)}, u32[]{:S(2)}, u32[]{:S(2)}) collective-permute-start(bf16[32,3072]{1,0:T(8,128)(2,1)S(1)} %add_add_fusion.1), channel_id=1, source_target_pairs={{0,24},{4,28},{8,16},{12,20},{16,8},{20,12},{24,0},{28,4},{32,56},... | collective-permute-start | bytes 589832 | tf_op jit(solution)/shard_map/ppermute | solution.py:109
  21.6 0.3 collective-permute-start.4
  22.5 0.4 tile.5
  22.9 0.6 reshape.33
  23.7 0.6 fusion.3
  24.3 6.1 %collective-permute-done.5 = bf16[32,3072]{1,0:T(8,128)(2,1)S(1)} collective-permute-done((bf16[32,3072]{1,0:T(8,128)(2,1)S(1)}, bf16[32,3072]{1,0:T(8,128)(2,1)S(1)}, u32[]{:S(2)}, u32[]{:S(2)}) %collective-permute-start.5) | collective-permute-done | bytes 196640 | tf_op jit(solution)/shard_map/ppermute | solution.py:109
  30.5 0.8 collective-permute-done.3
  31.3 0.4 collective-permute-start.6
  31.6 1.7 %convert_bitcast_fusion.1 = bf16[4,96,32,128]{3,2,1,0:T(8,128)(2,1)S(1)} fusion(bf16[96,32,256,1]{2,0,1,3:T(8,128)(2,1)S(1)} %fusion.3, bf16[4,128,159]{2,1,0:T(8,128)(2,1)S(1)} %reshape.33), kind=kOutput, calls=%fused_computation.5 | convolution fusion | flops 806879232 | bytes 4881408 | tf_op jit(solution)/shard_map/nru,btu->bnrt/dot_general | solution.py:41
  33.4 2.3 %pad.23.fw_ref = bf16[4,105,32,128]{3,2,1,0:T(8,128)(2,1)} pad(bf16[4,96,32,128]{3,2,1,0:T(8,128)(2,1)S(1)} %convert_bitcast_fusion.1, bf16[]{:T(256)} %constant.5.clone.1), padding=0_0x2_7x0_0x0_0 | pad | bytes 6586370 | tf_op jit(solution)/shard_map/jit(_pad)/pad | solution.py:144
  35.7 1.0 %collective-permute-done.6 = bf16[32,3072]{1,0:T(8,128)(2,1)S(1)} collective-permute-done((bf16[32,3072]{1,0:T(8,128)(2,1)S(1)}, bf16[32,3072]{1,0:T(8,128)(2,1)S(1)}, u32[]{:S(2)}, u32[]{:S(2)}) %collective-permute-start.6) | collective-permute-done | bytes 196640 | tf_op jit(solution)/shard_map/ppermute | solution.py:109
  36.7 11.2 %all_gather.7 = bf16[32,12288]{1,0:T(8,128)(2,1)S(1)} all-gather(bf16[32,3072]{1,0:T(8,128)(2,1)S(1)} %add.39), channel_id=1, replica_groups=mesh['sta'=32,'tm'=4] {'tm'}, dimensions={1}, use_global_device_ids=true | all-gather | bytes 983040 | tf_op jit(solution)/shard_map/all_gather | solution.py:133
  48.0 0.6 fusion.5
  48.6 1.7 %convert_bitcast_fusion = bf16[4,96,32,128]{3,2,1,0:T(8,128)(2,1)S(1)} fusion(bf16[96,32,256,1]{2,0,1,3:T(8,128)(2,1)S(1)} %fusion.5, bf16[4,128,159]{2,1,0:T(8,128)(2,1)S(1)} %reshape.33), kind=kOutput, calls=%fused_computation.4 | convolution fusion | flops 806879232 | bytes 4881408 | tf_op jit(solution)/shard_map/nru,btu->bnrt/dot_general | solution.py:41
  50.4 0.6 pad.25.pp_ref
  50.9 21.9 %shard_map.46 = bf16[4,512,256]{2,1,0:T(8,128)(2,1)S(1)} custom-call(s32[1]{0:T(128)} %bitcast.off_ref, bf16[4,105,32,128]{3,2,1,0:T(8,128)(2,1)} %pad.23.fw_ref, bf16[4,101,32,128]{3,2,1,0:T(8,128)(2,1)S(1)} %pad.25.pp_ref), custom_call_target="tpu_custom_call" | custom-call | tf_op jit(solution)/shard_map/pallas_call | solution.py:92
  72.9 0.5 copy.10
  73.4 3.8 %reshape.36 = bf16[4,16,32,2,16,8]{2,1,5,4,3,0:T(8,128)(2,1)} reshape(bf16[4,512,256]{1,2,0:T(8,128)(2,1)S(1)} %copy.10) | data formatting | bytes 2097152 | tf_op jit(solution)/shard_map/reshape | solution.py:152
  77.2 4.6 %copy.12 = bf16[2,4,16,32,128]{4,3,2,1,0:T(8,128)(2,1)} copy(bf16[2,4,16,32,128]{3,4,2,0,1:T(8,128)(2,1)} %bitcast.32) | data formatting | bytes 2097152 | tf_op jit(solution)/shard_map/reshape | solution.py:154
  (21 shorter events, 1.1 us)
Async XLA Ops:
  0.0 22.3 %copy-start.1 = (s32[4]{0:T(128)S(1)}, s32[4]{0:T(128)}, u32[]{:S(2)}) copy-start(s32[4]{0:T(128)} %param.6) | copy-start | bytes 52
  0.0 22.3 %copy-start = (f32[4,32]{1,0:T(4,128)S(1)}, f32[4,32]{1,0:T(4,128)}, u32[]{:S(2)}) copy-start(f32[4,32]{1,0:T(4,128)} %param.5) | copy-start | bytes 1540
  2.0 16.7 %collective-permute-start.2 = (bf16[32,3072]{1,0:T(8,128)(2,1)S(1)}, bf16[32,3072]{1,0:T(8,128)(2,1)S(1)}, u32[]{:S(2)}, u32[]{:S(2)}) collective-permute-start(bf16[32,3072]{1,0:T(8,128)(2,1)S(1)} %convolution_convert_fusion), channel_id=1, source_target_pairs={{0,96},{4,100},{8,104},{12,108},{16,112},{20,116},{24,120},{28,124... | collective-permute-start | bytes 589832 | tf_op jit(solution)/shard_map/ppermute | solution.py:109
  6.6 12.1 %collective-permute-start.1 = (bf16[32,3072]{1,0:T(8,128)(2,1)S(1)}, bf16[32,3072]{1,0:T(8,128)(2,1)S(1)}, u32[]{:S(2)}, u32[]{:S(2)}) collective-permute-start(bf16[32,3072]{1,0:T(8,128)(2,1)S(1)} %convolution_convert_fusion), channel_id=1, source_target_pairs={{0,64},{4,68},{8,72},{12,76},{16,80},{20,84},{24,88},{28,92},{32,9... | collective-permute-start | bytes 589832 | tf_op jit(solution)/shard_map/ppermute | solution.py:109
  6.6 12.1 %collective-permute-start = (bf16[32,3072]{1,0:T(8,128)(2,1)S(1)}, bf16[32,3072]{1,0:T(8,128)(2,1)S(1)}, u32[]{:S(2)}, u32[]{:S(2)}) collective-permute-start(bf16[32,3072]{1,0:T(8,128)(2,1)S(1)} %convolution_convert_fusion), channel_id=1, source_target_pairs={{0,32},{4,36},{8,40},{12,44},{16,48},{20,52},{24,56},{28,60},{32,0... | collective-permute-start | bytes 589832 | tf_op jit(solution)/shard_map/ppermute | solution.py:109
  18.8 11.7 %collective-permute-start.5 = (bf16[32,3072]{1,0:T(8,128)(2,1)S(1)}, bf16[32,3072]{1,0:T(8,128)(2,1)S(1)}, u32[]{:S(2)}, u32[]{:S(2)}) collective-permute-start(bf16[32,3072]{1,0:T(8,128)(2,1)S(1)} %add_add_fusion.1), channel_id=1, source_target_pairs={{0,24},{4,28},{8,16},{12,20},{16,8},{20,12},{24,0},{28,4},{32,56},... | collective-permute-start | bytes 589832 | tf_op jit(solution)/shard_map/ppermute | solution.py:109
  21.6 8.9 %collective-permute-start.4 = (bf16[32,3072]{1,0:T(8,128)(2,1)S(1)}, bf16[32,3072]{1,0:T(8,128)(2,1)S(1)}, u32[]{:S(2)}, u32[]{:S(2)}) collective-permute-start(bf16[32,3072]{1,0:T(8,128)(2,1)S(1)} %add_add_fusion.1), channel_id=1, source_target_pairs={{0,16},{4,20},{8,24},{12,28},{16,0},{20,4},{24,8},{28,12},{32,48},... | collective-permute-start | bytes 589832 | tf_op jit(solution)/shard_map/ppermute | solution.py:109
  21.9 9.3 %collective-permute-start.3 = (bf16[32,3072]{1,0:T(8,128)(2,1)S(1)}, bf16[32,3072]{1,0:T(8,128)(2,1)S(1)}, u32[]{:S(2)}, u32[]{:S(2)}) collective-permute-start(bf16[32,3072]{1,0:T(8,128)(2,1)S(1)} %add_add_fusion.1), channel_id=1, source_target_pairs={{0,8},{4,12},{8,0},{12,4},{16,24},{20,28},{24,16},{28,20},{32,40},... | collective-permute-start | bytes 589832 | tf_op jit(solution)/shard_map/ppermute | solution.py:109
  31.3 5.4 %collective-permute-start.6 = (bf16[32,3072]{1,0:T(8,128)(2,1)S(1)}, bf16[32,3072]{1,0:T(8,128)(2,1)S(1)}, u32[]{:S(2)}, u32[]{:S(2)}) collective-permute-start(bf16[32,3072]{1,0:T(8,128)(2,1)S(1)} %add_add_fusion), channel_id=1, source_target_pairs={{0,4},{4,0},{8,12},{12,8},{16,20},{20,16},{24,28},{28,24},{32,36},... | collective-permute-start | bytes 589832 | tf_op jit(solution)/shard_map/ppermute | solution.py:109

commit v18 on v17

--- a/solution.py
+++ b/solution.py
@@ -11,6 +11,7 @@
 MAXLAG = 256
 SHIFTS = 16
 CHUNK = 3200
+PAIR = 2
 
 
 def skew(values, count_rows):
@@ -44,29 +45,31 @@
 
 
 def corr_kernel(off_ref, fw_ref, pp_ref, out_ref, acc_ref, *, widths, groups, scale):
-    acc_ref[...] = jnp.zeros_like(acc_ref)
     off = off_ref[0]
-    first = 0
-    for width in widths:
-        per = width // 128
-        fa = jnp.concatenate([fw_ref[0, off + first + i] for i in range(per + 1)], axis=1)
-        pa = jnp.concatenate([pp_ref[0, first + i] for i in range(per + 1)], axis=1)
-        lhs = jnp.concatenate([fa[:, q : q + width] for q in range(SHIFTS)], axis=0)
-        rhs = jnp.concatenate(
-            [pa[:, 128 - g * SHIFTS : 128 - g * SHIFTS + width] for g in range(groups)], axis=0
-        )
-        acc_ref[...] += lax.dot_general(
-            lhs, rhs, (((1,), (1,)), ((), ())), preferred_element_type=jnp.float32
-        )
-        first += per
-
-    rounded = (acc_ref[...] * scale).astype(jnp.bfloat16)
-    n = rounded.shape[1]
+    n = acc_ref.shape[2]
     rows_p = n // groups
     src = lax.broadcasted_iota(jnp.int32, (n, n), 0)
     dst = lax.broadcasted_iota(jnp.int32, (n, n), 1)
     perm = ((src % rows_p) * groups + src // rows_p == dst).astype(jnp.bfloat16)
-    out_ref[0] = jnp.dot(rounded, perm, preferred_element_type=jnp.float32).astype(out_ref.dtype)
+    for band in range(acc_ref.shape[0]):
+        acc_ref[band] = jnp.zeros(acc_ref.shape[1:], acc_ref.dtype)
+        first = 0
+        for width in widths:
+            per = width // 128
+            fa = jnp.concatenate([fw_ref[band, off + first + i] for i in range(per + 1)], axis=1)
+            pa = jnp.concatenate([pp_ref[band, first + i] for i in range(per + 1)], axis=1)
+            lhs = jnp.concatenate([fa[:, q : q + width] for q in range(SHIFTS)], axis=0)
+            rhs = jnp.concatenate(
+                [pa[:, 128 - g * SHIFTS : 128 - g * SHIFTS + width] for g in range(groups)], axis=0
+            )
+            acc_ref[band] += lax.dot_general(
+                lhs, rhs, (((1,), (1,)), ((), ())), preferred_element_type=jnp.float32
+            )
+            first += per
+        rounded = (acc_ref[band] * scale).astype(jnp.bfloat16)
+        out_ref[band] = jnp.dot(rounded, perm, preferred_element_type=jnp.float32).astype(
+            out_ref.dtype
+        )
 
 
 def correlate(offset, f_blocks, p_blocks, lags, chunks, scale, span):
@@ -81,13 +84,13 @@
     n = groups * rows_p
     grid_spec = pltpu.PrefetchScalarGridSpec(
         num_scalar_prefetch=1,
-        grid=(bands,),
+        grid=(bands // PAIR,),
         in_specs=[
-            pl.BlockSpec((1, nf, rows_f, 128), lambda b, o: (b, 0, 0, 0)),
-            pl.BlockSpec((1, np_, rows_p, 128), lambda b, o: (b, 0, 0, 0)),
+            pl.BlockSpec((PAIR, nf, rows_f, 128), lambda b, o: (b, 0, 0, 0)),
+            pl.BlockSpec((PAIR, np_, rows_p, 128), lambda b, o: (b, 0, 0, 0)),
         ],
-        out_specs=pl.BlockSpec((1, m, n), lambda b, o: (b, 0, 0)),
-        scratch_shapes=[pltpu.VMEM((m, n), jnp.float32)],
+        out_specs=pl.BlockSpec((PAIR, m, n), lambda b, o: (b, 0, 0)),
+        scratch_shapes=[pltpu.VMEM((PAIR, m, n), jnp.float32)],
     )
     return pl.pallas_call(
         kernel,

time: 82 us -> 89 us (1.085)
  Pallas kernels: 21.9 us -> 29.1 us
    pallas_call x1, Pallas kernels: 21.9 us -> 29.1 us  [correlate(): pl.pallas_call(kernel, grid_spec=grid_spec, out_shape=jax.ShapeDtypeStruc...]
where the time goes in v18:
time: 89 us; the launch traced here: 88.8 us
  Pallas kernels  29.1 us (33%)
  blocking collectives  22.4 us (25%)
  local copies, waits for them, and re-layouts  13.3 us (15%)
  starting transfers between devices  9.19 us (10%)
  waiting for transfers between devices  7.91 us (9%)
  matrix products  4.63 us (5%)
  other arithmetic  2.12 us (2%)
    pallas_call x1, Pallas kernels, correlate(): pl.pallas_call(kernel, grid_spec=grid_spec, out_shape=jax.ShapeDtypeStruc...  29.1 us
    all_gather x2, blocking collectives, filtered_of(): rows = lax.all_gather(rows, 'tm', axis=1, tiled=True)  22.4 us
    ppermute x7, starting transfers between devices, summed_over(): lax.ppermute(value, axis, [(i, i ^ m) for i in range(count)])  9.19 us
    ppermute x7, waiting for transfers between devices, summed_over(): lax.ppermute(value, axis, [(i, i ^ m) for i in range(count)])  7.91 us
    reshape x1, local copies, waits for them, and re-layouts, per_device(): return out.reshape(ROUNDS, bands, count_src, channels, share)  4.56 us
    reshape x1, local copies, waits for them, and re-layouts, per_device(): out = out.reshape(bands, SHIFTS, channels, ROUNDS, count_src, groups)  3.8 us
    dot_general x2, matrix products, filter_in_blocks(): jnp.einsum('nru,btu->bnrt', pieces, banded, preferred_element_type=jnp.fl...  3.47 us
    pad x1, local copies, waits for them, and re-layouts, per_device(): jnp.pad(f_loc, ((0, 0), (f_front, blocks + lag_count // 128 - data_blocks...  2.29 us
  transfers between devices with their start and end apart: 7, of which 3 were waited for; matrix products, arithmetic and copies ran while one was open for 7% of the time, Pallas kernels for 0%

profile of v18, /device:TPU:1, one launch (start us, length us, event | category | flops | bytes accessed | tf_op | source)
XLA Modules:
  0.0 88.8 jit_solution(16055139461519482824)
XLA Ops:
  0.0 0.7 broadcast_subtract_fusion
  0.8 1.2 %convolution_convert_fusion = bf16[32,3072]{1,0:T(8,128)(2,1)S(1)} fusion(bf16[32,3072]{1,0:T(8,128)(2,1)} %param.4, s32[32]{0:T(128)S(1)} %sub.15), kind=kOutput, calls=%fused_computation | convolution fusion | flops 6390784 | bytes 393344 | tf_op jit(solution)/shard_map/dot_general | solution.py:132
  2.0 4.7 %collective-permute-start.2 = (bf16[32,3072]{1,0:T(8,128)(2,1)S(1)}, bf16[32,3072]{1,0:T(8,128)(2,1)S(1)}, u32[]{:S(2)}, u32[]{:S(2)}) collective-permute-start(bf16[32,3072]{1,0:T(8,128)(2,1)S(1)} %convolution_convert_fusion), channel_id=1, source_target_pairs={{0,96},{4,100},{8,104},{12,108},{16,112},{20,116},{24,120},{28,124... | collective-permute-start | bytes 589832 | tf_op jit(solution)/shard_map/ppermute | solution.py:112
  6.6 0.7 collective-permute-start
  7.3 11.4 %all_gather.6 = bf16[32,12288]{1,0:T(8,128)(2,1)S(1)} all-gather(bf16[32,3072]{1,0:T(8,128)(2,1)} %param.4), channel_id=1, replica_groups=mesh['sta'=32,'tm'=4] {'tm'}, dimensions={1}, use_global_device_ids=true | all-gather | bytes 983040 | tf_op jit(solution)/shard_map/all_gather | solution.py:136
  18.8 2.8 %collective-permute-start.5 = (bf16[32,3072]{1,0:T(8,128)(2,1)S(1)}, bf16[32,3072]{1,0:T(8,128)(2,1)S(1)}, u32[]{:S(2)}, u32[]{:S(2)}) collective-permute-start(bf16[32,3072]{1,0:T(8,128)(2,1)S(1)} %add_add_fusion.1), channel_id=1, source_target_pairs={{0,24},{4,28},{8,16},{12,20},{16,8},{20,12},{24,0},{28,4},{32,56},... | collective-permute-start | bytes 589832 | tf_op jit(solution)/shard_map/ppermute | solution.py:112
  21.6 0.3 collective-permute-start.4
  22.5 0.4 tile.5
  22.9 0.6 reshape.33
  23.7 0.6 fusion.3
  24.3 6.1 %collective-permute-done.5 = bf16[32,3072]{1,0:T(8,128)(2,1)S(1)} collective-permute-done((bf16[32,3072]{1,0:T(8,128)(2,1)S(1)}, bf16[32,3072]{1,0:T(8,128)(2,1)S(1)}, u32[]{:S(2)}, u32[]{:S(2)}) %collective-permute-start.5) | collective-permute-done | bytes 196640 | tf_op jit(solution)/shard_map/ppermute | solution.py:112
  30.5 0.8 collective-permute-done.3
  31.3 0.4 collective-permute-start.6
  31.6 1.7 %convert_bitcast_fusion.1 = bf16[4,96,32,128]{3,2,1,0:T(8,128)(2,1)S(1)} fusion(bf16[96,32,256,1]{2,0,1,3:T(8,128)(2,1)S(1)} %fusion.3, bf16[4,128,159]{2,1,0:T(8,128)(2,1)S(1)} %reshape.33), kind=kOutput, calls=%fused_computation.5 | convolution fusion | flops 806879232 | bytes 4881408 | tf_op jit(solution)/shard_map/nru,btu->bnrt/dot_general | solution.py:42
  33.4 2.3 %pad.23.fw_ref = bf16[4,105,32,128]{3,2,1,0:T(8,128)(2,1)} pad(bf16[4,96,32,128]{3,2,1,0:T(8,128)(2,1)S(1)} %convert_bitcast_fusion.1, bf16[]{:T(256)} %constant.5.clone.1), padding=0_0x2_7x0_0x0_0 | pad | bytes 6586370 | tf_op jit(solution)/shard_map/jit(_pad)/pad | solution.py:147
  35.7 1.0 %collective-permute-done.6 = bf16[32,3072]{1,0:T(8,128)(2,1)S(1)} collective-permute-done((bf16[32,3072]{1,0:T(8,128)(2,1)S(1)}, bf16[32,3072]{1,0:T(8,128)(2,1)S(1)}, u32[]{:S(2)}, u32[]{:S(2)}) %collective-permute-start.6) | collective-permute-done | bytes 196640 | tf_op jit(solution)/shard_map/ppermute | solution.py:112
  36.7 11.0 %all_gather.7 = bf16[32,12288]{1,0:T(8,128)(2,1)S(1)} all-gather(bf16[32,3072]{1,0:T(8,128)(2,1)S(1)} %add.39), channel_id=1, replica_groups=mesh['sta'=32,'tm'=4] {'tm'}, dimensions={1}, use_global_device_ids=true | all-gather | bytes 983040 | tf_op jit(solution)/shard_map/all_gather | solution.py:136
  47.8 0.6 fusion.5
  48.4 1.7 %convert_bitcast_fusion = bf16[4,96,32,128]{3,2,1,0:T(8,128)(2,1)S(1)} fusion(bf16[96,32,256,1]{2,0,1,3:T(8,128)(2,1)S(1)} %fusion.5, bf16[4,128,159]{2,1,0:T(8,128)(2,1)S(1)} %reshape.33), kind=kOutput, calls=%fused_computation.4 | convolution fusion | flops 806879232 | bytes 4881408 | tf_op jit(solution)/shard_map/nru,btu->bnrt/dot_general | solution.py:42
  50.2 0.6 pad.25.pp_ref
  50.7 29.1 %shard_map.46 = bf16[4,512,256]{2,1,0:T(8,128)(2,1)S(1)} custom-call(s32[1]{0:T(128)} %bitcast.off_ref, bf16[4,105,32,128]{3,2,1,0:T(8,128)(2,1)} %pad.23.fw_ref, bf16[4,101,32,128]{3,2,1,0:T(8,128)(2,1)S(1)} %pad.25.pp_ref), custom_call_target="tpu_custom_call" | custom-call | tf_op jit(solution)/shard_map/pallas_call | solution.py:95
  79.9 0.5 copy.10
  80.4 3.8 %reshape.36 = bf16[4,16,32,2,16,8]{2,1,5,4,3,0:T(8,128)(2,1)} reshape(bf16[4,512,256]{1,2,0:T(8,128)(2,1)S(1)} %copy.10) | data formatting | bytes 2097152 | tf_op jit(solution)/shard_map/reshape | solution.py:155
  84.2 4.6 %copy.12 = bf16[2,4,16,32,128]{4,3,2,1,0:T(8,128)(2,1)} copy(bf16[2,4,16,32,128]{3,4,2,0,1:T(8,128)(2,1)} %bitcast.32) | data formatting | bytes 2097152 | tf_op jit(solution)/shard_map/reshape | solution.py:157
  (21 shorter events, 1.1 us)
Async XLA Ops:
  0.0 22.3 %copy-start.1 = (s32[4]{0:T(128)S(1)}, s32[4]{0:T(128)}, u32[]{:S(2)}) copy-start(s32[4]{0:T(128)} %param.6) | copy-start | bytes 52
  0.0 22.3 %copy-start = (f32[4,32]{1,0:T(4,128)S(1)}, f32[4,32]{1,0:T(4,128)}, u32[]{:S(2)}) copy-start(f32[4,32]{1,0:T(4,128)} %param.5) | copy-start | bytes 1540
  2.0 16.7 %collective-permute-start.2 = (bf16[32,3072]{1,0:T(8,128)(2,1)S(1)}, bf16[32,3072]{1,0:T(8,128)(2,1)S(1)}, u32[]{:S(2)}, u32[]{:S(2)}) collective-permute-start(bf16[32,3072]{1,0:T(8,128)(2,1)S(1)} %convolution_convert_fusion), channel_id=1, source_target_pairs={{0,96},{4,100},{8,104},{12,108},{16,112},{20,116},{24,120},{28,124... | collective-permute-start | bytes 589832 | tf_op jit(solution)/shard_map/ppermute | solution.py:112
  6.6 12.1 %collective-permute-start.1 = (bf16[32,3072]{1,0:T(8,128)(2,1)S(1)}, bf16[32,3072]{1,0:T(8,128)(2,1)S(1)}, u32[]{:S(2)}, u32[]{:S(2)}) collective-permute-start(bf16[32,3072]{1,0:T(8,128)(2,1)S(1)} %convolution_convert_fusion), channel_id=1, source_target_pairs={{0,64},{4,68},{8,72},{12,76},{16,80},{20,84},{24,88},{28,92},{32,9... | collective-permute-start | bytes 589832 | tf_op jit(solution)/shard_map/ppermute | solution.py:112
  6.6 12.1 %collective-permute-start = (bf16[32,3072]{1,0:T(8,128)(2,1)S(1)}, bf16[32,3072]{1,0:T(8,128)(2,1)S(1)}, u32[]{:S(2)}, u32[]{:S(2)}) collective-permute-start(bf16[32,3072]{1,0:T(8,128)(2,1)S(1)} %convolution_convert_fusion), channel_id=1, source_target_pairs={{0,32},{4,36},{8,40},{12,44},{16,48},{20,52},{24,56},{28,60},{32,0... | collective-permute-start | bytes 589832 | tf_op jit(solution)/shard_map/ppermute | solution.py:112
  18.8 11.7 %collective-permute-start.5 = (bf16[32,3072]{1,0:T(8,128)(2,1)S(1)}, bf16[32,3072]{1,0:T(8,128)(2,1)S(1)}, u32[]{:S(2)}, u32[]{:S(2)}) collective-permute-start(bf16[32,3072]{1,0:T(8,128)(2,1)S(1)} %add_add_fusion.1), channel_id=1, source_target_pairs={{0,24},{4,28},{8,16},{12,20},{16,8},{20,12},{24,0},{28,4},{32,56},... | collective-permute-start | bytes 589832 | tf_op jit(solution)/shard_map/ppermute | solution.py:112
  21.6 8.9 %collective-permute-start.4 = (bf16[32,3072]{1,0:T(8,128)(2,1)S(1)}, bf16[32,3072]{1,0:T(8,128)(2,1)S(1)}, u32[]{:S(2)}, u32[]{:S(2)}) collective-permute-start(bf16[32,3072]{1,0:T(8,128)(2,1)S(1)} %add_add_fusion.1), channel_id=1, source_target_pairs={{0,16},{4,20},{8,24},{12,28},{16,0},{20,4},{24,8},{28,12},{32,48},... | collective-permute-start | bytes 589832 | tf_op jit(solution)/shard_map/ppermute | solution.py:112
  21.9 9.3 %collective-permute-start.3 = (bf16[32,3072]{1,0:T(8,128)(2,1)S(1)}, bf16[32,3072]{1,0:T(8,128)(2,1)S(1)}, u32[]{:S(2)}, u32[]{:S(2)}) collective-permute-start(bf16[32,3072]{1,0:T(8,128)(2,1)S(1)} %add_add_fusion.1), channel_id=1, source_target_pairs={{0,8},{4,12},{8,0},{12,4},{16,24},{20,28},{24,16},{28,20},{32,40},... | collective-permute-start | bytes 589832 | tf_op jit(solution)/shard_map/ppermute | solution.py:112
  31.3 5.4 %collective-permute-start.6 = (bf16[32,3072]{1,0:T(8,128)(2,1)S(1)}, bf16[32,3072]{1,0:T(8,128)(2,1)S(1)}, u32[]{:S(2)}, u32[]{:S(2)}) collective-permute-start(bf16[32,3072]{1,0:T(8,128)(2,1)S(1)} %add_add_fusion), channel_id=1, source_target_pairs={{0,4},{4,0},{8,12},{12,8},{16,20},{20,16},{24,28},{28,24},{32,36},... | collective-permute-start | bytes 589832 | tf_op jit(solution)/shard_map/ppermute | solution.py:112

commit v19 on v17

--- a/solution.py
+++ b/solution.py
@@ -123,10 +123,9 @@
 
     flat_src = sources.reshape(-1)
     local_ids = flat_src - lax.axis_index("sta") * channels
-    onehot = (local_ids[:, None] == jnp.arange(channels, dtype=jnp.int32)[None, :]).astype(
-        jnp.bfloat16
-    )
-    picks = jnp.dot(onehot, signal, preferred_element_type=jnp.float32).astype(jnp.bfloat16)
+    owned = (local_ids >= 0) & (local_ids < channels)
+    rows = jnp.take(signal, jnp.clip(local_ids, 0, channels - 1), axis=0)
+    picks = jnp.where(owned[:, None], rows, jnp.zeros_like(rows))
     picks = summed_over(picks, "sta")
 
     def filtered_of(rows):

time: 82 us -> 83.5 us (1.018)
  local copies, waits for them, and re-layouts: 13.3 us -> 15.3 us
  matrix products: 4.64 us -> 3.47 us
  other arithmetic: 2.12 us -> 3 us
    gather x0 -> x1, local copies, waits for them, and re-layouts: none -> 1.81 us  [per_device(): rows = jnp.take(signal, jnp.clip(local_ids, 0, channels - 1), axis=0)]
    dot_general x1 -> x0, matrix products: 1.17 us -> none  [per_device(): jnp.dot(onehot, signal, preferred_element_type=jnp.float32)]
where the time goes in v19:
time: 83.5 us; the launch traced here: 83.2 us
  blocking collectives  22.3 us (27%)
  Pallas kernels  21.9 us (26%)
  local copies, waits for them, and re-layouts  15.3 us (18%)
  starting transfers between devices  9.11 us (11%)
  waiting for transfers between devices  7.87 us (9%)
  matrix products  3.47 us (4%)
  other arithmetic  3 us (4%)
    all_gather x2, blocking collectives, filtered_of(): rows = lax.all_gather(rows, 'tm', axis=1, tiled=True)  22.3 us
    pallas_call x1, Pallas kernels, correlate(): pl.pallas_call(kernel, grid_spec=grid_spec, out_shape=jax.ShapeDtypeStruc...  21.9 us
    ppermute x7, starting transfers between devices, summed_over(): lax.ppermute(value, axis, [(i, i ^ m) for i in range(count)])  9.11 us
    ppermute x7, waiting for transfers between devices, summed_over(): lax.ppermute(value, axis, [(i, i ^ m) for i in range(count)])  7.87 us
    reshape x1, local copies, waits for them, and re-layouts, per_device(): return out.reshape(ROUNDS, bands, count_src, channels, share)  4.56 us
    reshape x1, local copies, waits for them, and re-layouts, per_device(): out = out.reshape(bands, SHIFTS, channels, ROUNDS, count_src, groups)  3.81 us
    dot_general x2, matrix products, filter_in_blocks(): jnp.einsum('nru,btu->bnrt', pieces, banded, preferred_element_type=jnp.fl...  3.47 us
    pad x1, local copies, waits for them, and re-layouts, per_device(): jnp.pad(f_loc, ((0, 0), (f_front, blocks + lag_count // 128 - data_blocks...  2.3 us
  transfers between devices with their start and end apart: 7, of which 3 were waited for; matrix products, arithmetic and copies ran while one was open for 7% of the time, Pallas kernels for 0%

profile of v19, /device:TPU:1, one launch (start us, length us, event | category | flops | bytes accessed | tf_op | source)
XLA Modules:
  0.0 83.2 jit_solution(11758752426041442685)
XLA Ops:
  0.0 0.7 compare_and_fusion.1
  0.7 0.7 subtract_clamp_fusion
  1.7 1.8 %gather_fusion = bf16[32,3072]{1,0:T(8,128)(2,1)S(1)} fusion(bf16[32,3072]{1,0:T(8,128)(2,1)} %param.4, s32[1024]{0:T(1024)S(1)} %pad_clamp_fusion), kind=kCustom, calls=%fused_computation | custom fusion | bytes 393344 | tf_op jit(solution)/shard_map/jit(_take)/gather | solution.py:127
  3.6 4.5 %collective-permute-start.1 = (bf16[32,3072]{1,0:T(8,128)(2,1)S(1)}, bf16[32,3072]{1,0:T(8,128)(2,1)S(1)}, u32[]{:S(2)}, u32[]{:S(2)}) collective-permute-start(bf16[32,3072]{1,0:T(8,128)(2,1)S(1)} %select_select_fusion), channel_id=1, source_target_pairs={{0,64},{4,68},{8,72},{12,76},{16,80},{20,84},{24,88},{28,92},{32,9... | collective-permute-start | bytes 589832 | tf_op jit(solution)/shard_map/ppermute | solution.py:109
  8.1 0.4 collective-permute-start.2
  8.9 11.2 %all_gather.6 = bf16[32,12288]{1,0:T(8,128)(2,1)S(1)} all-gather(bf16[32,3072]{1,0:T(8,128)(2,1)S(1)} %copy-done), channel_id=1, replica_groups=mesh['sta'=32,'tm'=4] {'tm'}, dimensions={1}, use_global_device_ids=true | all-gather | bytes 983040 | tf_op jit(solution)/shard_map/all_gather | solution.py:132
  20.2 2.8 %collective-permute-start.5 = (bf16[32,3072]{1,0:T(8,128)(2,1)S(1)}, bf16[32,3072]{1,0:T(8,128)(2,1)S(1)}, u32[]{:S(2)}, u32[]{:S(2)}) collective-permute-start(bf16[32,3072]{1,0:T(8,128)(2,1)S(1)} %add_add_fusion.1), channel_id=1, source_target_pairs={{0,24},{4,28},{8,16},{12,20},{16,8},{20,12},{24,0},{28,4},{32,56},... | collective-permute-start | bytes 589832 | tf_op jit(solution)/shard_map/ppermute | solution.py:109
  23.9 0.4 tile.5
  24.3 0.6 reshape.75
  25.1 0.6 fusion.3
  25.7 6.1 %collective-permute-done.5 = bf16[32,3072]{1,0:T(8,128)(2,1)S(1)} collective-permute-done((bf16[32,3072]{1,0:T(8,128)(2,1)S(1)}, bf16[32,3072]{1,0:T(8,128)(2,1)S(1)}, u32[]{:S(2)}, u32[]{:S(2)}) %collective-permute-start.5) | collective-permute-done | bytes 196640 | tf_op jit(solution)/shard_map/ppermute | solution.py:109
  31.9 0.8 collective-permute-done.3
  32.7 0.4 collective-permute-start.6
  33.1 1.7 %convert_bitcast_fusion.1 = bf16[4,96,32,128]{3,2,1,0:T(8,128)(2,1)S(1)} fusion(bf16[96,32,256,1]{2,0,1,3:T(8,128)(2,1)S(1)} %fusion.3, bf16[4,128,159]{2,1,0:T(8,128)(2,1)S(1)} %reshape.75), kind=kOutput, calls=%fused_computation.5 | convolution fusion | flops 806879232 | bytes 4881408 | tf_op jit(solution)/shard_map/nru,btu->bnrt/dot_general | solution.py:41
  34.8 2.3 %pad.23.fw_ref = bf16[4,105,32,128]{3,2,1,0:T(8,128)(2,1)} pad(bf16[4,96,32,128]{3,2,1,0:T(8,128)(2,1)S(1)} %convert_bitcast_fusion.1, bf16[]{:T(256)} %constant.12.clone.1), padding=0_0x2_7x0_0x0_0 | pad | bytes 6586370 | tf_op jit(solution)/shard_map/jit(_pad)/pad | solution.py:143
  37.1 1.0 %collective-permute-done.6 = bf16[32,3072]{1,0:T(8,128)(2,1)S(1)} collective-permute-done((bf16[32,3072]{1,0:T(8,128)(2,1)S(1)}, bf16[32,3072]{1,0:T(8,128)(2,1)S(1)}, u32[]{:S(2)}, u32[]{:S(2)}) %collective-permute-start.6) | collective-permute-done | bytes 196640 | tf_op jit(solution)/shard_map/ppermute | solution.py:109
  38.1 11.2 %all_gather.7 = bf16[32,12288]{1,0:T(8,128)(2,1)S(1)} all-gather(bf16[32,3072]{1,0:T(8,128)(2,1)S(1)} %add.58), channel_id=1, replica_groups=mesh['sta'=32,'tm'=4] {'tm'}, dimensions={1}, use_global_device_ids=true | all-gather | bytes 983040 | tf_op jit(solution)/shard_map/all_gather | solution.py:132
  49.4 0.6 fusion.5
  50.1 1.7 %convert_bitcast_fusion = bf16[4,96,32,128]{3,2,1,0:T(8,128)(2,1)S(1)} fusion(bf16[96,32,256,1]{2,0,1,3:T(8,128)(2,1)S(1)} %fusion.5, bf16[4,128,159]{2,1,0:T(8,128)(2,1)S(1)} %reshape.75), kind=kOutput, calls=%fused_computation.4 | convolution fusion | flops 806879232 | bytes 4881408 | tf_op jit(solution)/shard_map/nru,btu->bnrt/dot_general | solution.py:41
  51.8 0.6 pad.25.pp_ref
  52.4 21.9 %shard_map.46 = bf16[4,512,256]{2,1,0:T(8,128)(2,1)S(1)} custom-call(s32[1]{0:T(128)} %bitcast.off_ref, bf16[4,105,32,128]{3,2,1,0:T(8,128)(2,1)} %pad.23.fw_ref, bf16[4,101,32,128]{3,2,1,0:T(8,128)(2,1)S(1)} %pad.25.pp_ref), custom_call_target="tpu_custom_call" | custom-call | tf_op jit(solution)/shard_map/pallas_call | solution.py:92
  74.3 0.5 copy.10
  74.8 3.8 %reshape.78 = bf16[4,16,32,2,16,8]{2,1,5,4,3,0:T(8,128)(2,1)} reshape(bf16[4,512,256]{1,2,0:T(8,128)(2,1)S(1)} %copy.10) | data formatting | bytes 2097152 | tf_op jit(solution)/shard_map/reshape | solution.py:151
  78.6 4.6 %copy.12 = bf16[2,4,16,32,128]{4,3,2,1,0:T(8,128)(2,1)} copy(bf16[2,4,16,32,128]{3,4,2,0,1:T(8,128)(2,1)} %bitcast.33) | data formatting | bytes 2097152 | tf_op jit(solution)/shard_map/reshape | solution.py:153
  (30 shorter events, 2.1 us)
Async XLA Ops:
  0.0 8.9 %copy-start = (bf16[32,3072]{1,0:T(8,128)(2,1)S(1)}, bf16[32,3072]{1,0:T(8,128)(2,1)}, u32[]{:S(2)}) copy-start(bf16[32,3072]{1,0:T(8,128)(2,1)} %param.4) | copy-start | bytes 589828
  3.5 20.2 %copy-start.1 = (f32[4,32]{1,0:T(4,128)S(1)}, f32[4,32]{1,0:T(4,128)}, u32[]{:S(2)}) copy-start(f32[4,32]{1,0:T(4,128)} %param.5) | copy-start | bytes 1540
  3.5 20.2 %copy-start.2 = (s32[4]{0:T(128)S(1)}, s32[4]{0:T(128)}, u32[]{:S(2)}) copy-start(s32[4]{0:T(128)} %param.6) | copy-start | bytes 52
  3.6 16.4 %collective-permute-start.1 = (bf16[32,3072]{1,0:T(8,128)(2,1)S(1)}, bf16[32,3072]{1,0:T(8,128)(2,1)S(1)}, u32[]{:S(2)}, u32[]{:S(2)}) collective-permute-start(bf16[32,3072]{1,0:T(8,128)(2,1)S(1)} %select_select_fusion), channel_id=1, source_target_pairs={{0,64},{4,68},{8,72},{12,76},{16,80},{20,84},{24,88},{28,92},{32,9... | collective-permute-start | bytes 589832 | tf_op jit(solution)/shard_map/ppermute | solution.py:109
  8.1 11.9 %collective-permute-start.2 = (bf16[32,3072]{1,0:T(8,128)(2,1)S(1)}, bf16[32,3072]{1,0:T(8,128)(2,1)S(1)}, u32[]{:S(2)}, u32[]{:S(2)}) collective-permute-start(bf16[32,3072]{1,0:T(8,128)(2,1)S(1)} %select_select_fusion), channel_id=1, source_target_pairs={{0,96},{4,100},{8,104},{12,108},{16,112},{20,116},{24,120},{28,124... | collective-permute-start | bytes 589832 | tf_op jit(solution)/shard_map/ppermute | solution.py:109
  8.6 11.5 %collective-permute-start = (bf16[32,3072]{1,0:T(8,128)(2,1)S(1)}, bf16[32,3072]{1,0:T(8,128)(2,1)S(1)}, u32[]{:S(2)}, u32[]{:S(2)}) collective-permute-start(bf16[32,3072]{1,0:T(8,128)(2,1)S(1)} %select_select_fusion), channel_id=1, source_target_pairs={{0,32},{4,36},{8,40},{12,44},{16,48},{20,52},{24,56},{28,60},{32,0... | collective-permute-start | bytes 589832 | tf_op jit(solution)/shard_map/ppermute | solution.py:109
  20.2 11.7 %collective-permute-start.5 = (bf16[32,3072]{1,0:T(8,128)(2,1)S(1)}, bf16[32,3072]{1,0:T(8,128)(2,1)S(1)}, u32[]{:S(2)}, u32[]{:S(2)}) collective-permute-start(bf16[32,3072]{1,0:T(8,128)(2,1)S(1)} %add_add_fusion.1), channel_id=1, source_target_pairs={{0,24},{4,28},{8,16},{12,20},{16,8},{20,12},{24,0},{28,4},{32,56},... | collective-permute-start | bytes 589832 | tf_op jit(solution)/shard_map/ppermute | solution.py:109
  23.0 8.9 %collective-permute-start.4 = (bf16[32,3072]{1,0:T(8,128)(2,1)S(1)}, bf16[32,3072]{1,0:T(8,128)(2,1)S(1)}, u32[]{:S(2)}, u32[]{:S(2)}) collective-permute-start(bf16[32,3072]{1,0:T(8,128)(2,1)S(1)} %add_add_fusion.1), channel_id=1, source_target_pairs={{0,16},{4,20},{8,24},{12,28},{16,0},{20,4},{24,8},{28,12},{32,48},... | collective-permute-start | bytes 589832 | tf_op jit(solution)/shard_map/ppermute | solution.py:109
  23.4 9.3 %collective-permute-start.3 = (bf16[32,3072]{1,0:T(8,128)(2,1)S(1)}, bf16[32,3072]{1,0:T(8,128)(2,1)S(1)}, u32[]{:S(2)}, u32[]{:S(2)}) collective-permute-start(bf16[32,3072]{1,0:T(8,128)(2,1)S(1)} %add_add_fusion.1), channel_id=1, source_target_pairs={{0,8},{4,12},{8,0},{12,4},{16,24},{20,28},{24,16},{28,20},{32,40},... | collective-permute-start | bytes 589832 | tf_op jit(solution)/shard_map/ppermute | solution.py:109
  32.7 5.4 %collective-permute-start.6 = (bf16[32,3072]{1,0:T(8,128)(2,1)S(1)}, bf16[32,3072]{1,0:T(8,128)(2,1)S(1)}, u32[]{:S(2)}, u32[]{:S(2)}) collective-permute-start(bf16[32,3072]{1,0:T(8,128)(2,1)S(1)} %add_add_fusion), channel_id=1, source_target_pairs={{0,4},{4,0},{8,12},{12,8},{16,20},{20,16},{24,28},{28,24},{32,36},... | collective-permute-start | bytes 589832 | tf_op jit(solution)/shard_map/ppermute | solution.py:109

commit v20 on v17

--- a/solution.py
+++ b/solution.py
@@ -10,7 +10,7 @@
 ROUNDS = 2
 MAXLAG = 256
 SHIFTS = 16
-CHUNK = 3200
+CHUNK = 4224
 
 
 def skew(values, count_rows):

time: 82 us -> 81.7 us (level)
  no operation moved by 1% of the time
where the time goes in v20:
time: 81.7 us; the launch traced here: 81.4 us
  blocking collectives  22.5 us (28%)
  Pallas kernels  21.6 us (26%)
  local copies, waits for them, and re-layouts  13.3 us (16%)
  starting transfers between devices  9.19 us (11%)
  waiting for transfers between devices  7.91 us (10%)
  matrix products  4.64 us (6%)
  other arithmetic  2.12 us (3%)
    all_gather x2, blocking collectives, filtered_of(): rows = lax.all_gather(rows, 'tm', axis=1, tiled=True)  22.5 us
    pallas_call x1, Pallas kernels, correlate(): pl.pallas_call(kernel, grid_spec=grid_spec, out_shape=jax.ShapeDtypeStruc...  21.6 us
    ppermute x7, starting transfers between devices, summed_over(): lax.ppermute(value, axis, [(i, i ^ m) for i in range(count)])  9.19 us
    ppermute x7, waiting for transfers between devices, summed_over(): lax.ppermute(value, axis, [(i, i ^ m) for i in range(count)])  7.91 us
    reshape x1, local copies, waits for them, and re-layouts, per_device(): return out.reshape(ROUNDS, bands, count_src, channels, share)  4.56 us
    reshape x1, local copies, waits for them, and re-layouts, per_device(): out = out.reshape(bands, SHIFTS, channels, ROUNDS, count_src, groups)  3.8 us
    dot_general x2, matrix products, filter_in_blocks(): jnp.einsum('nru,btu->bnrt', pieces, banded, preferred_element_type=jnp.fl...  3.47 us
    pad x1, local copies, waits for them, and re-layouts, per_device(): jnp.pad(f_loc, ((0, 0), (f_front, blocks + lag_count // 128 - data_blocks...  2.29 us
  transfers between devices with their start and end apart: 7, of which 3 were waited for; matrix products, arithmetic and copies ran while one was open for 7% of the time, Pallas kernels for 0%

profile of v20, /device:TPU:1, one launch (start us, length us, event | category | flops | bytes accessed | tf_op | source)
XLA Modules:
  0.0 81.4 jit_solution(13233346426644846486)
XLA Ops:
  0.0 0.7 broadcast_subtract_fusion
  0.8 1.2 %convolution_convert_fusion = bf16[32,3072]{1,0:T(8,128)(2,1)S(1)} fusion(bf16[32,3072]{1,0:T(8,128)(2,1)} %param.4, s32[32]{0:T(128)S(1)} %sub.15), kind=kOutput, calls=%fused_computation | convolution fusion | flops 6390784 | bytes 393344 | tf_op jit(solution)/shard_map/dot_general | solution.py:129
  2.0 4.7 %collective-permute-start.2 = (bf16[32,3072]{1,0:T(8,128)(2,1)S(1)}, bf16[32,3072]{1,0:T(8,128)(2,1)S(1)}, u32[]{:S(2)}, u32[]{:S(2)}) collective-permute-start(bf16[32,3072]{1,0:T(8,128)(2,1)S(1)} %convolution_convert_fusion), channel_id=1, source_target_pairs={{0,96},{4,100},{8,104},{12,108},{16,112},{20,116},{24,120},{28,124... | collective-permute-start | bytes 589832 | tf_op jit(solution)/shard_map/ppermute | solution.py:109
  6.6 0.7 collective-permute-start
  7.3 11.4 %all_gather.6 = bf16[32,12288]{1,0:T(8,128)(2,1)S(1)} all-gather(bf16[32,3072]{1,0:T(8,128)(2,1)} %param.4), channel_id=1, replica_groups=mesh['sta'=32,'tm'=4] {'tm'}, dimensions={1}, use_global_device_ids=true | all-gather | bytes 983040 | tf_op jit(solution)/shard_map/all_gather | solution.py:133
  18.8 2.8 %collective-permute-start.5 = (bf16[32,3072]{1,0:T(8,128)(2,1)S(1)}, bf16[32,3072]{1,0:T(8,128)(2,1)S(1)}, u32[]{:S(2)}, u32[]{:S(2)}) collective-permute-start(bf16[32,3072]{1,0:T(8,128)(2,1)S(1)} %add_add_fusion.1), channel_id=1, source_target_pairs={{0,24},{4,28},{8,16},{12,20},{16,8},{20,12},{24,0},{28,4},{32,56},... | collective-permute-start | bytes 589832 | tf_op jit(solution)/shard_map/ppermute | solution.py:109
  21.6 0.3 collective-permute-start.4
  22.5 0.4 tile.5
  22.9 0.6 reshape.33
  23.7 0.6 fusion.3
  24.3 6.1 %collective-permute-done.5 = bf16[32,3072]{1,0:T(8,128)(2,1)S(1)} collective-permute-done((bf16[32,3072]{1,0:T(8,128)(2,1)S(1)}, bf16[32,3072]{1,0:T(8,128)(2,1)S(1)}, u32[]{:S(2)}, u32[]{:S(2)}) %collective-permute-start.5) | collective-permute-done | bytes 196640 | tf_op jit(solution)/shard_map/ppermute | solution.py:109
  30.5 0.8 collective-permute-done.3
  31.3 0.4 collective-permute-start.6
  31.6 1.7 %convert_bitcast_fusion.1 = bf16[4,96,32,128]{3,2,1,0:T(8,128)(2,1)S(1)} fusion(bf16[96,32,256,1]{2,0,1,3:T(8,128)(2,1)S(1)} %fusion.3, bf16[4,128,159]{2,1,0:T(8,128)(2,1)S(1)} %reshape.33), kind=kOutput, calls=%fused_computation.5 | convolution fusion | flops 806879232 | bytes 4881408 | tf_op jit(solution)/shard_map/nru,btu->bnrt/dot_general | solution.py:41
  33.4 2.3 %pad.23.fw_ref = bf16[4,104,32,128]{3,2,1,0:T(8,128)(2,1)} pad(bf16[4,96,32,128]{3,2,1,0:T(8,128)(2,1)S(1)} %convert_bitcast_fusion.1, bf16[]{:T(256)} %constant.5.clone.1), padding=0_0x2_6x0_0x0_0 | pad | bytes 6553602 | tf_op jit(solution)/shard_map/jit(_pad)/pad | solution.py:144
  35.7 1.0 %collective-permute-done.6 = bf16[32,3072]{1,0:T(8,128)(2,1)S(1)} collective-permute-done((bf16[32,3072]{1,0:T(8,128)(2,1)S(1)}, bf16[32,3072]{1,0:T(8,128)(2,1)S(1)}, u32[]{:S(2)}, u32[]{:S(2)}) %collective-permute-start.6) | collective-permute-done | bytes 196640 | tf_op jit(solution)/shard_map/ppermute | solution.py:109
  36.7 11.2 %all_gather.7 = bf16[32,12288]{1,0:T(8,128)(2,1)S(1)} all-gather(bf16[32,3072]{1,0:T(8,128)(2,1)S(1)} %add.39), channel_id=1, replica_groups=mesh['sta'=32,'tm'=4] {'tm'}, dimensions={1}, use_global_device_ids=true | all-gather | bytes 983040 | tf_op jit(solution)/shard_map/all_gather | solution.py:133
  48.0 0.6 fusion.5
  48.6 1.7 %convert_bitcast_fusion = bf16[4,96,32,128]{3,2,1,0:T(8,128)(2,1)S(1)} fusion(bf16[96,32,256,1]{2,0,1,3:T(8,128)(2,1)S(1)} %fusion.5, bf16[4,128,159]{2,1,0:T(8,128)(2,1)S(1)} %reshape.33), kind=kOutput, calls=%fused_computation.4 | convolution fusion | flops 806879232 | bytes 4881408 | tf_op jit(solution)/shard_map/nru,btu->bnrt/dot_general | solution.py:41
  50.4 0.6 pad.25.pp_ref
  50.9 21.6 %shard_map.46 = bf16[4,512,256]{2,1,0:T(8,128)(2,1)S(1)} custom-call(s32[1]{0:T(128)} %bitcast.off_ref, bf16[4,104,32,128]{3,2,1,0:T(8,128)(2,1)} %pad.23.fw_ref, bf16[4,100,32,128]{3,2,1,0:T(8,128)(2,1)S(1)} %pad.25.pp_ref), custom_call_target="tpu_custom_call" | custom-call | tf_op jit(solution)/shard_map/pallas_call | solution.py:92
  72.5 0.5 copy.10
  73.1 3.8 %reshape.36 = bf16[4,16,32,2,16,8]{2,1,5,4,3,0:T(8,128)(2,1)} reshape(bf16[4,512,256]{1,2,0:T(8,128)(2,1)S(1)} %copy.10) | data formatting | bytes 2097152 | tf_op jit(solution)/shard_map/reshape | solution.py:152
  76.9 4.6 %copy.12 = bf16[2,4,16,32,128]{4,3,2,1,0:T(8,128)(2,1)} copy(bf16[2,4,16,32,128]{3,4,2,0,1:T(8,128)(2,1)} %bitcast.32) | data formatting | bytes 2097152 | tf_op jit(solution)/shard_map/reshape | solution.py:154
  (21 shorter events, 1.1 us)
Async XLA Ops:
  0.0 22.3 %copy-start.1 = (s32[4]{0:T(128)S(1)}, s32[4]{0:T(128)}, u32[]{:S(2)}) copy-start(s32[4]{0:T(128)} %param.6) | copy-start | bytes 52
  0.0 22.3 %copy-start = (f32[4,32]{1,0:T(4,128)S(1)}, f32[4,32]{1,0:T(4,128)}, u32[]{:S(2)}) copy-start(f32[4,32]{1,0:T(4,128)} %param.5) | copy-start | bytes 1540
  2.0 16.7 %collective-permute-start.2 = (bf16[32,3072]{1,0:T(8,128)(2,1)S(1)}, bf16[32,3072]{1,0:T(8,128)(2,1)S(1)}, u32[]{:S(2)}, u32[]{:S(2)}) collective-permute-start(bf16[32,3072]{1,0:T(8,128)(2,1)S(1)} %convolution_convert_fusion), channel_id=1, source_target_pairs={{0,96},{4,100},{8,104},{12,108},{16,112},{20,116},{24,120},{28,124... | collective-permute-start | bytes 589832 | tf_op jit(solution)/shard_map/ppermute | solution.py:109
  6.6 12.1 %collective-permute-start.1 = (bf16[32,3072]{1,0:T(8,128)(2,1)S(1)}, bf16[32,3072]{1,0:T(8,128)(2,1)S(1)}, u32[]{:S(2)}, u32[]{:S(2)}) collective-permute-start(bf16[32,3072]{1,0:T(8,128)(2,1)S(1)} %convolution_convert_fusion), channel_id=1, source_target_pairs={{0,64},{4,68},{8,72},{12,76},{16,80},{20,84},{24,88},{28,92},{32,9... | collective-permute-start | bytes 589832 | tf_op jit(solution)/shard_map/ppermute | solution.py:109
  6.6 12.1 %collective-permute-start = (bf16[32,3072]{1,0:T(8,128)(2,1)S(1)}, bf16[32,3072]{1,0:T(8,128)(2,1)S(1)}, u32[]{:S(2)}, u32[]{:S(2)}) collective-permute-start(bf16[32,3072]{1,0:T(8,128)(2,1)S(1)} %convolution_convert_fusion), channel_id=1, source_target_pairs={{0,32},{4,36},{8,40},{12,44},{16,48},{20,52},{24,56},{28,60},{32,0... | collective-permute-start | bytes 589832 | tf_op jit(solution)/shard_map/ppermute | solution.py:109
  18.8 11.7 %collective-permute-start.5 = (bf16[32,3072]{1,0:T(8,128)(2,1)S(1)}, bf16[32,3072]{1,0:T(8,128)(2,1)S(1)}, u32[]{:S(2)}, u32[]{:S(2)}) collective-permute-start(bf16[32,3072]{1,0:T(8,128)(2,1)S(1)} %add_add_fusion.1), channel_id=1, source_target_pairs={{0,24},{4,28},{8,16},{12,20},{16,8},{20,12},{24,0},{28,4},{32,56},... | collective-permute-start | bytes 589832 | tf_op jit(solution)/shard_map/ppermute | solution.py:109
  21.6 8.9 %collective-permute-start.4 = (bf16[32,3072]{1,0:T(8,128)(2,1)S(1)}, bf16[32,3072]{1,0:T(8,128)(2,1)S(1)}, u32[]{:S(2)}, u32[]{:S(2)}) collective-permute-start(bf16[32,3072]{1,0:T(8,128)(2,1)S(1)} %add_add_fusion.1), channel_id=1, source_target_pairs={{0,16},{4,20},{8,24},{12,28},{16,0},{20,4},{24,8},{28,12},{32,48},... | collective-permute-start | bytes 589832 | tf_op jit(solution)/shard_map/ppermute | solution.py:109
  21.9 9.3 %collective-permute-start.3 = (bf16[32,3072]{1,0:T(8,128)(2,1)S(1)}, bf16[32,3072]{1,0:T(8,128)(2,1)S(1)}, u32[]{:S(2)}, u32[]{:S(2)}) collective-permute-start(bf16[32,3072]{1,0:T(8,128)(2,1)S(1)} %add_add_fusion.1), channel_id=1, source_target_pairs={{0,8},{4,12},{8,0},{12,4},{16,24},{20,28},{24,16},{28,20},{32,40},... | collective-permute-start | bytes 589832 | tf_op jit(solution)/shard_map/ppermute | solution.py:109
  31.3 5.4 %collective-permute-start.6 = (bf16[32,3072]{1,0:T(8,128)(2,1)S(1)}, bf16[32,3072]{1,0:T(8,128)(2,1)S(1)}, u32[]{:S(2)}, u32[]{:S(2)}) collective-permute-start(bf16[32,3072]{1,0:T(8,128)(2,1)S(1)} %add_add_fusion), channel_id=1, source_target_pairs={{0,4},{4,0},{8,12},{12,8},{16,20},{20,16},{24,28},{28,24},{32,36},... | collective-permute-start | bytes 589832 | tf_op jit(solution)/shard_map/ppermute | solution.py:109
